TPU v7x, 128 devices: a whole 4x4x4 slice. The times are simulated.
128 devices in a mesh: wave: 16 (over y, z_lo, core), pole: 8 (over x, z_hi).
Axes of the slice: x: 4, y: 4, z: 4 (z_hi: 2, z_lo: 2; z = z_hi * 2 + z_lo), core: 2. Of those that a mesh axis runs over, the one named last changes fastest.
Arguments:
- grid: float32 [6, 256, 3072], P(None, None, 'wave'), may hold values from -6 to 6
- legendre: bfloat16 [256, 2, 1536, 1024], P('wave', None, None, 'pole'), may hold values from -0.15625 to 0.15625
- wave_table: int32 [256], replicated, may hold values from 0 to 255, each once
- pole_table: float32 [4, 64], replicated, may hold values from -1.5 to 2.5, as said below
- pole_index: int32 [32], replicated, may hold values from 0 to 63
Outputs:
- next_state: float32 [6, 2, 256, 1024], P(None, None, 'wave', 'pole')
Inputs may be any that keep to these rules, and one draw needn't show every extreme that they name: Slot s holds zonal wavenumber wave_table[s], every wavenumber of 0 to 255 once; row s of legendre belongs to it. `pole_table`: shift real parts lie in 1.5 to 2.5, shift imaginary parts in -1.5 to 1.5, weights in -1.2 to 1.2.
All inputs are finite; a program needn't handle non-finite values.
Results may differ from a plain program's by a relative error of at most 0.0003.
Values sent between devices are 32-bit elements; how exact they have to be, the bound alone decides.
No kernel may reach another device: no remote copies, remote signals or barrier semaphores. Data moves between devices by JAX's collectives and lax.ppermute only.
A program may use at most 128 MiB of HBM per device.

v0:
```python
import jax
import jax.numpy as jnp
from jax import lax
from jax.experimental import pallas as pl
from jax.experimental.pallas import tpu as pltpu
from jax.sharding import PartitionSpec as P

SWEEPS = 8
HALO = 8
RING = 256
CHUNK = 8


coriolis_step = 1.2
gravity_step = 0.0008


def split_high(values):
    upper_part = values.astype(jnp.bfloat16)
    kept = lax.optimization_barrier(upper_part)
    lower_part = (values - kept.astype(jnp.float32)).astype(jnp.bfloat16)
    return (upper_part, lower_part)


def coefficients(wavenum, base, width, total):
    lane = jnp.arange(RING, dtype=jnp.int32)
    index = jnp.where(lane >= RING - HALO, base + lane - RING, base + lane)
    inside = ((lane < width + HALO) | (lane >= RING - HALO)) & (index >= 0) & (index < total)
    index = jnp.clip(index, 0, total - 1).astype(jnp.float32)
    parity = jnp.arange(2, dtype=jnp.int32).astype(jnp.float32)
    order = (2.0 * index[None, :] + parity[:, None])[:, None, :]
    upper_inside = inside[None, None, :] & (order + 1.0 < 2.0 * total)
    wave = wavenum[None, :, None]
    degree = wave + order
    product = degree * (degree + 1.0)
    rossby = coriolis_step * wave / jnp.maximum(product, 2.0)
    gravity = gravity_step * jnp.sqrt(product)
    e_lo = jnp.sqrt(order * (2.0 * wave + order) / jnp.maximum(4.0 * degree * degree - 1.0, 1.0))
    after = order + 1.0
    upper_deg = degree + 1.0
    e_hi = jnp.sqrt(
        after * (2.0 * wave + after) / jnp.maximum(4.0 * upper_deg * upper_deg - 1.0, 1.0)
    )
    e_lo = jnp.where(inside[None, None, :], e_lo, 0.0)
    e_hi = jnp.where(upper_inside, e_hi, 0.0)
    return jnp.stack([e_lo, e_hi, rossby, gravity], axis=0)


def pole_kernel(poles_ref, spec_ref, coef_ref, out_ref):
    npoles = poles_ref.shape[1]
    rows = spec_ref.shape[2]
    lanes = spec_ref.shape[3]
    width = out_ref.shape[3]
    out_ref[...] = jnp.zeros(out_ref.shape, jnp.float32)

    def one_pole(q, carry):
        a_re = poles_ref[0, q]
        a_im = poles_ref[1, q]
        w_re = poles_ref[2, q]
        w_im = poles_ref[3, q]
        for r0 in range(0, rows, CHUNK):
            sl = pl.ds(r0, CHUNK)

            def ld(ref, i, p):
                return ref[i, p, sl, :]

            def near(x):
                n0 = ld(coef_ref, 0, 0) * pltpu.roll(x[1], 1, 1) + ld(coef_ref, 1, 0) * x[1]
                n1 = ld(coef_ref, 0, 1) * x[0] + ld(coef_ref, 1, 1) * pltpu.roll(x[0], lanes - 1, 1)
                return (n0, n1)

            inv, dinv, hb = [], [], []
            for p in range(2):
                grav = ld(coef_ref, 3, p)
                b_im = a_im + ld(coef_ref, 2, p)
                b_mag = a_re * a_re + b_im * b_im
                inv.append((a_re / b_mag, -b_im / b_mag))
                det_re = a_re * a_re - b_im * a_im + grav * grav
                det_im = a_re * a_im + b_im * a_re
                det_mag = det_re * det_re + det_im * det_im
                dinv.append((det_re / det_mag, -det_im / det_mag))
                h0r = ld(spec_ref, 4, p)
                h0i = ld(spec_ref, 5, p)
                hb.append((a_re * h0r - b_im * h0i, a_re * h0i + b_im * h0r))
            zr = zi = dr = di = hr = hi = None
            for sweep in range(SWEEPS):
                if sweep > 0:
                    nzr, nzi, ndr, ndi = near(zr), near(zi), near(dr), near(di)
                zr, zi, dr, di, hr, hi = [], [], [], [], [], []
                for p in range(2):
                    if sweep == 0:
                        rzr, rzi = ld(spec_ref, 0, p), ld(spec_ref, 1, p)
                        rdr, rdi = ld(spec_ref, 2, p), ld(spec_ref, 3, p)
                    else:
                        rzr = ld(spec_ref, 0, p) - coriolis_step * ndr[p]
                        rzi = ld(spec_ref, 1, p) - coriolis_step * ndi[p]
                        rdr = ld(spec_ref, 2, p) + coriolis_step * nzr[p]
                        rdi = ld(spec_ref, 3, p) + coriolis_step * nzi[p]
                    z_re, z_im = cmul(rzr, rzi, inv[p][0], inv[p][1])
                    zr.append(z_re)
                    zi.append(z_im)
                    grav = ld(coef_ref, 3, p)
                    nd_re, nd_im = cmul(a_re, a_im, rdr, rdi)
                    nd_re = nd_re + grav * ld(spec_ref, 4, p)
                    nd_im = nd_im + grav * ld(spec_ref, 5, p)
                    d_re, d_im = cmul(nd_re, nd_im, dinv[p][0], dinv[p][1])
                    dr.append(d_re)
                    di.append(d_im)
                    if sweep == SWEEPS - 1:
                        nh_re = hb[p][0] - grav * rdr
                        nh_im = hb[p][1] - grav * rdi
                        h_re, h_im = cmul(nh_re, nh_im, dinv[p][0], dinv[p][1])
                        hr.append(h_re)
                        hi.append(h_im)
            for field, (f_re, f_im) in enumerate(((zr, zi), (dr, di), (hr, hi))):
                for p in range(2):
                    o_re, o_im = cmul(w_re, w_im, f_re[p], f_im[p])
                    out_ref[2 * field, p, sl, :] += o_re[:, :width]
                    out_ref[2 * field + 1, p, sl, :] += o_im[:, :width]
        return carry

    lax.fori_loop(0, npoles, one_pole, 0)


def solve_poles(poles, wide, coef, width):
    comps, parities, rows, _ = wide.shape
    return pl.pallas_call(
        pole_kernel,
        out_shape=jax.ShapeDtypeStruct((comps, parities, rows, width), jnp.float32),
        in_specs=[
            pl.BlockSpec(memory_space=pltpu.SMEM),
            pl.BlockSpec(memory_space=pltpu.VMEM),
            pl.BlockSpec(memory_space=pltpu.VMEM),
        ],
        out_specs=pl.BlockSpec(memory_space=pltpu.VMEM),
    )(poles, wide, coef)


def cmul(are, aim, bre, bim):
    return (are * bre - aim * bim, are * bim + aim * bre)


def zero_extend(field):
    return jnp.pad(field, ((0, 0), (0, 0), (0, 0), (0, 0), (1, 1)))


def solve(spectra, coef, shifts, extend):
    e_lo, e_hi, rossby, gravity = coef
    count = spectra.shape[3]
    shift_re = shifts[:, 0][:, None, None, None]
    shift_im = shifts[:, 1][:, None, None, None]
    weight_re = shifts[:, 2][:, None, None, None]
    weight_im = shifts[:, 3][:, None, None, None]
    z0r, z0i = (spectra[0][None], spectra[1][None])
    d0r, d0i = (spectra[2][None], spectra[3][None])
    h0r, h0i = (spectra[4][None], spectra[5][None])
    b_re = shift_re + 0.0 * rossby[None]
    b_im = shift_im + rossby[None]
    b_mag = b_re * b_re + b_im * b_im
    inv_re, inv_im = (b_re / b_mag, -b_im / b_mag)
    det_re, det_im = cmul(b_re, b_im, shift_re, shift_im)
    det_re = det_re + gravity[None] * gravity[None]
    det_mag = det_re * det_re + det_im * det_im
    dinv_re, dinv_im = (det_re / det_mag, -det_im / det_mag)
    grav = gravity[None]
    hb_re, hb_im = cmul(b_re, b_im, h0r, h0i)
    zr, zi, dr, di, hr, hi = (z0r, z0i, d0r, d0i, h0r, h0i)
    for sweep in range(SWEEPS):
        if sweep == 0:
            rzr, rzi, rdr, rdi = (z0r, z0i, d0r, d0i)
        else:
            both = jnp.stack([zr, zi, dr, di], axis=0)
            ext = extend(both)
            lower = jnp.stack([ext[:, :, 1, :, 0:count], ext[:, :, 0, :, 1 : count + 1]], axis=2)
            upper = jnp.stack(
                [ext[:, :, 1, :, 1 : count + 1], ext[:, :, 0, :, 2 : count + 2]], axis=2
            )
            near = e_lo * lower + e_hi * upper
            rzr = z0r - coriolis_step * near[2]
            rzi = z0i - coriolis_step * near[3]
            rdr = d0r + coriolis_step * near[0]
            rdi = d0i + coriolis_step * near[1]
        zr, zi = cmul(rzr, rzi, inv_re, inv_im)
        nd_re, nd_im = cmul(shift_re, shift_im, rdr, rdi)
        nd_re = nd_re + grav * h0r
        nd_im = nd_im + grav * h0i
        nh_re = hb_re - grav * rdr
        nh_im = hb_im - grav * rdi
        dr, di = cmul(nd_re, nd_im, dinv_re, dinv_im)
        hr, hi = cmul(nh_re, nh_im, dinv_re, dinv_im)
    parts = []
    for field_re, field_im in ((zr, zi), (dr, di), (hr, hi)):
        out_re, out_im = cmul(weight_re, weight_im, field_re, field_im)
        parts.append(jnp.sum(out_re, axis=0))
        parts.append(jnp.sum(out_im, axis=0))
    return jnp.stack(parts, axis=0)


def lookup(pole_table, chosen):
    columns = jnp.arange(pole_table.shape[1], dtype=jnp.int32)
    onehot = (chosen[:, None] == columns[None, :]).astype(jnp.float32)
    return jnp.dot(onehot, jnp.transpose(pole_table), precision=lax.Precision.HIGHEST)


def shards(grid, legendre, wave_table, pole_table, pole_index):
    slots = legendre.shape[0]
    local_k = legendre.shape[3]
    lat_rows = grid.shape[2]
    wave_count = lax.axis_size("wave")
    half_count = wave_count // 2
    columns = jnp.take(grid, wave_table, axis=1)
    regrouped = lax.all_to_all(columns[None], "wave", split_axis=2, concat_axis=0, tiled=True)
    north = regrouped[:half_count]
    south = regrouped[half_count:]
    parts = jnp.stack([north + south, north - south], axis=0)
    high, low = split_high(parts)
    leg_blocks = legendre.reshape(slots, 2, half_count, lat_rows, local_k)
    first = jnp.einsum("mpwlk,pwcml->cpmk", leg_blocks, high, preferred_element_type=jnp.float32)
    second = jnp.einsum("mpwlk,pwcml->cpmk", leg_blocks, low, preferred_element_type=jnp.float32)
    spectra = first + second
    own_waves = lax.dynamic_slice_in_dim(wave_table, lax.axis_index("wave") * slots, slots).astype(
        jnp.float32
    )
    pole_count = lax.axis_size("pole")
    pole_pos = lax.axis_index("pole")
    rightward = [(i, i + 1) for i in range(pole_count - 1)]
    leftward = [(i + 1, i) for i in range(pole_count - 1)]
    left_halo = lax.ppermute(spectra[..., local_k - HALO :], "pole", rightward)
    right_halo = lax.ppermute(spectra[..., :HALO], "pole", leftward)
    gap = jnp.zeros(spectra.shape[:3] + (RING - local_k - 2 * HALO,), jnp.float32)
    wide = jnp.concatenate([spectra, right_halo, gap, left_halo], axis=3)
    coef = coefficients(own_waves, pole_pos * local_k, local_k, local_k * pole_count)
    poles = jnp.take(pole_table, pole_index, axis=1)
    return solve_poles(poles, wide, coef, local_k)


def solution(mesh):
    in_specs = (P(None, None, "wave"), P("wave", None, None, "pole"), P(), P(), P())
    out_specs = P(None, None, "wave", "pole")
    return jax.shard_map(shards, mesh=mesh, in_specs=in_specs, out_specs=out_specs, check_vma=False)
```

profile of v0, /device:TPU:6, one launch (start us, length us, event | category | flops | bytes accessed | tf_op | source)
XLA Modules:
  0.0 88.0 jit_solution(13291747715761512905)
XLA Ops:
  0.0 0.7 compare_select_fusion
  0.7 0.7 compare_and_fusion.2
  1.4 2.9 %copy.23 = f32[6,256,192]{2,0,1:T(8,128)} copy(f32[6,256,192]{1,2,0:T(8,128)} %param.5) | data formatting | bytes 2359296 | tf_op args[0]
  4.2 2.3 %gather_fusion.1 = f32[256,6,192]{2,1,0:T(8,128)S(1)} fusion(f32[6,256,192]{2,0,1:T(8,128)} %copy.23, s32[1024]{0:T(1024)S(1)} %pad_clamp_fusion), kind=kCustom, calls=%fused_computation.1 | custom fusion | bytes 2360320 | tf_op jit(solution)/shard_map/jit(_take)/gather | solution.py:211
  6.6 0.3 bitcast_select_fusion
  6.9 2.8 %copy.24 = f32[1,6,256,192]{3,0,1,2:T(1,128)} copy(f32[1,6,256,192]{3,1,2,0:T(8,128)S(1)} %bitcast_select_fusion) | data formatting | bytes 2359296 | tf_op jit(solution)/shard_map/jit(_take)/select_n | solution.py:211
  9.7 6.1 %all-to-all-start = ((f32[1,6,256,192]{3,0,1,2:T(1,128)}), f32[1,6,256,192]{3,0,1,2:T(1,128)S(1)}, u32[]{:S(2)}, u32[]{:S(2)}) async-start(f32[1,6,256,192]{3,0,1,2:T(1,128)} %copy.24), calls=%async_computation | async-start | bytes 3145728 | tf_op jit(solution)/shard_map/all_to_all | solution.py:212
  15.9 0.1 copy.21
  16.0 0.6 gather_fusion
  16.8 0.6 select_bitcast_fusion.poles_ref
  17.5 0.1 fusion.27
  17.6 20.3 %all-to-all-done = f32[1,6,256,192]{3,0,1,2:T(1,128)S(1)} async-done(((f32[1,6,256,192]{3,0,1,2:T(1,128)}), f32[1,6,256,192]{3,0,1,2:T(1,128)S(1)}, u32[]{:S(2)}, u32[]{:S(2)}) %all-to-all-start) | async-done | bytes 1179680 | tf_op jit(solution)/shard_map/all_to_all | solution.py:212
  37.9 0.1 copy.25
  38.1 0.9 %copy.46 = f32[1,6,16,16,192]{4,1,2,3,0:T(8,128)S(1)} copy(f32[1,6,16,16,192]{4,3,2,1,0:T(8,128)S(1)} %bitcast.29) | data formatting | bytes 2359296 | tf_op jit(solution)/shard_map/all_to_all | solution.py:212
  39.0 0.2 add_bitcast_fusion
  39.3 0.2 fusion.4
  39.5 6.9 %fusion.5 = f32[2,16,6,128]{3,2,1,0:T(8,128)S(1)} fusion(bf16[2,8,6,16,192]{4,2,1,3,0:T(8,128)(2,1)S(1)} %fusion.4, bf16[16,2,8,192,128]{4,3,2,1,0:T(8,128)(2,1)} %bitcast.24), kind=kOutput, calls=%fused_computation.11 | convolution fusion | flops 75497472 | bytes 13271040 | tf_op jit(solution)/shard_map/mpwlk,pwcml->cpmk/dot_general | solution.py:218
  46.5 2.2 %fusion.8 = f32[2,16,6,128]{3,2,1,0:T(8,128)S(1)} fusion(bf16[16,2,8,192,128]{4,3,2,1,0:T(8,128)(2,1)S(1)} %bitcast.27, bf16[2,8,6,16,192]{4,2,1,3,0:T(8,128)(2,1)S(1)} %fusion.4, f32[1,8,6,16,192]{4,2,1,3,0:T(8,128)S(1)} %get-tuple-element.8, f32[1,8,6,16,192]{4,2,1,3,0:T(8,128)S(1)} %get-tuple-element.7), kind=kOutput, calls=%fused_computation.12 | convolution fusion | flops 76677120 | bytes 14450688 | tf_op jit(solution)/shard_map/mpwlk,pwcml->cpmk/dot_general | solution.py:219
  48.8 5.5 %collective-permute-start.1 = (f32[6,2,16,8]{3,2,1,0:T(8,128)S(1)}, f32[6,2,16,8]{3,2,1,0:T(8,128)S(1)}, u32[]{:S(2)}, u32[]{:S(2)}) collective-permute-start(f32[6,2,16,8]{3,2,1,0:T(8,128)S(1)} %get-tuple-element.10), channel_id=1, source_target_pairs={{0,1},{1,2},{2,3},{3,4},{4,5},{5,6},{6,7},{8,9},{9,10},{10,11},{11... | collective-permute-start | bytes 18440 | tf_op jit(solution)/shard_map/ppermute | solution.py:228
  54.3 2.8 %collective-permute-start = (f32[6,2,16,8]{3,2,1,0:T(8,128)S(1)}, f32[6,2,16,8]{3,2,1,0:T(8,128)S(1)}, u32[]{:S(2)}, u32[]{:S(2)}) collective-permute-start(f32[6,2,16,8]{3,2,1,0:T(8,128)S(1)} %get-tuple-element.9), channel_id=1, source_target_pairs={{1,0},{2,1},{3,2},{4,3},{5,4},{6,5},{7,6},{9,8},{10,9},{11,10},{12... | collective-permute-start | bytes 18440 | tf_op jit(solution)/shard_map/ppermute | solution.py:229
  57.1 0.7 pad_maximum_fusion.2.coef_ref
  57.8 4.5 %collective-permute-done = f32[6,2,16,8]{3,2,1,0:T(8,128)S(1)} collective-permute-done((f32[6,2,16,8]{3,2,1,0:T(8,128)S(1)}, f32[6,2,16,8]{3,2,1,0:T(8,128)S(1)}, u32[]{:S(2)}, u32[]{:S(2)}) %collective-permute-start) | collective-permute-done | bytes 6176 | tf_op jit(solution)/shard_map/ppermute | solution.py:229
  62.3 0.8 pad_maximum_fusion.1.spec_ref
  63.1 24.9 %shard_map.55 = f32[6,2,16,128]{3,2,1,0:T(8,128)} custom-call(f32[4,32]{1,0:T(4,128)} %select_bitcast_fusion.poles_ref, f32[6,2,16,256]{3,2,1,0:T(8,128)} %pad_maximum_fusion.1.spec_ref, f32[4,2,16,256]{3,2,1,0:T(8,128)} %pad_maximum_fusion.2.coef_ref), custom_call_target="tpu_custom_call" | custom-call | tf_op jit(solution)/shard_map/pallas_call | solution.py:127
  (30 shorter events, 0.7 us)
Async XLA Ops:
  9.7 6.1 %copy-start.2 = (s32[32]{0:T(128)S(1)}, s32[32]{0:T(128)}, u32[]{:S(2)}) copy-start(s32[32]{0:T(128)} %param.9) | copy-start | bytes 388
  9.7 6.2 %copy-start.1 = (f32[4,64]{1,0:T(4,128)S(1)}, f32[4,64]{1,0:T(4,128)}, u32[]{:S(2)}) copy-start(f32[4,64]{1,0:T(4,128)} %param.8) | copy-start | bytes 3076
  9.7 6.9 %copy-start = (s32[256]{0:T(256)S(1)}, s32[256]{0:T(256)}, u32[]{:S(2)}) copy-start(s32[256]{0:T(256)} %param.7) | copy-start | bytes 3076
  9.7 28.2 %all-to-all-start = ((f32[1,6,256,192]{3,0,1,2:T(1,128)}), f32[1,6,256,192]{3,0,1,2:T(1,128)S(1)}, u32[]{:S(2)}, u32[]{:S(2)}) async-start(f32[1,6,256,192]{3,0,1,2:T(1,128)} %copy.24), calls=%async_computation | async-start | bytes 3145728 | tf_op jit(solution)/shard_map/all_to_all | solution.py:212
  38.0 8.3 %slice-start = ((s8[12582912]{0:T(1024)(128)(4,1)}), s8[4194304]{0:T(1024)(128)(4,1)S(1)}, s32[]{:S(2)}) async-start(s8[12582912]{0:T(1024)(128)(4,1)} %bitcast.25), calls=%async_computation.1 | async-start | bytes 8388608
  39.2 7.2 %slice-start.1 = ((s8[12582912]{0:T(1024)(128)(4,1)}), s8[4194304]{0:T(1024)(128)(4,1)S(1)}, s32[]{:S(2)}) async-start(s8[12582912]{0:T(1024)(128)(4,1)} %bitcast.25), calls=%async_computation.2 | async-start | bytes 8388608
  39.5 6.9 %slice-start.2 = ((s8[12582912]{0:T(1024)(128)(4,1)}), s8[4194304]{0:T(1024)(128)(4,1)S(1)}, s32[]{:S(2)}) async-start(s8[12582912]{0:T(1024)(128)(4,1)} %bitcast.25), calls=%async_computation.3 | async-start | bytes 8388608
  48.8 9.0 %collective-permute-start.1 = (f32[6,2,16,8]{3,2,1,0:T(8,128)S(1)}, f32[6,2,16,8]{3,2,1,0:T(8,128)S(1)}, u32[]{:S(2)}, u32[]{:S(2)}) collective-permute-start(f32[6,2,16,8]{3,2,1,0:T(8,128)S(1)} %get-tuple-element.10), channel_id=1, source_target_pairs={{0,1},{1,2},{2,3},{3,4},{4,5},{5,6},{6,7},{8,9},{9,10},{10,11},{11... | collective-permute-start | bytes 18440 | tf_op jit(solution)/shard_map/ppermute | solution.py:228
  54.3 8.0 %collective-permute-start = (f32[6,2,16,8]{3,2,1,0:T(8,128)S(1)}, f32[6,2,16,8]{3,2,1,0:T(8,128)S(1)}, u32[]{:S(2)}, u32[]{:S(2)}) collective-permute-start(f32[6,2,16,8]{3,2,1,0:T(8,128)S(1)} %get-tuple-element.9), channel_id=1, source_target_pairs={{1,0},{2,1},{3,2},{4,3},{5,4},{6,5},{7,6},{9,8},{10,9},{11,10},{12... | collective-permute-start | bytes 18440 | tf_op jit(solution)/shard_map/ppermute | solution.py:229
where the time goes:
time: 88.4 us; the launch traced here: 88 us
  Pallas kernels  24.9 us (28%)
  waiting for transfers between devices  24.8 us (28%)
  starting transfers between devices  14.3 us (16%)
  local copies, waits for them, and re-layouts  10.1 us (11%)
  matrix products  9.08 us (10%)
  other arithmetic  4.64 us (5%)
    pallas_call x1, Pallas kernels, solve_poles(): pl.pallas_call(pole_kernel, out_shape=jax.ShapeDtypeStruct((comps, pariti...  24.9 us
    all_to_all x1, waiting for transfers between devices, shards(): lax.all_to_all(columns[None], 'wave', split_axis=2, concat_axis=0, tiled=...  20.3 us
    dot_general x1, matrix products, shards(): jnp.einsum('mpwlk,pwcml->cpmk', leg_blocks, high, preferred_element_type=...  6.86 us
    all_to_all x1, starting transfers between devices, shards(): lax.all_to_all(columns[None], 'wave', split_axis=2, concat_axis=0, tiled=...  6.06 us
    ppermute x1, starting transfers between devices, shards(): left_halo = lax.ppermute(spectra[..., local_k - HALO:], 'pole', rightward)  5.49 us
    ppermute x1, waiting for transfers between devices, shards(): right_halo = lax.ppermute(spectra[..., :HALO], 'pole', leftward)  4.51 us
    unnamed x14, local copies, waits for them, and re-layouts  3.05 us
    select_n x1, local copies, waits for them, and re-layouts, shards(): columns = jnp.take(grid, wave_table, axis=1)  2.79 us
  transfers between devices with their start and end apart: 3, of which 2 were waited for; matrix products, arithmetic and copies ran while one was open for 3% of the time, Pallas kernels for 0%

commit v1 on v0

--- a/solution.py
+++ b/solution.py
@@ -69,46 +69,47 @@
                 n1 = ld(coef_ref, 0, 1) * x[0] + ld(coef_ref, 1, 1) * pltpu.roll(x[0], lanes - 1, 1)
                 return (n0, n1)
 
-            inv, dinv, hb = [], [], []
+            inv, dinv, lift, base = [], [], [], []
             for p in range(2):
                 grav = ld(coef_ref, 3, p)
                 b_im = a_im + ld(coef_ref, 2, p)
-                b_mag = a_re * a_re + b_im * b_im
-                inv.append((a_re / b_mag, -b_im / b_mag))
+                b_rec = 1.0 / (a_re * a_re + b_im * b_im)
+                inv.append((a_re * b_rec, -b_im * b_rec))
                 det_re = a_re * a_re - b_im * a_im + grav * grav
                 det_im = a_re * a_im + b_im * a_re
-                det_mag = det_re * det_re + det_im * det_im
-                dinv.append((det_re / det_mag, -det_im / det_mag))
-                h0r = ld(spec_ref, 4, p)
-                h0i = ld(spec_ref, 5, p)
-                hb.append((a_re * h0r - b_im * h0i, a_re * h0i + b_im * h0r))
-            zr = zi = dr = di = hr = hi = None
+                det_rec = 1.0 / (det_re * det_re + det_im * det_im)
+                dv = (det_re * det_rec, -det_im * det_rec)
+                dinv.append(dv)
+                lift.append(cmul(a_re, a_im, dv[0], dv[1]))
+                base.append(cmul(ld(spec_ref, 6, p), ld(spec_ref, 7, p), dv[0], dv[1]))
+            zr = zi = dr = di = None
             for sweep in range(SWEEPS):
                 if sweep > 0:
                     nzr, nzi, ndr, ndi = near(zr), near(zi), near(dr), near(di)
-                zr, zi, dr, di, hr, hi = [], [], [], [], [], []
+                zr, zi, dr, di = [], [], [], []
+                hr, hi = [], []
                 for p in range(2):
                     if sweep == 0:
                         rzr, rzi = ld(spec_ref, 0, p), ld(spec_ref, 1, p)
                         rdr, rdi = ld(spec_ref, 2, p), ld(spec_ref, 3, p)
                     else:
-                        rzr = ld(spec_ref, 0, p) - coriolis_step * ndr[p]
-                        rzi = ld(spec_ref, 1, p) - coriolis_step * ndi[p]
-                        rdr = ld(spec_ref, 2, p) + coriolis_step * nzr[p]
-                        rdi = ld(spec_ref, 3, p) + coriolis_step * nzi[p]
+                        rzr = ld(spec_ref, 0, p) - ndr[p]
+                        rzi = ld(spec_ref, 1, p) - ndi[p]
+                        rdr = ld(spec_ref, 2, p) + nzr[p]
+                        rdi = ld(spec_ref, 3, p) + nzi[p]
                     z_re, z_im = cmul(rzr, rzi, inv[p][0], inv[p][1])
                     zr.append(z_re)
                     zi.append(z_im)
-                    grav = ld(coef_ref, 3, p)
-                    nd_re, nd_im = cmul(a_re, a_im, rdr, rdi)
-                    nd_re = nd_re + grav * ld(spec_ref, 4, p)
-                    nd_im = nd_im + grav * ld(spec_ref, 5, p)
-                    d_re, d_im = cmul(nd_re, nd_im, dinv[p][0], dinv[p][1])
-                    dr.append(d_re)
-                    di.append(d_im)
+                    d_re, d_im = cmul(lift[p][0], lift[p][1], rdr, rdi)
+                    dr.append(d_re + base[p][0])
+                    di.append(d_im + base[p][1])
                     if sweep == SWEEPS - 1:
-                        nh_re = hb[p][0] - grav * rdr
-                        nh_im = hb[p][1] - grav * rdi
+                        grav = ld(coef_ref, 3, p)
+                        b_im = a_im + ld(coef_ref, 2, p)
+                        h0r = ld(spec_ref, 4, p)
+                        h0i = ld(spec_ref, 5, p)
+                        nh_re = a_re * h0r - b_im * h0i - grav * rdr
+                        nh_im = a_re * h0i + b_im * h0r - grav * rdi
                         h_re, h_im = cmul(nh_re, nh_im, dinv[p][0], dinv[p][1])
                         hr.append(h_re)
                         hi.append(h_im)
@@ -123,10 +124,10 @@
 
 
 def solve_poles(poles, wide, coef, width):
-    comps, parities, rows, _ = wide.shape
+    _, parities, rows, _ = wide.shape
     return pl.pallas_call(
         pole_kernel,
-        out_shape=jax.ShapeDtypeStruct((comps, parities, rows, width), jnp.float32),
+        out_shape=jax.ShapeDtypeStruct((6, parities, rows, width), jnp.float32),
         in_specs=[
             pl.BlockSpec(memory_space=pltpu.SMEM),
             pl.BlockSpec(memory_space=pltpu.VMEM),
@@ -215,9 +216,10 @@
     parts = jnp.stack([north + south, north - south], axis=0)
     high, low = split_high(parts)
     leg_blocks = legendre.reshape(slots, 2, half_count, lat_rows, local_k)
-    first = jnp.einsum("mpwlk,pwcml->cpmk", leg_blocks, high, preferred_element_type=jnp.float32)
-    second = jnp.einsum("mpwlk,pwcml->cpmk", leg_blocks, low, preferred_element_type=jnp.float32)
-    spectra = first + second
+    both = jnp.concatenate([high, low], axis=2)
+    products = jnp.einsum("mpwlk,pwcml->cpmk", leg_blocks, both, preferred_element_type=jnp.float32)
+    comps = high.shape[2]
+    spectra = products[:comps] + products[comps:]
     own_waves = lax.dynamic_slice_in_dim(wave_table, lax.axis_index("wave") * slots, slots).astype(
         jnp.float32
     )
@@ -230,6 +232,8 @@
     gap = jnp.zeros(spectra.shape[:3] + (RING - local_k - 2 * HALO,), jnp.float32)
     wide = jnp.concatenate([spectra, right_halo, gap, left_halo], axis=3)
     coef = coefficients(own_waves, pole_pos * local_k, local_k, local_k * pole_count)
+    wide = jnp.concatenate([wide, coef[3][None] * wide[4:6]], axis=0)
+    coef = jnp.concatenate([coriolis_step * coef[:2], coef[2:]], axis=0)
     poles = jnp.take(pole_table, pole_index, axis=1)
     return solve_poles(poles, wide, coef, local_k)
 

time: 88.4 us -> 83.4 us (0.943)
  matrix products: 9.08 us -> 5.71 us
  Pallas kernels: 24.9 us -> 21.6 us
  waiting for transfers between devices: 24.8 us -> 26.5 us
    ppermute x1, waiting for transfers between devices: 0.01 us -> 6.32 us  [shards(): left_halo = lax.ppermute(spectra[..., local_k - HALO:], 'pole', rightward)]
    ppermute x1, waiting for transfers between devices: 4.51 us -> 0.01 us  [shards(): right_halo = lax.ppermute(spectra[..., :HALO], 'pole', leftward)]
    ppermute x1, starting transfers between devices: 5.49 us -> 1.92 us  [shards(): left_halo = lax.ppermute(spectra[..., local_k - HALO:], 'pole', rightward)]
    dot_general x2 -> x1, matrix products: 9.08 us -> 5.71 us  [shards(): jnp.einsum('mpwlk,pwcml->cpmk', leg_blocks, both, preferred_element_type=...]
    pallas_call x1, Pallas kernels: 24.9 us -> 21.6 us  [solve_poles(): pl.pallas_call(pole_kernel, out_shape=jax.ShapeDtypeStruct((6, parities,...]
    ppermute x1, starting transfers between devices: 2.75 us -> 5.76 us  [shards(): right_halo = lax.ppermute(spectra[..., :HALO], 'pole', leftward)]
    unnamed x14 -> x8, local copies, waits for them, and re-layouts: 3.05 us -> 2.98 us
where the time goes in v1:
time: 83.4 us; the launch traced here: 83.1 us
  waiting for transfers between devices  26.5 us (32%)
  Pallas kernels  21.6 us (26%)
  starting transfers between devices  13.7 us (16%)
  local copies, waits for them, and re-layouts  9.99 us (12%)
  matrix products  5.71 us (7%)
  other arithmetic  5.33 us (6%)
    pallas_call x1, Pallas kernels, solve_poles(): pl.pallas_call(pole_kernel, out_shape=jax.ShapeDtypeStruct((6, parities,...  21.6 us
    all_to_all x1, waiting for transfers between devices, shards(): lax.all_to_all(columns[None], 'wave', split_axis=2, concat_axis=0, tiled=...  20.2 us
    ppermute x1, waiting for transfers between devices, shards(): left_halo = lax.ppermute(spectra[..., local_k - HALO:], 'pole', rightward)  6.32 us
    all_to_all x1, starting transfers between devices, shards(): lax.all_to_all(columns[None], 'wave', split_axis=2, concat_axis=0, tiled=...  6.06 us
    ppermute x1, starting transfers between devices, shards(): right_halo = lax.ppermute(spectra[..., :HALO], 'pole', leftward)  5.76 us
    dot_general x1, matrix products, shards(): jnp.einsum('mpwlk,pwcml->cpmk', leg_blocks, both, preferred_element_type=...  5.71 us
    unnamed x8, local copies, waits for them, and re-layouts  2.98 us
    select_n x1, local copies, waits for them, and re-layouts, shards(): columns = jnp.take(grid, wave_table, axis=1)  2.77 us
  transfers between devices with their start and end apart: 3, of which 2 were waited for; matrix products, arithmetic and copies ran while one was open for 3% of the time, Pallas kernels for 0%

profile of v1, /device:TPU:6, one launch (start us, length us, event | category | flops | bytes accessed | tf_op | source)
XLA Modules:
  0.0 83.1 jit_solution(1467449392102722236)
XLA Ops:
  0.0 0.7 compare_select_fusion
  0.7 0.7 compare_and_fusion.2
  1.4 2.9 %copy.19 = f32[6,256,192]{2,0,1:T(8,128)} copy(f32[6,256,192]{1,2,0:T(8,128)} %param.5) | data formatting | bytes 2359296 | tf_op args[0]
  4.2 2.3 %gather_fusion.1 = f32[256,6,192]{2,1,0:T(8,128)S(1)} fusion(f32[6,256,192]{2,0,1:T(8,128)} %copy.19, s32[1024]{0:T(1024)S(1)} %pad_clamp_fusion), kind=kCustom, calls=%fused_computation.1 | custom fusion | bytes 2360320 | tf_op jit(solution)/shard_map/jit(_take)/gather | solution.py:212
  6.6 0.3 bitcast_select_fusion
  6.9 2.8 %copy.20 = f32[1,6,256,192]{3,0,1,2:T(1,128)} copy(f32[1,6,256,192]{3,1,2,0:T(8,128)S(1)} %bitcast_select_fusion) | data formatting | bytes 2359296 | tf_op jit(solution)/shard_map/jit(_take)/select_n | solution.py:212
  9.7 6.1 %all-to-all-start = ((f32[1,6,256,192]{3,0,1,2:T(1,128)}), f32[1,6,256,192]{3,0,1,2:T(1,128)S(1)}, u32[]{:S(2)}, u32[]{:S(2)}) async-start(f32[1,6,256,192]{3,0,1,2:T(1,128)} %copy.20), calls=%async_computation | async-start | bytes 3145728 | tf_op jit(solution)/shard_map/all_to_all | solution.py:213
  16.1 0.1 copy.17
  16.2 0.6 gather_fusion
  16.9 0.1 fusion.29
  17.0 0.6 select_bitcast_fusion.poles_ref
  17.7 20.2 %all-to-all-done = f32[1,6,256,192]{3,0,1,2:T(1,128)S(1)} async-done(((f32[1,6,256,192]{3,0,1,2:T(1,128)}), f32[1,6,256,192]{3,0,1,2:T(1,128)S(1)}, u32[]{:S(2)}, u32[]{:S(2)}) %all-to-all-start) | async-done | bytes 1179680 | tf_op jit(solution)/shard_map/all_to_all | solution.py:213
  37.9 0.1 copy.21
  38.0 0.9 %copy.32 = f32[1,6,16,16,192]{4,1,2,3,0:T(8,128)S(1)} copy(f32[1,6,16,16,192]{4,3,2,1,0:T(8,128)S(1)} %bitcast.22) | data formatting | bytes 2359296 | tf_op jit(solution)/shard_map/all_to_all | solution.py:213
  39.0 0.2 add_bitcast_fusion
  39.2 0.2 fusion.5
  39.5 0.5 subtract_convert_fusion
  40.0 5.7 %fusion.6 = f32[2,16,12,128]{3,2,1,0:T(8,128)S(1)} fusion(bf16[16,2,8,192,128]{4,3,2,1,0:T(8,128)(2,1)} %bitcast.24, bf16[2,8,6,16,192]{4,2,1,3,0:T(8,128)(2,1)S(1)} %subtract_convert_fusion, bf16[2,8,6,16,192]{4,2,1,3,0:T(8,128)(2,1)S(1)} %fusion.5), kind=kOutput, calls=%fused_computation.12 | convolution fusion | flops 153354240 | bytes 13959168 | tf_op jit(solution)/shard_map/mpwlk,pwcml->cpmk/dot_general | solution.py:220
  45.9 5.8 %collective-permute-start = (f32[6,2,16,8]{3,2,1,0:T(8,128)S(1)}, f32[6,2,16,8]{3,2,1,0:T(8,128)S(1)}, u32[]{:S(2)}, u32[]{:S(2)}) collective-permute-start(f32[6,2,16,8]{3,2,1,0:T(8,128)S(1)} %get-tuple-element.9), channel_id=1, source_target_pairs={{1,0},{2,1},{3,2},{4,3},{5,4},{6,5},{7,6},{9,8},{10,9},{11,10},{12... | collective-permute-start | bytes 18440 | tf_op jit(solution)/shard_map/ppermute | solution.py:231
  51.6 1.9 %collective-permute-start.1 = (f32[6,2,16,8]{3,2,1,0:T(8,128)S(1)}, f32[6,2,16,8]{3,2,1,0:T(8,128)S(1)}, u32[]{:S(2)}, u32[]{:S(2)}) collective-permute-start(f32[6,2,16,8]{3,2,1,0:T(8,128)S(1)} %get-tuple-element.10), channel_id=1, source_target_pairs={{0,1},{1,2},{2,3},{3,4},{4,5},{5,6},{6,7},{8,9},{9,10},{10,11},{11... | collective-permute-start | bytes 18440 | tf_op jit(solution)/shard_map/ppermute | solution.py:230
  53.6 0.7 pad_maximum_fusion.2.coef_ref
  54.2 6.3 %collective-permute-done.1 = f32[6,2,16,8]{3,2,1,0:T(8,128)S(1)} collective-permute-done((f32[6,2,16,8]{3,2,1,0:T(8,128)S(1)}, f32[6,2,16,8]{3,2,1,0:T(8,128)S(1)}, u32[]{:S(2)}, u32[]{:S(2)}) %collective-permute-start.1) | collective-permute-done | bytes 6176 | tf_op jit(solution)/shard_map/ppermute | solution.py:230
  60.7 0.8 %pad_maximum_fusion.1.spec_ref = f32[8,2,16,256]{3,2,1,0:T(8,128)} fusion(f32[2,2,16,256]{3,2,1,0:T(8,128)S(1)} %fusion.11, f32[6,2,16,8]{3,2,1,0:T(8,128)S(1)} %collective-permute-done.1, f32[6,2,16,112]{3,2,1,0:T(8,128)S(1)} %broadcast_in_dim.62, f32[6,2,16,8]{3,2,1,0:T(8,128)S(1)} %collective-permute-done, f32[6,2,16,128]{3,2,1,0:T(8,128)S(1)} %slice_add_fusion), kind=kLoop, calls=%fused_computation.15 | loop fusion | flops 262144 | bytes 524288 | tf_op jit(solution)/shard_map/concatenate | solution.py:235
  61.5 21.6 %shard_map.55 = f32[6,2,16,128]{3,2,1,0:T(8,128)} custom-call(f32[4,32]{1,0:T(4,128)} %select_bitcast_fusion.poles_ref, f32[8,2,16,256]{3,2,1,0:T(8,128)} %pad_maximum_fusion.1.spec_ref, f32[4,2,16,256]{3,2,1,0:T(8,128)} %pad_maximum_fusion.2.coef_ref), custom_call_target="tpu_custom_call" | custom-call | tf_op jit(solution)/shard_map/pallas_call | solution.py:128
  (26 shorter events, 0.7 us)
Async XLA Ops:
  9.7 6.1 %copy-start = (s32[256]{0:T(256)S(1)}, s32[256]{0:T(256)}, u32[]{:S(2)}) copy-start(s32[256]{0:T(256)} %param.7) | copy-start | bytes 3076
  9.7 6.4 %copy-start.1 = (f32[4,64]{1,0:T(4,128)S(1)}, f32[4,64]{1,0:T(4,128)}, u32[]{:S(2)}) copy-start(f32[4,64]{1,0:T(4,128)} %param.8) | copy-start | bytes 3076
  9.7 6.5 %copy-start.2 = (s32[32]{0:T(128)S(1)}, s32[32]{0:T(128)}, u32[]{:S(2)}) copy-start(s32[32]{0:T(128)} %param.9) | copy-start | bytes 388
  9.7 28.2 %all-to-all-start = ((f32[1,6,256,192]{3,0,1,2:T(1,128)}), f32[1,6,256,192]{3,0,1,2:T(1,128)S(1)}, u32[]{:S(2)}, u32[]{:S(2)}) async-start(f32[1,6,256,192]{3,0,1,2:T(1,128)} %copy.20), calls=%async_computation | async-start | bytes 3145728 | tf_op jit(solution)/shard_map/all_to_all | solution.py:213
  45.9 8.4 %collective-permute-start = (f32[6,2,16,8]{3,2,1,0:T(8,128)S(1)}, f32[6,2,16,8]{3,2,1,0:T(8,128)S(1)}, u32[]{:S(2)}, u32[]{:S(2)}) collective-permute-start(f32[6,2,16,8]{3,2,1,0:T(8,128)S(1)} %get-tuple-element.9), channel_id=1, source_target_pairs={{1,0},{2,1},{3,2},{4,3},{5,4},{6,5},{7,6},{9,8},{10,9},{11,10},{12... | collective-permute-start | bytes 18440 | tf_op jit(solution)/shard_map/ppermute | solution.py:231
  51.6 8.9 %collective-permute-start.1 = (f32[6,2,16,8]{3,2,1,0:T(8,128)S(1)}, f32[6,2,16,8]{3,2,1,0:T(8,128)S(1)}, u32[]{:S(2)}, u32[]{:S(2)}) collective-permute-start(f32[6,2,16,8]{3,2,1,0:T(8,128)S(1)} %get-tuple-element.10), channel_id=1, source_target_pairs={{0,1},{1,2},{2,3},{3,4},{4,5},{5,6},{6,7},{8,9},{9,10},{10,11},{11... | collective-permute-start | bytes 18440 | tf_op jit(solution)/shard_map/ppermute | solution.py:230

commit v2 on v1

--- a/solution.py
+++ b/solution.py
@@ -209,16 +209,20 @@
     lat_rows = grid.shape[2]
     wave_count = lax.axis_size("wave")
     half_count = wave_count // 2
-    columns = jnp.take(grid, wave_table, axis=1)
-    regrouped = lax.all_to_all(columns[None], "wave", split_axis=2, concat_axis=0, tiled=True)
+    waves = grid.shape[1]
+    comps = grid.shape[0]
+    onehot = (wave_table[:, None] == jnp.arange(waves, dtype=jnp.int32)[None, :]).astype(jnp.float32)
+    columns = jnp.einsum("sm,cml->scl", onehot, grid, precision=lax.Precision.HIGHEST)
+    columns = columns.reshape(waves, comps * lat_rows)
+    regrouped = lax.all_to_all(columns, "wave", split_axis=0, concat_axis=0, tiled=True)
+    regrouped = regrouped.reshape(wave_count, slots, comps, lat_rows)
     north = regrouped[:half_count]
     south = regrouped[half_count:]
     parts = jnp.stack([north + south, north - south], axis=0)
     high, low = split_high(parts)
     leg_blocks = legendre.reshape(slots, 2, half_count, lat_rows, local_k)
-    both = jnp.concatenate([high, low], axis=2)
-    products = jnp.einsum("mpwlk,pwcml->cpmk", leg_blocks, both, preferred_element_type=jnp.float32)
-    comps = high.shape[2]
+    both = jnp.concatenate([high, low], axis=3)
+    products = jnp.einsum("mpwlk,pwmcl->cpmk", leg_blocks, both, preferred_element_type=jnp.float32)
     spectra = products[:comps] + products[comps:]
     own_waves = lax.dynamic_slice_in_dim(wave_table, lax.axis_index("wave") * slots, slots).astype(
         jnp.float32

time: 83.4 us -> 74.8 us (0.90)
  local copies, waits for them, and re-layouts: 9.99 us -> 4.18 us
  waiting for transfers between devices: 26.5 us -> 22.3 us
  matrix products: 5.71 us -> 8.31 us
  other arithmetic: 5.33 us -> 4.28 us
    all_to_all x1, waiting for transfers between devices: 20.2 us -> 16 us  [shards(): lax.all_to_all(columns, 'wave', split_axis=0, concat_axis=0, tiled=True)]
    select_n x1 -> x0, local copies, waits for them, and re-layouts: 2.77 us -> none  [shards(): columns = jnp.take(grid, wave_table, axis=1)]
    unnamed x0 -> x1, matrix products: none -> 2.59 us
    gather x1 -> x0, local copies, waits for them, and re-layouts: 2.34 us -> none  [shards(): columns = jnp.take(grid, wave_table, axis=1)]
    unnamed x8 -> x9, local copies, waits for them, and re-layouts: 2.98 us -> 1.38 us
    sub x0 -> x1, local copies, waits for them, and re-layouts: none -> 1.46 us  [shards(): parts = jnp.stack([north + south, north - south], axis=0)]
    all_to_all x2 -> x0, local copies, waits for them, and re-layouts: 1.09 us -> none  [shards(): lax.all_to_all(columns[None], 'wave', split_axis=2, concat_axis=0, tiled=...]
    select_n x2 -> x0, other arithmetic: 1.02 us -> none  [shards(): columns = jnp.take(grid, wave_table, axis=1)]
where the time goes in v2:
time: 74.8 us; the launch traced here: 74.5 us
  waiting for transfers between devices  22.3 us (30%)
  Pallas kernels  21.6 us (29%)
  starting transfers between devices  13.6 us (18%)
  matrix products  8.31 us (11%)
  other arithmetic  4.28 us (6%)
  local copies, waits for them, and re-layouts  4.18 us (6%)
    pallas_call x1, Pallas kernels, solve_poles(): pl.pallas_call(pole_kernel, out_shape=jax.ShapeDtypeStruct((6, parities,...  21.6 us
    all_to_all x1, waiting for transfers between devices, shards(): lax.all_to_all(columns, 'wave', split_axis=0, concat_axis=0, tiled=True)  16 us
    ppermute x1, waiting for transfers between devices, shards(): left_halo = lax.ppermute(spectra[..., local_k - HALO:], 'pole', rightward)  6.31 us
    all_to_all x1, starting transfers between devices, shards(): lax.all_to_all(columns, 'wave', split_axis=0, concat_axis=0, tiled=True)  5.93 us
    ppermute x1, starting transfers between devices, shards(): right_halo = lax.ppermute(spectra[..., :HALO], 'pole', leftward)  5.76 us
    dot_general x1, matrix products, shards(): jnp.einsum('mpwlk,pwmcl->cpmk', leg_blocks, both, preferred_element_type=...  5.71 us
    unnamed x1, matrix products  2.59 us
    ppermute x1, starting transfers between devices, shards(): left_halo = lax.ppermute(spectra[..., local_k - HALO:], 'pole', rightward)  1.92 us
  transfers between devices with their start and end apart: 3, of which 2 were waited for; matrix products, arithmetic and copies ran while one was open for 3% of the time, Pallas kernels for 0%

profile of v2, /device:TPU:6, one launch (start us, length us, event | category | flops | bytes accessed | tf_op | source)
XLA Modules:
  0.0 74.5 jit_solution(14665672055029624149)
XLA Ops:
  0.0 1.3 %copy-done = f32[6,256,192]{1,2,0:T(8,128)S(1)} copy-done((f32[6,256,192]{1,2,0:T(8,128)S(1)}, f32[6,256,192]{1,2,0:T(8,128)}, u32[]{:S(2)}) %copy-start) | copy-done | bytes 1179672
  1.3 2.6 %fusion.10 = f32[256,1152]{1,0:T(8,128)} fusion(f32[256,1152]{0,1:T(8,128)S(1)} %bitcast.15, s32[256]{0:T(256)} %param.7), kind=kOutput, calls=%fused_computation.14 | convolution fusion | flops 906035200 | bytes 2360320
  3.9 5.9 %all-to-all-start = ((f32[16,16,1152]{2,1,0:T(8,128)}), f32[16,16,1152]{2,1,0:T(8,128)S(1)}, u32[]{:S(2)}, u32[]{:S(2)}) async-start(f32[16,16,1152]{2,1,0:T(8,128)} %bitcast.9), calls=%async_computation | async-start | bytes 2359296 | tf_op jit(solution)/shard_map/all_to_all | solution.py:217
  10.1 0.1 copy.12
  10.2 0.6 gather_fusion
  10.9 0.1 fusion.30
  11.0 0.6 select_bitcast_fusion.poles_ref
  11.6 0.1 fusion.20
  11.7 16.0 %all-to-all-done = f32[16,16,1152]{2,1,0:T(8,128)S(1)} async-done(((f32[16,16,1152]{2,1,0:T(8,128)}), f32[16,16,1152]{2,1,0:T(8,128)S(1)}, u32[]{:S(2)}, u32[]{:S(2)}) %all-to-all-start) | async-done | bytes 1179680 | tf_op jit(solution)/shard_map/all_to_all | solution.py:217
  27.7 0.9 %slice_add_fusion = (f32[8,16,1152]{2,1,0:T(8,128)S(1)}, f32[8,16,1152]{2,1,0:T(8,128)}) fusion(f32[16,16,1152]{2,1,0:T(8,128)S(1)} %all-to-all-done), kind=kLoop, calls=%fused_computation.11 | loop fusion | flops 294912 | bytes 2359296 | tf_op jit(solution)/shard_map/add | solution.py:221
  28.6 0.4 add.197
  29.0 1.5 %sub.27 = f32[1,8,16,6,192]{4,3,2,1,0:T(8,128)S(1)} reshape(f32[8,16,1152]{2,1,0:T(8,128)} %get-tuple-element.8) | data formatting | bytes 1179648 | tf_op jit(solution)/shard_map/sub | solution.py:221
  30.5 0.3 pad_maximum_fusion
  30.7 0.1 copy.28
  30.9 0.4 subtract_convert_fusion
  31.3 5.7 %fusion.5 = f32[2,16,12,128]{3,2,1,0:T(8,128)S(1)} fusion(bf16[16,2,8,192,128]{4,3,2,1,0:T(8,128)(2,1)} %bitcast.17, bf16[2,8,16,6,192]{4,3,1,2,0:T(8,128)(2,1)S(1)} %subtract_convert_fusion, bf16[2,8,16,6,192]{4,3,1,2,0:T(8,128)(2,1)S(1)} %copy.28), kind=kOutput, calls=%fused_computation.9 | convolution fusion | flops 153354240 | bytes 13959168 | tf_op jit(solution)/shard_map/mpwlk,pwmcl->cpmk/dot_general | solution.py:225
  37.1 0.1 fusion.32
  37.2 5.8 %collective-permute-start = (f32[6,2,16,8]{3,2,1,0:T(8,128)S(1)}, f32[6,2,16,8]{3,2,1,0:T(8,128)S(1)}, u32[]{:S(2)}, u32[]{:S(2)}) collective-permute-start(f32[6,2,16,8]{3,2,1,0:T(8,128)S(1)} %get-tuple-element.9), channel_id=1, source_target_pairs={{1,0},{2,1},{3,2},{4,3},{5,4},{6,5},{7,6},{9,8},{10,9},{11,10},{12... | collective-permute-start | bytes 18440 | tf_op jit(solution)/shard_map/ppermute | solution.py:235
  43.0 1.9 %collective-permute-start.1 = (f32[6,2,16,8]{3,2,1,0:T(8,128)S(1)}, f32[6,2,16,8]{3,2,1,0:T(8,128)S(1)}, u32[]{:S(2)}, u32[]{:S(2)}) collective-permute-start(f32[6,2,16,8]{3,2,1,0:T(8,128)S(1)} %get-tuple-element.10), channel_id=1, source_target_pairs={{0,1},{1,2},{2,3},{3,4},{4,5},{5,6},{6,7},{8,9},{9,10},{10,11},{11... | collective-permute-start | bytes 18440 | tf_op jit(solution)/shard_map/ppermute | solution.py:234
  44.9 0.7 pad_maximum_fusion.2.coef_ref
  45.6 6.3 %collective-permute-done.1 = f32[6,2,16,8]{3,2,1,0:T(8,128)S(1)} collective-permute-done((f32[6,2,16,8]{3,2,1,0:T(8,128)S(1)}, f32[6,2,16,8]{3,2,1,0:T(8,128)S(1)}, u32[]{:S(2)}, u32[]{:S(2)}) %collective-permute-start.1) | collective-permute-done | bytes 6176 | tf_op jit(solution)/shard_map/ppermute | solution.py:234
  51.9 0.1 fusion.12
  52.0 0.8 %pad_maximum_fusion.1.spec_ref = f32[8,2,16,256]{3,2,1,0:T(8,128)} fusion(f32[2,2,16,256]{3,2,1,0:T(8,128)S(1)} %fusion.12, f32[6,2,16,8]{3,2,1,0:T(8,128)S(1)} %collective-permute-done.1, f32[6,2,16,112]{3,2,1,0:T(8,128)S(1)} %broadcast_in_dim.48, f32[6,2,16,8]{3,2,1,0:T(8,128)S(1)} %collective-permute-done, f32[6,2,16,128]{3,2,1,0:T(8,128)S(1)} %slice_add_fusion.1), kind=kLoop, calls=%fused_computation.12 | loop fusion | flops 262144 | bytes 524288 | tf_op jit(solution)/shard_map/concatenate | solution.py:239
  52.8 21.6 %shard_map.55 = f32[6,2,16,128]{3,2,1,0:T(8,128)} custom-call(f32[4,32]{1,0:T(4,128)} %select_bitcast_fusion.poles_ref, f32[8,2,16,256]{3,2,1,0:T(8,128)} %pad_maximum_fusion.1.spec_ref, f32[4,2,16,256]{3,2,1,0:T(8,128)} %pad_maximum_fusion.2.coef_ref), custom_call_target="tpu_custom_call" | custom-call | tf_op jit(solution)/shard_map/pallas_call | solution.py:128
  (23 shorter events, 0.5 us)
Async XLA Ops:
  0.0 1.3 %copy-start = (f32[6,256,192]{1,2,0:T(8,128)S(1)}, f32[6,256,192]{1,2,0:T(8,128)}, u32[]{:S(2)}) copy-start(f32[6,256,192]{1,2,0:T(8,128)} %param.5) | copy-start | bytes 3538948
  1.3 8.6 %copy-start.1 = (s32[256]{0:T(256)S(1)}, s32[256]{0:T(256)}, u32[]{:S(2)}) copy-start(s32[256]{0:T(256)} %param.7) | copy-start | bytes 3076
  1.3 8.8 %copy-start.2 = (f32[4,64]{1,0:T(4,128)S(1)}, f32[4,64]{1,0:T(4,128)}, u32[]{:S(2)}) copy-start(f32[4,64]{1,0:T(4,128)} %param.8) | copy-start | bytes 3076
  1.3 8.9 %copy-start.3 = (s32[32]{0:T(128)S(1)}, s32[32]{0:T(128)}, u32[]{:S(2)}) copy-start(s32[32]{0:T(128)} %param.9) | copy-start | bytes 388
  3.9 23.8 %all-to-all-start = ((f32[16,16,1152]{2,1,0:T(8,128)}), f32[16,16,1152]{2,1,0:T(8,128)S(1)}, u32[]{:S(2)}, u32[]{:S(2)}) async-start(f32[16,16,1152]{2,1,0:T(8,128)} %bitcast.9), calls=%async_computation | async-start | bytes 2359296 | tf_op jit(solution)/shard_map/all_to_all | solution.py:217
  37.2 8.4 %collective-permute-start = (f32[6,2,16,8]{3,2,1,0:T(8,128)S(1)}, f32[6,2,16,8]{3,2,1,0:T(8,128)S(1)}, u32[]{:S(2)}, u32[]{:S(2)}) collective-permute-start(f32[6,2,16,8]{3,2,1,0:T(8,128)S(1)} %get-tuple-element.9), channel_id=1, source_target_pairs={{1,0},{2,1},{3,2},{4,3},{5,4},{6,5},{7,6},{9,8},{10,9},{11,10},{12... | collective-permute-start | bytes 18440 | tf_op jit(solution)/shard_map/ppermute | solution.py:235
  43.0 8.9 %collective-permute-start.1 = (f32[6,2,16,8]{3,2,1,0:T(8,128)S(1)}, f32[6,2,16,8]{3,2,1,0:T(8,128)S(1)}, u32[]{:S(2)}, u32[]{:S(2)}) collective-permute-start(f32[6,2,16,8]{3,2,1,0:T(8,128)S(1)} %get-tuple-element.10), channel_id=1, source_target_pairs={{0,1},{1,2},{2,3},{3,4},{4,5},{5,6},{6,7},{8,9},{9,10},{10,11},{11... | collective-permute-start | bytes 18440 | tf_op jit(solution)/shard_map/ppermute | solution.py:234

commit v3 on v2

--- a/solution.py
+++ b/solution.py
@@ -9,6 +9,7 @@
 HALO = 8
 RING = 256
 CHUNK = 8
+GROUPS = 2
 
 
 coriolis_step = 1.2
@@ -211,35 +212,43 @@
     half_count = wave_count // 2
     waves = grid.shape[1]
     comps = grid.shape[0]
-    onehot = (wave_table[:, None] == jnp.arange(waves, dtype=jnp.int32)[None, :]).astype(jnp.float32)
-    columns = jnp.einsum("sm,cml->scl", onehot, grid, precision=lax.Precision.HIGHEST)
-    columns = columns.reshape(waves, comps * lat_rows)
-    regrouped = lax.all_to_all(columns, "wave", split_axis=0, concat_axis=0, tiled=True)
-    regrouped = regrouped.reshape(wave_count, slots, comps, lat_rows)
-    north = regrouped[:half_count]
-    south = regrouped[half_count:]
-    parts = jnp.stack([north + south, north - south], axis=0)
-    high, low = split_high(parts)
-    leg_blocks = legendre.reshape(slots, 2, half_count, lat_rows, local_k)
-    both = jnp.concatenate([high, low], axis=3)
-    products = jnp.einsum("mpwlk,pwmcl->cpmk", leg_blocks, both, preferred_element_type=jnp.float32)
-    spectra = products[:comps] + products[comps:]
-    own_waves = lax.dynamic_slice_in_dim(wave_table, lax.axis_index("wave") * slots, slots).astype(
-        jnp.float32
-    )
+    group = slots // GROUPS
     pole_count = lax.axis_size("pole")
     pole_pos = lax.axis_index("pole")
     rightward = [(i, i + 1) for i in range(pole_count - 1)]
     leftward = [(i + 1, i) for i in range(pole_count - 1)]
-    left_halo = lax.ppermute(spectra[..., local_k - HALO :], "pole", rightward)
-    right_halo = lax.ppermute(spectra[..., :HALO], "pole", leftward)
-    gap = jnp.zeros(spectra.shape[:3] + (RING - local_k - 2 * HALO,), jnp.float32)
-    wide = jnp.concatenate([spectra, right_halo, gap, left_halo], axis=3)
-    coef = coefficients(own_waves, pole_pos * local_k, local_k, local_k * pole_count)
-    wide = jnp.concatenate([wide, coef[3][None] * wide[4:6]], axis=0)
-    coef = jnp.concatenate([coriolis_step * coef[:2], coef[2:]], axis=0)
+    own_waves = lax.dynamic_slice_in_dim(wave_table, lax.axis_index("wave") * slots, slots).astype(
+        jnp.float32
+    )
+    coef_all = coefficients(own_waves, pole_pos * local_k, local_k, local_k * pole_count)
+    coef_all = jnp.concatenate([coriolis_step * coef_all[:2], coef_all[2:]], axis=0)
     poles = jnp.take(pole_table, pole_index, axis=1)
-    return solve_poles(poles, wide, coef, local_k)
+    onehot = (wave_table[:, None] == jnp.arange(waves, dtype=jnp.int32)[None, :]).astype(jnp.float32)
+    onehot = onehot.reshape(wave_count, GROUPS, group, waves)
+    leg_blocks = legendre.reshape(slots, 2, half_count, lat_rows, local_k)
+    outs = []
+    for g in range(GROUPS):
+        pick = onehot[:, g].reshape(wave_count * group, waves)
+        columns = jnp.einsum("sm,cml->scl", pick, grid, precision=lax.Precision.HIGHEST)
+        columns = columns.reshape(wave_count * group, comps * lat_rows)
+        regrouped = lax.all_to_all(columns, "wave", split_axis=0, concat_axis=0, tiled=True)
+        regrouped = regrouped.reshape(wave_count, group, comps, lat_rows)
+        north = regrouped[:half_count]
+        south = regrouped[half_count:]
+        parts = jnp.stack([north + south, north - south], axis=0)
+        high, low = split_high(parts)
+        both = jnp.concatenate([high, low], axis=3)
+        leg = leg_blocks[g * group : (g + 1) * group]
+        products = jnp.einsum("mpwlk,pwmcl->cpmk", leg, both, preferred_element_type=jnp.float32)
+        spectra = products[:comps] + products[comps:]
+        left_halo = lax.ppermute(spectra[..., local_k - HALO :], "pole", rightward)
+        right_halo = lax.ppermute(spectra[..., :HALO], "pole", leftward)
+        gap = jnp.zeros(spectra.shape[:3] + (RING - local_k - 2 * HALO,), jnp.float32)
+        wide = jnp.concatenate([spectra, right_halo, gap, left_halo], axis=3)
+        coef = coef_all[:, :, g * group : (g + 1) * group]
+        wide = jnp.concatenate([wide, coef[3][None] * wide[4:6]], axis=0)
+        outs.append(solve_poles(poles, wide, coef, local_k))
+    return jnp.concatenate(outs, axis=2)
 
 
 def solution(mesh):

time: 74.8 us -> 117 us (1.56)
  local copies, waits for them, and re-layouts: 4.18 us -> 24.7 us
  Pallas kernels: 21.6 us -> 41.4 us
  waiting for transfers between devices: 22.3 us -> 3.22 us
  starting transfers between devices: 13.6 us -> 28.1 us
  other arithmetic: 4.28 us -> 7.81 us
  matrix products: 8.31 us -> 10.9 us
    slice x0 -> x4, local copies, waits for them, and re-layouts: none -> 21.5 us  [the longest x3 20.9 us: shards(): leg = leg_blocks[g * group:(g + 1) * group]]
    pallas_call x1 -> x2, Pallas kernels: 21.6 us -> 41.4 us  [solve_poles(): pl.pallas_call(pole_kernel, out_shape=jax.ShapeDtypeStruct((6, parities,...]
    all_to_all x1 -> x2, waiting for transfers between devices: 16 us -> 0.01 us  [shards(): lax.all_to_all(columns, 'wave', split_axis=0, concat_axis=0, tiled=True)]
    ppermute x1 -> x2, starting transfers between devices: 1.92 us -> 10.1 us  [shards(): left_halo = lax.ppermute(spectra[..., local_k - HALO:], 'pole', rightward)]
    ppermute x1 -> x2, waiting for transfers between devices: 6.31 us -> 0.01 us  [shards(): left_halo = lax.ppermute(spectra[..., local_k - HALO:], 'pole', rightward)]
    all_to_all x1 -> x2, starting transfers between devices: 5.93 us -> 11.6 us  [shards(): lax.all_to_all(columns, 'wave', split_axis=0, concat_axis=0, tiled=True)]
    dot_general x1 -> x4, matrix products: 5.71 us -> 10.9 us  [the longest x2 7.72 us: shards(): jnp.einsum('mpwlk,pwmcl->cpmk', leg, both, preferred_element_type=jnp.flo...]
    ppermute x1 -> x2, waiting for transfers between devices: 0.01 us -> 3.21 us  [shards(): right_halo = lax.ppermute(spectra[..., :HALO], 'pole', leftward)]
  transfers between devices with their start and end apart: 3 -> 6, of which waited for: 2 -> 1; matrix products, arithmetic and copies ran while one was open for 3% -> 33% of each run, Pallas kernels for 0% -> 0%
where the time goes in v3:
time: 117 us; the launch traced here: 116 us
  Pallas kernels  41.4 us (35%)
  starting transfers between devices  28.1 us (24%)
  local copies, waits for them, and re-layouts  24.7 us (21%)
  matrix products  10.9 us (9%)
  other arithmetic  7.81 us (7%)
  waiting for transfers between devices  3.22 us (3%)
    pallas_call x2, Pallas kernels, solve_poles(): pl.pallas_call(pole_kernel, out_shape=jax.ShapeDtypeStruct((6, parities,...  41.4 us
    slice x3, local copies, waits for them, and re-layouts, shards(): leg = leg_blocks[g * group:(g + 1) * group]  20.9 us
    all_to_all x2, starting transfers between devices, shards(): lax.all_to_all(columns, 'wave', split_axis=0, concat_axis=0, tiled=True)  11.6 us
    ppermute x2, starting transfers between devices, shards(): left_halo = lax.ppermute(spectra[..., local_k - HALO:], 'pole', rightward)  10.1 us
    dot_general x2, matrix products, shards(): jnp.einsum('mpwlk,pwmcl->cpmk', leg, both, preferred_element_type=jnp.flo...  7.72 us
    ppermute x2, starting transfers between devices, shards(): right_halo = lax.ppermute(spectra[..., :HALO], 'pole', leftward)  6.41 us
    ppermute x2, waiting for transfers between devices, shards(): right_halo = lax.ppermute(spectra[..., :HALO], 'pole', leftward)  3.21 us
    dot_general x2, matrix products, shards(): jnp.einsum('sm,cml->scl', pick, grid, precision=lax.Precision.HIGHEST)  3.14 us
  transfers between devices with their start and end apart: 6, of which 1 were waited for; matrix products, arithmetic and copies ran while one was open for 33% of the time, Pallas kernels for 0%

profile of v3, /device:TPU:6, one launch (start us, length us, event | category | flops | bytes accessed | tf_op | source)
XLA Modules:
  0.0 116.5 jit_solution(201078301054149588)
XLA Ops:
  0.0 0.9 eq.16
  1.3 1.5 %fusion.11 = f32[16,8,1152]{2,1,0:T(8,128)} fusion(f32[1152,256,1]{1,0,2:T(8,128)S(1)} %bitcast.35, pred[16,2,8,256]{3,2,0,1:T(8,128)(4,1)S(1)} %iota_compare_fusion), kind=kOutput, calls=%fused_computation.30 | convolution fusion | flops 452984832 | bytes 1802240 | tf_op jit(solution)/shard_map/sm,cml->scl/dot_general | solution.py:232
  2.8 6.0 %all-to-all-start = ((f32[16,8,1152]{2,1,0:T(8,128)}), f32[16,8,1152]{2,1,0:T(8,128)}, u32[]{:S(2)}, u32[]{:S(2)}) async-start(f32[16,8,1152]{2,1,0:T(8,128)} %fusion.11), calls=%async_computation | async-start | bytes 1179648 | tf_op jit(solution)/shard_map/all_to_all | solution.py:234
  8.8 0.7 compare_select_fusion
  9.5 1.3 %compare_and_fusion.2 = pred[32]{0:T(512)(128)(4,1)} fusion(s32[32]{0:T(128)} %param.9), kind=kLoop, calls=%fused_computation.72 | loop fusion | flops 192 | bytes 160 | tf_op jit(solution)/shard_map/jit(_take)/and | solution.py:225
  10.8 11.7 %fusion.34 = (bf16[8,2,1536,128]{3,2,1,0:T(8,128)(2,1)}, bf16[8,2,1536,128]{3,2,1,0:T(8,128)(2,1)}) fusion(bf16[16,2,1536,128]{3,2,1,0:T(8,128)(2,1)} %param.6), kind=kLoop, calls=%fused_computation.84 | loop fusion | bytes 25165824 | tf_op jit(solution)/shard_map/slice | solution.py:241
  23.6 0.7 gather_fusion
  24.3 6.2 %copy.21 = bf16[8,2,1536,128]{3,2,0,1:T(8,128)(2,1)} copy(bf16[8,2,1536,128]{3,2,1,0:T(8,128)(2,1)} %get-tuple-element.7) | data formatting | bytes 12582912 | tf_op jit(solution)/shard_map/slice | solution.py:241
  30.5 3.0 %copy.25 = bf16[8,2,1536,128]{3,2,0,1:T(8,128)(2,1)} copy(bf16[8,2,1536,128]{3,2,1,0:T(8,128)(2,1)S(1)} %bitcast.40) | data formatting | bytes 12582912 | tf_op jit(solution)/shard_map/slice | solution.py:241
  33.6 0.6 fusion.35
  34.2 1.6 %fusion.10 = f32[16,8,1152]{2,1,0:T(8,128)} fusion(f32[1152,256,1]{1,0,2:T(8,128)S(1)} %bitcast.36, pred[16,2,8,256]{3,2,0,1:T(8,128)(4,1)S(1)} %iota_compare_fusion), kind=kOutput, calls=%fused_computation.28 | convolution fusion | flops 452984832 | bytes 1802240 | tf_op jit(solution)/shard_map/sm,cml->scl/dot_general | solution.py:232
  35.8 5.7 %all-to-all-start.1 = ((f32[16,8,1152]{2,1,0:T(8,128)}), f32[16,8,1152]{2,1,0:T(8,128)S(1)}, u32[]{:S(2)}, u32[]{:S(2)}) async-start(f32[16,8,1152]{2,1,0:T(8,128)} %fusion.10), calls=%async_computation.1 | async-start | bytes 1179648 | tf_op jit(solution)/shard_map/all_to_all | solution.py:234
  41.5 1.1 slice_add_fusion.1
  43.4 3.9 %convolution_bitcast_fusion.1 = f32[2,8,12,128]{3,2,1,0:T(8,128)S(1)} fusion(bf16[8,2,8,192,128]{4,3,2,0,1:T(8,128)(2,1)} %bitcast.38, bf16[2,8,8,6,192]{4,3,1,2,0:T(8,128)(2,1)S(1)} %subtract_convert_fusion.1, bf16[2,8,8,6,192]{4,3,1,2,0:T(8,128)(2,1)S(1)} %copy.38), kind=kOutput, calls=%fused_computation.2 | convolution fusion | flops 76677120 | bytes 6979584 | tf_op jit(solution)/shard_map/mpwlk,pwmcl->cpmk/dot_general | solution.py:242
  47.4 5.5 %collective-permute-start.1 = (f32[6,2,8,8]{3,2,1,0:T(8,128)S(1)}, f32[6,2,8,8]{3,2,1,0:T(8,128)S(1)}, u32[]{:S(2)}, u32[]{:S(2)}) collective-permute-start(f32[6,2,8,8]{3,2,1,0:T(8,128)S(1)} %get-tuple-element.20), channel_id=1, source_target_pairs={{0,1},{1,2},{2,3},{3,4},{4,5},{5,6},{6,7},{8,9},{9,10},{10,11},{11... | collective-permute-start | bytes 9224 | tf_op jit(solution)/shard_map/ppermute | solution.py:244
  52.9 2.8 %collective-permute-start = (f32[6,2,8,8]{3,2,1,0:T(8,128)S(1)}, f32[6,2,8,8]{3,2,1,0:T(8,128)S(1)}, u32[]{:S(2)}, u32[]{:S(2)}) collective-permute-start(f32[6,2,8,8]{3,2,1,0:T(8,128)S(1)} %get-tuple-element.19), channel_id=1, source_target_pairs={{1,0},{2,1},{3,2},{4,3},{5,4},{6,5},{7,6},{9,8},{10,9},{11,10},{12... | collective-permute-start | bytes 9224 | tf_op jit(solution)/shard_map/ppermute | solution.py:245
  56.6 3.9 %convolution_bitcast_fusion = f32[2,8,12,128]{3,2,1,0:T(8,128)S(1)} fusion(bf16[8,2,8,192,128]{4,3,2,0,1:T(8,128)(2,1)} %bitcast.37, bf16[2,8,8,6,192]{4,3,1,2,0:T(8,128)(2,1)S(1)} %subtract_convert_fusion, bf16[2,8,8,6,192]{4,3,1,2,0:T(8,128)(2,1)S(1)} %copy.37), kind=kOutput, calls=%fused_computation.1 | convolution fusion | flops 76677120 | bytes 6979584 | tf_op jit(solution)/shard_map/mpwlk,pwmcl->cpmk/dot_general | solution.py:242
  60.6 4.6 %collective-permute-start.3 = (f32[6,2,8,8]{3,2,1,0:T(8,128)S(1)}, f32[6,2,8,8]{3,2,1,0:T(8,128)S(1)}, u32[]{:S(2)}, u32[]{:S(2)}) collective-permute-start(f32[6,2,8,8]{3,2,1,0:T(8,128)S(1)} %get-tuple-element.22), channel_id=1, source_target_pairs={{0,1},{1,2},{2,3},{3,4},{4,5},{5,6},{6,7},{8,9},{9,10},{10,11},{11... | collective-permute-start | bytes 9224 | tf_op jit(solution)/shard_map/ppermute | solution.py:244
  65.2 3.7 %collective-permute-start.2 = (f32[6,2,8,8]{3,2,1,0:T(8,128)S(1)}, f32[6,2,8,8]{3,2,1,0:T(8,128)S(1)}, u32[]{:S(2)}, u32[]{:S(2)}) collective-permute-start(f32[6,2,8,8]{3,2,1,0:T(8,128)S(1)} %get-tuple-element.21), channel_id=1, source_target_pairs={{1,0},{2,1},{3,2},{4,3},{5,4},{6,5},{7,6},{9,8},{10,9},{11,10},{12... | collective-permute-start | bytes 9224 | tf_op jit(solution)/shard_map/ppermute | solution.py:245
  69.5 3.2 %collective-permute-done.2 = f32[6,2,8,8]{3,2,1,0:T(8,128)S(1)} collective-permute-done((f32[6,2,8,8]{3,2,1,0:T(8,128)S(1)}, f32[6,2,8,8]{3,2,1,0:T(8,128)S(1)}, u32[]{:S(2)}, u32[]{:S(2)}) %collective-permute-start.2) | collective-permute-done | bytes 3104 | tf_op jit(solution)/shard_map/ppermute | solution.py:245
  72.8 0.8 fusion.7
  73.6 20.7 %shard_map.56 = f32[6,2,8,128]{3,2,1,0:T(8,128)} custom-call(f32[4,32]{1,0:T(4,128)} %select_bitcast_fusion.poles_ref, f32[8,2,8,256]{3,2,1,0:T(8,128)} %get-tuple-element.16.spec_ref, f32[4,2,8,256]{3,2,1,0:T(8,128)} %get-tuple-element.14.coef_ref), custom_call_target="tpu_custom_call" | custom-call | tf_op jit(solution)/shard_map/pallas_call | solution.py:129
  94.3 20.7 %shard_map.55 = f32[6,2,8,128]{3,2,1,0:T(8,128)} custom-call(f32[4,32]{1,0:T(4,128)} %select_bitcast_fusion.poles_ref, f32[8,2,8,256]{3,2,1,0:T(8,128)} %get-tuple-element.15.spec_ref, f32[4,2,8,256]{3,2,1,0:T(8,128)} %get-tuple-element.13.coef_ref), custom_call_target="tpu_custom_call" | custom-call | tf_op jit(solution)/shard_map/pallas_call | solution.py:129
  115.0 1.5 %pad_maximum_fusion.5 = f32[6,2,16,128]{3,2,1,0:T(8,128)} fusion(f32[6,2,8,128]{3,2,1,0:T(8,128)} %shard_map.56, f32[6,2,8,128]{3,2,1,0:T(8,128)} %shard_map.55), kind=kLoop, calls=%fused_computation.31 | loop fusion | flops 24576 | bytes 196608 | tf_op jit(solution)/shard_map/concatenate | solution.py:251
  (54 shorter events, 4.2 us)
Async XLA Ops:
  0.0 1.3 %copy-start = (f32[6,256,192]{1,2,0:T(8,128)S(1)}, f32[6,256,192]{1,2,0:T(8,128)}, u32[]{:S(2)}) copy-start(f32[6,256,192]{1,2,0:T(8,128)} %param.5) | copy-start | bytes 3538948
  2.8 33.0 %all-to-all-start = ((f32[16,8,1152]{2,1,0:T(8,128)}), f32[16,8,1152]{2,1,0:T(8,128)}, u32[]{:S(2)}, u32[]{:S(2)}) async-start(f32[16,8,1152]{2,1,0:T(8,128)} %fusion.11), calls=%async_computation | async-start | bytes 1179648 | tf_op jit(solution)/shard_map/all_to_all | solution.py:234
  10.7 11.7 %copy-start.1 = (s32[256]{0:T(256)S(1)}, s32[256]{0:T(256)}, u32[]{:S(2)}) copy-start(s32[256]{0:T(256)} %param.7) | copy-start | bytes 3076
  10.8 12.7 %copy-start.2 = (f32[4,64]{1,0:T(4,128)S(1)}, f32[4,64]{1,0:T(4,128)}, u32[]{:S(2)}) copy-start(f32[4,64]{1,0:T(4,128)} %param.8) | copy-start | bytes 3076
  22.8 7.7 %slice-start = ((s8[6291456]{0:T(1024)(128)(4,1)}), s8[2097152]{0:T(1024)(128)(4,1)S(1)}, s32[]{:S(2)}) async-start(s8[6291456]{0:T(1024)(128)(4,1)} %bitcast.39), calls=%async_computation.2 | async-start | bytes 4194304
  24.3 6.2 %slice-start.1 = ((s8[6291456]{0:T(1024)(128)(4,1)}), s8[4194304]{0:T(1024)(128)(4,1)S(1)}, s32[]{:S(2)}) async-start(s8[6291456]{0:T(1024)(128)(4,1)} %bitcast.39), calls=%async_computation.3 | async-start | bytes 8388608
  35.8 19.9 %all-to-all-start.1 = ((f32[16,8,1152]{2,1,0:T(8,128)}), f32[16,8,1152]{2,1,0:T(8,128)S(1)}, u32[]{:S(2)}, u32[]{:S(2)}) async-start(f32[16,8,1152]{2,1,0:T(8,128)} %fusion.10), calls=%async_computation.1 | async-start | bytes 1179648 | tf_op jit(solution)/shard_map/all_to_all | solution.py:234
  47.4 22.0 %collective-permute-start.1 = (f32[6,2,8,8]{3,2,1,0:T(8,128)S(1)}, f32[6,2,8,8]{3,2,1,0:T(8,128)S(1)}, u32[]{:S(2)}, u32[]{:S(2)}) collective-permute-start(f32[6,2,8,8]{3,2,1,0:T(8,128)S(1)} %get-tuple-element.20), channel_id=1, source_target_pairs={{0,1},{1,2},{2,3},{3,4},{4,5},{5,6},{6,7},{8,9},{9,10},{10,11},{11... | collective-permute-start | bytes 9224 | tf_op jit(solution)/shard_map/ppermute | solution.py:244
  52.9 16.5 %collective-permute-start = (f32[6,2,8,8]{3,2,1,0:T(8,128)S(1)}, f32[6,2,8,8]{3,2,1,0:T(8,128)S(1)}, u32[]{:S(2)}, u32[]{:S(2)}) collective-permute-start(f32[6,2,8,8]{3,2,1,0:T(8,128)S(1)} %get-tuple-element.19), channel_id=1, source_target_pairs={{1,0},{2,1},{3,2},{4,3},{5,4},{6,5},{7,6},{9,8},{10,9},{11,10},{12... | collective-permute-start | bytes 9224 | tf_op jit(solution)/shard_map/ppermute | solution.py:245
  56.6 12.3 %copy-start.3 = (pred[32]{0:T(512)(128)(4,1)S(1)}, pred[32]{0:T(512)(128)(4,1)}, u32[]{:S(2)}) copy-start(pred[32]{0:T(512)(128)(4,1)} %compare_and_fusion.2) | copy-start | bytes 100
  60.6 8.9 %collective-permute-start.3 = (f32[6,2,8,8]{3,2,1,0:T(8,128)S(1)}, f32[6,2,8,8]{3,2,1,0:T(8,128)S(1)}, u32[]{:S(2)}, u32[]{:S(2)}) collective-permute-start(f32[6,2,8,8]{3,2,1,0:T(8,128)S(1)} %get-tuple-element.22), channel_id=1, source_target_pairs={{0,1},{1,2},{2,3},{3,4},{4,5},{5,6},{6,7},{8,9},{9,10},{10,11},{11... | collective-permute-start | bytes 9224 | tf_op jit(solution)/shard_map/ppermute | solution.py:244
  65.2 7.5 %collective-permute-start.2 = (f32[6,2,8,8]{3,2,1,0:T(8,128)S(1)}, f32[6,2,8,8]{3,2,1,0:T(8,128)S(1)}, u32[]{:S(2)}, u32[]{:S(2)}) collective-permute-start(f32[6,2,8,8]{3,2,1,0:T(8,128)S(1)} %get-tuple-element.21), channel_id=1, source_target_pairs={{1,0},{2,1},{3,2},{4,3},{5,4},{6,5},{7,6},{9,8},{10,9},{11,10},{12... | collective-permute-start | bytes 9224 | tf_op jit(solution)/shard_map/ppermute | solution.py:245

commit v4 on v3

--- a/solution.py
+++ b/solution.py
@@ -9,7 +9,8 @@
 HALO = 8
 RING = 256
 CHUNK = 8
-GROUPS = 2
+GROUPS = 1
+INTERLEAVE = 4
 
 
 coriolis_step = 1.2
@@ -54,26 +55,30 @@
     width = out_ref.shape[3]
     out_ref[...] = jnp.zeros(out_ref.shape, jnp.float32)
 
-    def one_pole(q, carry):
-        a_re = poles_ref[0, q]
-        a_im = poles_ref[1, q]
-        w_re = poles_ref[2, q]
-        w_im = poles_ref[3, q]
-        for r0 in range(0, rows, CHUNK):
-            sl = pl.ds(r0, CHUNK)
-
-            def ld(ref, i, p):
-                return ref[i, p, sl, :]
-
-            def near(x):
-                n0 = ld(coef_ref, 0, 0) * pltpu.roll(x[1], 1, 1) + ld(coef_ref, 1, 0) * x[1]
-                n1 = ld(coef_ref, 0, 1) * x[0] + ld(coef_ref, 1, 1) * pltpu.roll(x[0], lanes - 1, 1)
-                return (n0, n1)
-
+    def pole_step(step, carry):
+        lanes_work = []
+        for u in range(INTERLEAVE):
+            q = step * INTERLEAVE + u
+            scal = [poles_ref[i, q] for i in range(4)]
+            for r0 in range(0, rows, CHUNK):
+                lanes_work.append((scal, pl.ds(r0, CHUNK)))
+
+        def ld(ref, i, p, sl):
+            return ref[i, p, sl, :]
+
+        def near(x, sl):
+            n0 = ld(coef_ref, 0, 0, sl) * pltpu.roll(x[1], 1, 1) + ld(coef_ref, 1, 0, sl) * x[1]
+            n1 = ld(coef_ref, 0, 1, sl) * x[0] + ld(coef_ref, 1, 1, sl) * pltpu.roll(
+                x[0], lanes - 1, 1
+            )
+            return (n0, n1)
+
+        prep = []
+        for (a_re, a_im, _, _), sl in lanes_work:
             inv, dinv, lift, base = [], [], [], []
             for p in range(2):
-                grav = ld(coef_ref, 3, p)
-                b_im = a_im + ld(coef_ref, 2, p)
+                grav = ld(coef_ref, 3, p, sl)
+                b_im = a_im + ld(coef_ref, 2, p, sl)
                 b_rec = 1.0 / (a_re * a_re + b_im * b_im)
                 inv.append((a_re * b_rec, -b_im * b_rec))
                 det_re = a_re * a_re - b_im * a_im + grav * grav
@@ -82,22 +87,25 @@
                 dv = (det_re * det_rec, -det_im * det_rec)
                 dinv.append(dv)
                 lift.append(cmul(a_re, a_im, dv[0], dv[1]))
-                base.append(cmul(ld(spec_ref, 6, p), ld(spec_ref, 7, p), dv[0], dv[1]))
-            zr = zi = dr = di = None
-            for sweep in range(SWEEPS):
+                base.append(cmul(ld(spec_ref, 6, p, sl), ld(spec_ref, 7, p, sl), dv[0], dv[1]))
+            prep.append((inv, dinv, lift, base))
+        state = [None] * len(lanes_work)
+        for sweep in range(SWEEPS):
+            for n, ((a_re, a_im, _, _), sl) in enumerate(lanes_work):
+                inv, dinv, lift, base = prep[n]
                 if sweep > 0:
-                    nzr, nzi, ndr, ndi = near(zr), near(zi), near(dr), near(di)
-                zr, zi, dr, di = [], [], [], []
-                hr, hi = [], []
+                    zr, zi, dr, di, _, _ = state[n]
+                    nzr, nzi, ndr, ndi = near(zr, sl), near(zi, sl), near(dr, sl), near(di, sl)
+                zr, zi, dr, di, hr, hi = [], [], [], [], [], []
                 for p in range(2):
                     if sweep == 0:
-                        rzr, rzi = ld(spec_ref, 0, p), ld(spec_ref, 1, p)
-                        rdr, rdi = ld(spec_ref, 2, p), ld(spec_ref, 3, p)
+                        rzr, rzi = ld(spec_ref, 0, p, sl), ld(spec_ref, 1, p, sl)
+                        rdr, rdi = ld(spec_ref, 2, p, sl), ld(spec_ref, 3, p, sl)
                     else:
-                        rzr = ld(spec_ref, 0, p) - ndr[p]
-                        rzi = ld(spec_ref, 1, p) - ndi[p]
-                        rdr = ld(spec_ref, 2, p) + nzr[p]
-                        rdi = ld(spec_ref, 3, p) + nzi[p]
+                        rzr = ld(spec_ref, 0, p, sl) - ndr[p]
+                        rzi = ld(spec_ref, 1, p, sl) - ndi[p]
+                        rdr = ld(spec_ref, 2, p, sl) + nzr[p]
+                        rdi = ld(spec_ref, 3, p, sl) + nzi[p]
                     z_re, z_im = cmul(rzr, rzi, inv[p][0], inv[p][1])
                     zr.append(z_re)
                     zi.append(z_im)
@@ -105,15 +113,18 @@
                     dr.append(d_re + base[p][0])
                     di.append(d_im + base[p][1])
                     if sweep == SWEEPS - 1:
-                        grav = ld(coef_ref, 3, p)
-                        b_im = a_im + ld(coef_ref, 2, p)
-                        h0r = ld(spec_ref, 4, p)
-                        h0i = ld(spec_ref, 5, p)
+                        grav = ld(coef_ref, 3, p, sl)
+                        b_im = a_im + ld(coef_ref, 2, p, sl)
+                        h0r = ld(spec_ref, 4, p, sl)
+                        h0i = ld(spec_ref, 5, p, sl)
                         nh_re = a_re * h0r - b_im * h0i - grav * rdr
                         nh_im = a_re * h0i + b_im * h0r - grav * rdi
                         h_re, h_im = cmul(nh_re, nh_im, dinv[p][0], dinv[p][1])
                         hr.append(h_re)
                         hi.append(h_im)
+                state[n] = (zr, zi, dr, di, hr, hi)
+        for n, ((_, _, w_re, w_im), sl) in enumerate(lanes_work):
+            zr, zi, dr, di, hr, hi = state[n]
             for field, (f_re, f_im) in enumerate(((zr, zi), (dr, di), (hr, hi))):
                 for p in range(2):
                     o_re, o_im = cmul(w_re, w_im, f_re[p], f_im[p])
@@ -121,7 +132,7 @@
                     out_ref[2 * field + 1, p, sl, :] += o_im[:, :width]
         return carry
 
-    lax.fori_loop(0, npoles, one_pole, 0)
+    lax.fori_loop(0, npoles // INTERLEAVE, pole_step, 0)
 
 
 def solve_poles(poles, wide, coef, width):

time: 117 us -> 65.8 us (0.56)
  Pallas kernels: 41.4 us -> 12.6 us
  local copies, waits for them, and re-layouts: 24.7 us -> 4.18 us
  waiting for transfers between devices: 3.22 us -> 22.3 us
  starting transfers between devices: 28.1 us -> 13.6 us
  other arithmetic: 7.81 us -> 4.28 us
  matrix products: 10.9 us -> 8.31 us
    pallas_call x2 -> x1, Pallas kernels: 41.4 us -> 12.6 us  [solve_poles(): pl.pallas_call(pole_kernel, out_shape=jax.ShapeDtypeStruct((6, parities,...]
    slice x4 -> x0, local copies, waits for them, and re-layouts: 21.5 us -> none  [the longest x3 20.9 us: shards(): leg = leg_blocks[g * group:(g + 1) * group]]
    all_to_all x2 -> x1, waiting for transfers between devices: 0.01 us -> 16 us  [shards(): lax.all_to_all(columns, 'wave', split_axis=0, concat_axis=0, tiled=True)]
    ppermute x2 -> x1, starting transfers between devices: 10.1 us -> 1.92 us  [shards(): left_halo = lax.ppermute(spectra[..., local_k - HALO:], 'pole', rightward)]
    ppermute x2 -> x1, waiting for transfers between devices: 0.01 us -> 6.31 us  [shards(): left_halo = lax.ppermute(spectra[..., local_k - HALO:], 'pole', rightward)]
    all_to_all x2 -> x1, starting transfers between devices: 11.6 us -> 5.93 us  [shards(): lax.all_to_all(columns, 'wave', split_axis=0, concat_axis=0, tiled=True)]
    ppermute x2 -> x1, waiting for transfers between devices: 3.21 us -> 0.01 us  [shards(): right_halo = lax.ppermute(spectra[..., :HALO], 'pole', leftward)]
    dot_general x2 -> x0, matrix products: 3.14 us -> none  [shards(): jnp.einsum('sm,cml->scl', pick, grid, precision=lax.Precision.HIGHEST)]
  transfers between devices with their start and end apart: 6 -> 3, of which waited for: 1 -> 2; matrix products, arithmetic and copies ran while one was open for 33% -> 4% of each run, Pallas kernels for 0% -> 0%
where the time goes in v4:
time: 65.8 us; the launch traced here: 65.4 us
  waiting for transfers between devices  22.3 us (34%)
  starting transfers between devices  13.6 us (21%)
  Pallas kernels  12.6 us (19%)
  matrix products  8.31 us (13%)
  other arithmetic  4.28 us (7%)
  local copies, waits for them, and re-layouts  4.18 us (6%)
    all_to_all x1, waiting for transfers between devices, shards(): lax.all_to_all(columns, 'wave', split_axis=0, concat_axis=0, tiled=True)  16 us
    pallas_call x1, Pallas kernels, solve_poles(): pl.pallas_call(pole_kernel, out_shape=jax.ShapeDtypeStruct((6, parities,...  12.6 us
    ppermute x1, waiting for transfers between devices, shards(): left_halo = lax.ppermute(spectra[..., local_k - HALO:], 'pole', rightward)  6.31 us
    all_to_all x1, starting transfers between devices, shards(): lax.all_to_all(columns, 'wave', split_axis=0, concat_axis=0, tiled=True)  5.93 us
    ppermute x1, starting transfers between devices, shards(): right_halo = lax.ppermute(spectra[..., :HALO], 'pole', leftward)  5.76 us
    dot_general x1, matrix products, shards(): jnp.einsum('mpwlk,pwmcl->cpmk', leg, both, preferred_element_type=jnp.flo...  5.71 us
    unnamed x1, matrix products  2.59 us
    ppermute x1, starting transfers between devices, shards(): left_halo = lax.ppermute(spectra[..., local_k - HALO:], 'pole', rightward)  1.92 us
  transfers between devices with their start and end apart: 3, of which 2 were waited for; matrix products, arithmetic and copies ran while one was open for 4% of the time, Pallas kernels for 0%

profile of v4, /device:TPU:6, one launch (start us, length us, event | category | flops | bytes accessed | tf_op | source)
XLA Modules:
  0.0 65.4 jit_solution(6040582135364712756)
XLA Ops:
  0.0 1.3 %copy-done = f32[6,256,192]{1,2,0:T(8,128)S(1)} copy-done((f32[6,256,192]{1,2,0:T(8,128)S(1)}, f32[6,256,192]{1,2,0:T(8,128)}, u32[]{:S(2)}) %copy-start) | copy-done | bytes 1179672
  1.3 2.6 %fusion.10 = f32[256,1152]{1,0:T(8,128)} fusion(f32[256,1152]{0,1:T(8,128)S(1)} %bitcast.15, s32[256]{0:T(256)} %param.7), kind=kOutput, calls=%fused_computation.14 | convolution fusion | flops 906035200 | bytes 2360320
  3.9 5.9 %all-to-all-start = ((f32[16,16,1152]{2,1,0:T(8,128)}), f32[16,16,1152]{2,1,0:T(8,128)S(1)}, u32[]{:S(2)}, u32[]{:S(2)}) async-start(f32[16,16,1152]{2,1,0:T(8,128)} %bitcast.9), calls=%async_computation | async-start | bytes 2359296 | tf_op jit(solution)/shard_map/all_to_all | solution.py:245
  10.1 0.1 copy.12
  10.2 0.6 gather_fusion
  10.9 0.1 fusion.30
  11.0 0.6 select_bitcast_fusion.poles_ref
  11.6 0.1 fusion.20
  11.7 16.0 %all-to-all-done = f32[16,16,1152]{2,1,0:T(8,128)S(1)} async-done(((f32[16,16,1152]{2,1,0:T(8,128)}), f32[16,16,1152]{2,1,0:T(8,128)S(1)}, u32[]{:S(2)}, u32[]{:S(2)}) %all-to-all-start) | async-done | bytes 1179680 | tf_op jit(solution)/shard_map/all_to_all | solution.py:245
  27.7 0.9 %slice_add_fusion = (f32[8,16,1152]{2,1,0:T(8,128)S(1)}, f32[8,16,1152]{2,1,0:T(8,128)}) fusion(f32[16,16,1152]{2,1,0:T(8,128)S(1)} %all-to-all-done), kind=kLoop, calls=%fused_computation.11 | loop fusion | flops 294912 | bytes 2359296 | tf_op jit(solution)/shard_map/add | solution.py:249
  28.6 0.4 add.193
  29.0 1.5 %sub.27 = f32[1,8,16,6,192]{4,3,2,1,0:T(8,128)S(1)} reshape(f32[8,16,1152]{2,1,0:T(8,128)} %get-tuple-element.8) | data formatting | bytes 1179648 | tf_op jit(solution)/shard_map/sub | solution.py:249
  30.5 0.3 pad_maximum_fusion
  30.7 0.1 copy.28
  30.9 0.4 subtract_convert_fusion
  31.3 5.7 %fusion.5 = f32[2,16,12,128]{3,2,1,0:T(8,128)S(1)} fusion(bf16[16,2,8,192,128]{4,3,2,1,0:T(8,128)(2,1)} %bitcast.17, bf16[2,8,16,6,192]{4,3,1,2,0:T(8,128)(2,1)S(1)} %subtract_convert_fusion, bf16[2,8,16,6,192]{4,3,1,2,0:T(8,128)(2,1)S(1)} %copy.28), kind=kOutput, calls=%fused_computation.9 | convolution fusion | flops 153354240 | bytes 13959168 | tf_op jit(solution)/shard_map/mpwlk,pwmcl->cpmk/dot_general | solution.py:253
  37.1 0.1 fusion.32
  37.2 5.8 %collective-permute-start = (f32[6,2,16,8]{3,2,1,0:T(8,128)S(1)}, f32[6,2,16,8]{3,2,1,0:T(8,128)S(1)}, u32[]{:S(2)}, u32[]{:S(2)}) collective-permute-start(f32[6,2,16,8]{3,2,1,0:T(8,128)S(1)} %get-tuple-element.9), channel_id=1, source_target_pairs={{1,0},{2,1},{3,2},{4,3},{5,4},{6,5},{7,6},{9,8},{10,9},{11,10},{12... | collective-permute-start | bytes 18440 | tf_op jit(solution)/shard_map/ppermute | solution.py:256
  43.0 1.9 %collective-permute-start.1 = (f32[6,2,16,8]{3,2,1,0:T(8,128)S(1)}, f32[6,2,16,8]{3,2,1,0:T(8,128)S(1)}, u32[]{:S(2)}, u32[]{:S(2)}) collective-permute-start(f32[6,2,16,8]{3,2,1,0:T(8,128)S(1)} %get-tuple-element.10), channel_id=1, source_target_pairs={{0,1},{1,2},{2,3},{3,4},{4,5},{5,6},{6,7},{8,9},{9,10},{10,11},{11... | collective-permute-start | bytes 18440 | tf_op jit(solution)/shard_map/ppermute | solution.py:255
  44.9 0.7 %pad_maximum_fusion.2.coef_ref = f32[4,2,16,256]{3,2,1,0:T(8,128)} fusion(f32[1,2,16,256]{3,2,1,0:T(8,128)S(1)} %get-tuple-element.13, f32[1,2,16,256]{3,2,1,0:T(8,128)S(1)} %get-tuple-element.14, f32[2,2,16,256]{3,2,1,0:T(8,128)S(1)} %maximum_multiply_fusion), kind=kLoop, calls=%fused_computation.16 | loop fusion | flops 65536 | bytes 262144 | tf_op jit(solution)/shard_map/concatenate | solution.py:235
  45.6 6.3 %collective-permute-done.1 = f32[6,2,16,8]{3,2,1,0:T(8,128)S(1)} collective-permute-done((f32[6,2,16,8]{3,2,1,0:T(8,128)S(1)}, f32[6,2,16,8]{3,2,1,0:T(8,128)S(1)}, u32[]{:S(2)}, u32[]{:S(2)}) %collective-permute-start.1) | collective-permute-done | bytes 6176 | tf_op jit(solution)/shard_map/ppermute | solution.py:255
  51.9 0.1 fusion.12
  52.0 0.8 %pad_maximum_fusion.1.spec_ref = f32[8,2,16,256]{3,2,1,0:T(8,128)} fusion(f32[2,2,16,256]{3,2,1,0:T(8,128)S(1)} %fusion.12, f32[6,2,16,8]{3,2,1,0:T(8,128)S(1)} %collective-permute-done.1, f32[6,2,16,112]{3,2,1,0:T(8,128)S(1)} %broadcast_in_dim.48, f32[6,2,16,8]{3,2,1,0:T(8,128)S(1)} %collective-permute-done, f32[6,2,16,128]{3,2,1,0:T(8,128)S(1)} %slice_add_fusion.1), kind=kLoop, calls=%fused_computation.12 | loop fusion | flops 262144 | bytes 524288 | tf_op jit(solution)/shard_map/concatenate | solution.py:260
  52.8 12.6 %shard_map.55 = f32[6,2,16,128]{3,2,1,0:T(8,128)} custom-call(f32[4,32]{1,0:T(4,128)} %select_bitcast_fusion.poles_ref, f32[8,2,16,256]{3,2,1,0:T(8,128)} %pad_maximum_fusion.1.spec_ref, f32[4,2,16,256]{3,2,1,0:T(8,128)} %pad_maximum_fusion.2.coef_ref), custom_call_target="tpu_custom_call" | custom-call | tf_op jit(solution)/shard_map/pallas_call | solution.py:140
  (23 shorter events, 0.5 us)
Async XLA Ops:
  0.0 1.3 %copy-start = (f32[6,256,192]{1,2,0:T(8,128)S(1)}, f32[6,256,192]{1,2,0:T(8,128)}, u32[]{:S(2)}) copy-start(f32[6,256,192]{1,2,0:T(8,128)} %param.5) | copy-start | bytes 3538948
  1.3 8.6 %copy-start.1 = (s32[256]{0:T(256)S(1)}, s32[256]{0:T(256)}, u32[]{:S(2)}) copy-start(s32[256]{0:T(256)} %param.7) | copy-start | bytes 3076
  1.3 8.8 %copy-start.2 = (f32[4,64]{1,0:T(4,128)S(1)}, f32[4,64]{1,0:T(4,128)}, u32[]{:S(2)}) copy-start(f32[4,64]{1,0:T(4,128)} %param.8) | copy-start | bytes 3076
  1.3 8.9 %copy-start.3 = (s32[32]{0:T(128)S(1)}, s32[32]{0:T(128)}, u32[]{:S(2)}) copy-start(s32[32]{0:T(128)} %param.9) | copy-start | bytes 388
  3.9 23.8 %all-to-all-start = ((f32[16,16,1152]{2,1,0:T(8,128)}), f32[16,16,1152]{2,1,0:T(8,128)S(1)}, u32[]{:S(2)}, u32[]{:S(2)}) async-start(f32[16,16,1152]{2,1,0:T(8,128)} %bitcast.9), calls=%async_computation | async-start | bytes 2359296 | tf_op jit(solution)/shard_map/all_to_all | solution.py:245
  37.2 8.4 %collective-permute-start = (f32[6,2,16,8]{3,2,1,0:T(8,128)S(1)}, f32[6,2,16,8]{3,2,1,0:T(8,128)S(1)}, u32[]{:S(2)}, u32[]{:S(2)}) collective-permute-start(f32[6,2,16,8]{3,2,1,0:T(8,128)S(1)} %get-tuple-element.9), channel_id=1, source_target_pairs={{1,0},{2,1},{3,2},{4,3},{5,4},{6,5},{7,6},{9,8},{10,9},{11,10},{12... | collective-permute-start | bytes 18440 | tf_op jit(solution)/shard_map/ppermute | solution.py:256
  43.0 8.9 %collective-permute-start.1 = (f32[6,2,16,8]{3,2,1,0:T(8,128)S(1)}, f32[6,2,16,8]{3,2,1,0:T(8,128)S(1)}, u32[]{:S(2)}, u32[]{:S(2)}) collective-permute-start(f32[6,2,16,8]{3,2,1,0:T(8,128)S(1)} %get-tuple-element.10), channel_id=1, source_target_pairs={{0,1},{1,2},{2,3},{3,4},{4,5},{5,6},{6,7},{8,9},{9,10},{10,11},{11... | collective-permute-start | bytes 18440 | tf_op jit(solution)/shard_map/ppermute | solution.py:255

commit v5 on v4

--- a/solution.py
+++ b/solution.py
@@ -1,3 +1,5 @@
+import functools
+
 import jax
 import jax.numpy as jnp
 from jax import lax
@@ -11,6 +13,8 @@
 CHUNK = 8
 GROUPS = 1
 INTERLEAVE = 4
+EDGE_INTERLEAVE = 16
+WINDOW = 32
 
 
 coriolis_step = 1.2
@@ -48,20 +52,21 @@
     return jnp.stack([e_lo, e_hi, rossby, gravity], axis=0)
 
 
-def pole_kernel(poles_ref, spec_ref, coef_ref, out_ref):
+def pole_kernel(poles_ref, spec_ref, coef_ref, out_ref, *, interleave):
     npoles = poles_ref.shape[1]
     rows = spec_ref.shape[2]
+    chunk = min(CHUNK, rows)
     lanes = spec_ref.shape[3]
     width = out_ref.shape[3]
     out_ref[...] = jnp.zeros(out_ref.shape, jnp.float32)
 
     def pole_step(step, carry):
         lanes_work = []
-        for u in range(INTERLEAVE):
-            q = step * INTERLEAVE + u
+        for u in range(interleave):
+            q = step * interleave + u
             scal = [poles_ref[i, q] for i in range(4)]
-            for r0 in range(0, rows, CHUNK):
-                lanes_work.append((scal, pl.ds(r0, CHUNK)))
+            for r0 in range(0, rows, chunk):
+                lanes_work.append((scal, pl.ds(r0, chunk)))
 
         def ld(ref, i, p, sl):
             return ref[i, p, sl, :]
@@ -132,13 +137,13 @@
                     out_ref[2 * field + 1, p, sl, :] += o_im[:, :width]
         return carry
 
-    lax.fori_loop(0, npoles // INTERLEAVE, pole_step, 0)
-
-
-def solve_poles(poles, wide, coef, width):
+    lax.fori_loop(0, npoles // interleave, pole_step, 0)
+
+
+def solve_poles(poles, wide, coef, width, interleave):
     _, parities, rows, _ = wide.shape
     return pl.pallas_call(
-        pole_kernel,
+        functools.partial(pole_kernel, interleave=interleave),
         out_shape=jax.ShapeDtypeStruct((6, parities, rows, width), jnp.float32),
         in_specs=[
             pl.BlockSpec(memory_space=pltpu.SMEM),
@@ -252,13 +257,35 @@
         leg = leg_blocks[g * group : (g + 1) * group]
         products = jnp.einsum("mpwlk,pwmcl->cpmk", leg, both, preferred_element_type=jnp.float32)
         spectra = products[:comps] + products[comps:]
+        coef = coef_all[:, :, g * group : (g + 1) * group]
+        gap = jnp.zeros(spectra.shape[:3] + (RING - local_k,), jnp.float32)
+        wide = jnp.concatenate([spectra, gap], axis=3)
+        wide = jnp.concatenate([wide, coef[3][None] * wide[4:6]], axis=0)
+        main = solve_poles(poles, wide, coef, local_k, INTERLEAVE)
         left_halo = lax.ppermute(spectra[..., local_k - HALO :], "pole", rightward)
         right_halo = lax.ppermute(spectra[..., :HALO], "pole", leftward)
-        gap = jnp.zeros(spectra.shape[:3] + (RING - local_k - 2 * HALO,), jnp.float32)
-        wide = jnp.concatenate([spectra, right_halo, gap, left_halo], axis=3)
-        coef = coef_all[:, :, g * group : (g + 1) * group]
-        wide = jnp.concatenate([wide, coef[3][None] * wide[4:6]], axis=0)
-        outs.append(solve_poles(poles, wide, coef, local_k))
+        edge = HALO // 2
+        pad = jnp.zeros(spectra.shape[:3] + (edge,), jnp.float32)
+        tail = jnp.zeros(spectra.shape[:3] + (WINDOW - 2 * HALO - 2 * edge,), jnp.float32)
+        win = jnp.concatenate([pad, right_halo, left_halo, pad, tail], axis=3)
+        win_coef = jnp.concatenate(
+            [
+                coef[..., local_k - edge : local_k + HALO],
+                coef[..., RING - HALO :],
+                coef[..., :edge],
+                jnp.zeros(coef.shape[:3] + (WINDOW - 2 * HALO - 2 * edge,), jnp.float32),
+            ],
+            axis=3,
+        )
+        win = jnp.concatenate([win, win_coef[3][None] * win[4:6]], axis=0)
+        packed = 128 // WINDOW
+        win = win.reshape(win.shape[0], 2, group // packed, 128)
+        win_coef = win_coef.reshape(win_coef.shape[0], 2, group // packed, 128)
+        fix = solve_poles(poles, win, win_coef, 128, EDGE_INTERLEAVE)
+        fix = fix.reshape(fix.shape[0], 2, group, WINDOW)
+        main = main.at[..., local_k - edge :].add(fix[..., :edge])
+        main = main.at[..., :edge].add(fix[..., 2 * HALO + edge : 2 * HALO + 2 * edge])
+        outs.append(main)
     return jnp.concatenate(outs, axis=2)
 
 

time: 65.8 us -> 71.5 us (1.087)
  waiting for transfers between devices: 22.3 us -> 14.9 us
  local copies, waits for them, and re-layouts: 4.18 us -> 11.1 us
  Pallas kernels: 12.6 us -> 16.8 us
  other arithmetic: 4.28 us -> 5.52 us
    ppermute x1, waiting for transfers between devices: 6.31 us -> 0.01 us  [shards(): left_halo = lax.ppermute(spectra[..., local_k - HALO:], 'pole', rightward)]
    scatter-add x0 -> x2, local copies, waits for them, and re-layouts: none -> 4.26 us  [the longest x1 2.69 us: shards(): main = main.at[..., local_k - edge:].add(fix[..., :edge])]
    pallas_call x1 -> x2, Pallas kernels: 12.6 us -> 16.8 us  [solve_poles(): pl.pallas_call(functools.partial(pole_kernel, interleave=interleave), out...]
    reshape x0 -> x3, local copies, waits for them, and re-layouts: none -> 2.22 us  [the longest x1 0.82 us: shards(): fix = fix.reshape(fix.shape[0], 2, group, WINDOW)]
    add x0 -> x2, other arithmetic: none -> 1.97 us  [the longest x1 0.98 us: shards(): main.at[..., :edge].add(fix[..., 2 * HALO + edge:2 * HALO + 2 * edge])]
    all_to_all x1, waiting for transfers between devices: 16 us -> 14.9 us  [shards(): lax.all_to_all(columns, 'wave', split_axis=0, concat_axis=0, tiled=True)]
    sub x1, local copies, waits for them, and re-layouts: 1.46 us -> 0.39 us  [shards(): parts = jnp.stack([north + south, north - south], axis=0)]
    add x1, local copies, waits for them, and re-layouts: 0.39 us -> 1.46 us  [shards(): parts = jnp.stack([north + south, north - south], axis=0)]
  transfers between devices with their start and end apart: 3 -> 3, of which waited for: 2 -> 1; matrix products, arithmetic and copies ran while one was open for 4% -> 5% of each run, Pallas kernels for 0% -> 18%
where the time goes in v5:
time: 71.5 us; the launch traced here: 70.7 us
  Pallas kernels  16.8 us (23%)
  waiting for transfers between devices  14.9 us (21%)
  starting transfers between devices  13.7 us (19%)
  local copies, waits for them, and re-layouts  11.1 us (16%)
  matrix products  8.31 us (12%)
  other arithmetic  5.52 us (8%)
    pallas_call x2, Pallas kernels, solve_poles(): pl.pallas_call(functools.partial(pole_kernel, interleave=interleave), out...  16.8 us
    all_to_all x1, waiting for transfers between devices, shards(): lax.all_to_all(columns, 'wave', split_axis=0, concat_axis=0, tiled=True)  14.9 us
    all_to_all x1, starting transfers between devices, shards(): lax.all_to_all(columns, 'wave', split_axis=0, concat_axis=0, tiled=True)  6.06 us
    ppermute x1, starting transfers between devices, shards(): right_halo = lax.ppermute(spectra[..., :HALO], 'pole', leftward)  5.76 us
    dot_general x1, matrix products, shards(): jnp.einsum('mpwlk,pwmcl->cpmk', leg, both, preferred_element_type=jnp.flo...  5.71 us
    scatter-add x1, local copies, waits for them, and re-layouts, shards(): main = main.at[..., local_k - edge:].add(fix[..., :edge])  2.69 us
    unnamed x1, matrix products  2.59 us
    ppermute x1, starting transfers between devices, shards(): left_halo = lax.ppermute(spectra[..., local_k - HALO:], 'pole', rightward)  1.92 us
  transfers between devices with their start and end apart: 3, of which 1 were waited for; matrix products, arithmetic and copies ran while one was open for 5% of the time, Pallas kernels for 18%

profile of v5, /device:TPU:6, one launch (start us, length us, event | category | flops | bytes accessed | tf_op | source)
XLA Modules:
  0.0 70.7 jit_solution(6589037224763567824)
XLA Ops:
  0.0 1.3 %copy-done = f32[6,256,192]{1,2,0:T(8,128)S(1)} copy-done((f32[6,256,192]{1,2,0:T(8,128)S(1)}, f32[6,256,192]{1,2,0:T(8,128)}, u32[]{:S(2)}) %copy-start) | copy-done | bytes 1179672
  1.3 2.6 %fusion.10 = f32[256,1152]{1,0:T(8,128)} fusion(f32[256,1152]{0,1:T(8,128)S(1)} %bitcast.21, s32[256]{0:T(256)} %param.11), kind=kOutput, calls=%fused_computation.14 | convolution fusion | flops 906035200 | bytes 2360320
  3.9 6.1 %all-to-all-start = ((f32[16,16,1152]{2,1,0:T(8,128)}), f32[16,16,1152]{2,1,0:T(8,128)S(1)}, u32[]{:S(2)}, u32[]{:S(2)}) async-start(f32[16,16,1152]{2,1,0:T(8,128)} %bitcast.10), calls=%async_computation | async-start | bytes 2359296 | tf_op jit(solution)/shard_map/all_to_all | solution.py:250
  10.7 0.6 gather_fusion
  11.6 0.7 reshape.319.coef_ref
  12.3 0.6 select_bitcast_fusion.poles_ref
  13.0 14.9 %all-to-all-done = f32[16,16,1152]{2,1,0:T(8,128)S(1)} async-done(((f32[16,16,1152]{2,1,0:T(8,128)}), f32[16,16,1152]{2,1,0:T(8,128)S(1)}, u32[]{:S(2)}, u32[]{:S(2)}) %all-to-all-start) | async-done | bytes 1179680 | tf_op jit(solution)/shard_map/all_to_all | solution.py:250
  27.8 0.9 %slice_add_fusion = (f32[8,16,1152]{2,1,0:T(8,128)}, f32[8,16,1152]{2,1,0:T(8,128)S(1)}) fusion(f32[16,16,1152]{2,1,0:T(8,128)S(1)} %all-to-all-done), kind=kLoop, calls=%fused_computation.11 | loop fusion | flops 294912 | bytes 2359296 | tf_op jit(solution)/shard_map/add | solution.py:254
  28.7 0.4 sub.27
  29.1 1.5 %add.209 = f32[1,8,16,6,192]{4,3,2,1,0:T(8,128)S(1)} reshape(f32[8,16,1152]{2,1,0:T(8,128)} %get-tuple-element.31) | data formatting | bytes 1179648 | tf_op jit(solution)/shard_map/add | solution.py:254
  30.6 0.3 pad_maximum_fusion
  31.0 0.4 subtract_convert_fusion
  31.5 5.7 %fusion.5 = f32[2,16,12,128]{3,2,1,0:T(8,128)S(1)} fusion(bf16[16,2,8,192,128]{4,3,2,1,0:T(8,128)(2,1)} %bitcast.23, bf16[2,8,16,6,192]{4,3,1,2,0:T(8,128)(2,1)S(1)} %subtract_convert_fusion, bf16[2,8,16,6,192]{4,3,1,2,0:T(8,128)(2,1)S(1)} %copy.28), kind=kOutput, calls=%fused_computation.9 | convolution fusion | flops 153354240 | bytes 13959168 | tf_op jit(solution)/shard_map/mpwlk,pwmcl->cpmk/dot_general | solution.py:258
  37.4 5.8 %collective-permute-start = (f32[6,2,16,8]{3,2,1,0:T(8,128)S(1)}, f32[6,2,16,8]{3,2,1,0:T(8,128)S(1)}, u32[]{:S(2)}, u32[]{:S(2)}) collective-permute-start(f32[6,2,16,8]{3,2,1,0:T(8,128)S(1)} %get-tuple-element.34), channel_id=1, source_target_pairs={{1,0},{2,1},{3,2},{4,3},{5,4},{6,5},{7,6},{9,8},{10,9},{11,10},{12... | collective-permute-start | bytes 18440 | tf_op jit(solution)/shard_map/ppermute | solution.py:266
  43.2 1.9 %collective-permute-start.1 = (f32[6,2,16,8]{3,2,1,0:T(8,128)S(1)}, f32[6,2,16,8]{3,2,1,0:T(8,128)S(1)}, u32[]{:S(2)}, u32[]{:S(2)}) collective-permute-start(f32[6,2,16,8]{3,2,1,0:T(8,128)S(1)} %get-tuple-element.33), channel_id=1, source_target_pairs={{0,1},{1,2},{2,3},{3,4},{4,5},{5,6},{6,7},{8,9},{9,10},{10,11},{11... | collective-permute-start | bytes 18440 | tf_op jit(solution)/shard_map/ppermute | solution.py:265
  45.1 0.7 %pad_maximum_fusion.1.spec_ref = f32[8,2,16,256]{3,2,1,0:T(8,128)} fusion(f32[2,2,16,256]{3,2,1,0:T(8,128)S(1)} %slice_multiply_fusion, f32[6,2,16,256]{3,2,1,0:T(8,128)S(1)} %concatenate.29), kind=kLoop, calls=%fused_computation.12 | loop fusion | flops 65536 | bytes 524288 | tf_op jit(solution)/shard_map/concatenate | solution.py:263
  45.8 12.6 %shard_map.55 = f32[6,2,16,128]{3,2,1,0:T(8,128)} custom-call(f32[4,32]{1,0:T(4,128)} %select_bitcast_fusion.poles_ref, f32[8,2,16,256]{3,2,1,0:T(8,128)} %pad_maximum_fusion.1.spec_ref, f32[4,2,16,256]{3,2,1,0:T(8,128)} %copy-done.1), custom_call_target="tpu_custom_call" | custom-call | tf_op jit(solution)/shard_map/pallas_call | solution.py:145
  58.7 0.7 %reshape.318.spec_ref = f32[8,2,4,128]{3,2,1,0:T(4,128)} reshape(f32[8,2,16,32]{3,2,1,0:T(8,128)S(1)} %pad_maximum_fusion.3) | data formatting | bytes 65536 | tf_op jit(solution)/shard_map/reshape | solution.py:282
  59.4 4.2 %shard_map.56 = f32[6,2,4,128]{3,2,1,0:T(4,128)} custom-call(f32[4,32]{1,0:T(4,128)} %select_bitcast_fusion.poles_ref, f32[8,2,4,128]{3,2,1,0:T(4,128)} %reshape.318.spec_ref, f32[4,2,4,128]{3,2,1,0:T(4,128)} %reshape.319.coef_ref), custom_call_target="tpu_custom_call" | custom-call | tf_op jit(solution)/shard_map/pallas_call | solution.py:145
  63.6 0.8 %reshape.320 = f32[6,2,16,32]{3,2,1,0:T(8,128)S(1)} reshape(f32[6,2,4,128]{3,2,1,0:T(4,128)} %shard_map.56) | data formatting | bytes 49152 | tf_op jit(solution)/shard_map/reshape | solution.py:285
  64.4 1.0 %slice_add_fusion.2 = f32[6,2,16,4]{3,2,1,0:T(8,128)S(1)} fusion(f32[6,2,16,32]{3,2,1,0:T(8,128)S(1)} %reshape.320, f32[6,2,16,128]{3,2,1,0:T(8,128)} %shard_map.55), kind=kLoop, calls=%fused_computation.20 | loop fusion | flops 768 | bytes 9216 | tf_op jit(solution)/shard_map/add | solution.py:286
  65.4 2.7 %scatter-add.6 = f32[6,2,16,128]{3,2,1,0:T(8,128)} dynamic-update-slice(f32[6,2,16,128]{3,2,1,0:T(8,128)} %shard_map.55, f32[6,2,16,4]{3,2,1,0:T(8,128)S(1)} %slice_add_fusion.2, s32[]{:T(128)} %constant.99.clone.1, s32[]{:T(128)} %constant.99.clone.1, s32[]{:T(128)} %constant.99.clone.1, s32[]{:T(128)} %constant.122.clone.1) | dynamic-update-slice | bytes 6148 | tf_op jit(solution)/shard_map/scatter-add | solution.py:286
  68.1 1.0 %slice_add_fusion.1 = f32[6,2,16,4]{3,2,1,0:T(8,128)S(1)} fusion(f32[6,2,16,32]{3,2,1,0:T(8,128)S(1)} %reshape.320, f32[6,2,16,128]{3,2,1,0:T(8,128)} %scatter-add.6), kind=kLoop, calls=%fused_computation.19 | loop fusion | flops 768 | bytes 9216 | tf_op jit(solution)/shard_map/add | solution.py:287
  69.1 1.6 %scatter-add.9 = f32[6,2,16,128]{3,2,1,0:T(8,128)} dynamic-update-slice(f32[6,2,16,128]{3,2,1,0:T(8,128)} %scatter-add.6, f32[6,2,16,4]{3,2,1,0:T(8,128)S(1)} %slice_add_fusion.1, s32[]{:T(128)} %constant.99.clone.1, s32[]{:T(128)} %constant.99.clone.1, s32[]{:T(128)} %constant.99.clone.1, s32[]{:T(128)} %constant.99.clone.1) | dynamic-update-slice | bytes 6148 | tf_op jit(solution)/shard_map/scatter-add | solution.py:287
  (45 shorter events, 1.6 us)
Async XLA Ops:
  0.0 1.3 %copy-start = (f32[6,256,192]{1,2,0:T(8,128)S(1)}, f32[6,256,192]{1,2,0:T(8,128)}, u32[]{:S(2)}) copy-start(f32[6,256,192]{1,2,0:T(8,128)} %param.9) | copy-start | bytes 3538948
  1.3 8.7 %copy-start.2 = (s32[256]{0:T(256)S(1)}, s32[256]{0:T(256)}, u32[]{:S(2)}) copy-start(s32[256]{0:T(256)} %param.11) | copy-start | bytes 3076
  3.9 6.7 %copy-start.3 = (f32[4,64]{1,0:T(4,128)S(1)}, f32[4,64]{1,0:T(4,128)}, u32[]{:S(2)}) copy-start(f32[4,64]{1,0:T(4,128)} %param.12) | copy-start | bytes 3076
  3.9 6.8 %copy-start.4 = (s32[32]{0:T(128)S(1)}, s32[32]{0:T(128)}, u32[]{:S(2)}) copy-start(s32[32]{0:T(128)} %param.13) | copy-start | bytes 388
  3.9 23.9 %all-to-all-start = ((f32[16,16,1152]{2,1,0:T(8,128)}), f32[16,16,1152]{2,1,0:T(8,128)S(1)}, u32[]{:S(2)}, u32[]{:S(2)}) async-start(f32[16,16,1152]{2,1,0:T(8,128)} %bitcast.10), calls=%async_computation | async-start | bytes 2359296 | tf_op jit(solution)/shard_map/all_to_all | solution.py:250
  10.4 18.7 %copy-start.1 = (f32[4,2,16,256]{3,2,1,0:T(8,128)}, f32[4,2,16,256]{3,2,1,0:T(8,128)S(1)}, u32[]{:S(2)}) copy-start(f32[4,2,16,256]{3,2,1,0:T(8,128)S(1)} %pad_maximum_fusion.2.coef_ref) | copy-start | bytes 393220
  37.4 21.0 %collective-permute-start = (f32[6,2,16,8]{3,2,1,0:T(8,128)S(1)}, f32[6,2,16,8]{3,2,1,0:T(8,128)S(1)}, u32[]{:S(2)}, u32[]{:S(2)}) collective-permute-start(f32[6,2,16,8]{3,2,1,0:T(8,128)S(1)} %get-tuple-element.34), channel_id=1, source_target_pairs={{1,0},{2,1},{3,2},{4,3},{5,4},{6,5},{7,6},{9,8},{10,9},{11,10},{12... | collective-permute-start | bytes 18440 | tf_op jit(solution)/shard_map/ppermute | solution.py:266
  43.2 15.2 %collective-permute-start.1 = (f32[6,2,16,8]{3,2,1,0:T(8,128)S(1)}, f32[6,2,16,8]{3,2,1,0:T(8,128)S(1)}, u32[]{:S(2)}, u32[]{:S(2)}) collective-permute-start(f32[6,2,16,8]{3,2,1,0:T(8,128)S(1)} %get-tuple-element.33), channel_id=1, source_target_pairs={{0,1},{1,2},{2,3},{3,4},{4,5},{5,6},{6,7},{8,9},{9,10},{10,11},{11... | collective-permute-start | bytes 18440 | tf_op jit(solution)/shard_map/ppermute | solution.py:265

commit v6 on v4

--- a/solution.py
+++ b/solution.py
@@ -6,7 +6,7 @@
 from jax.sharding import PartitionSpec as P
 
 SWEEPS = 8
-HALO = 8
+HALO = 4
 RING = 256
 CHUNK = 8
 GROUPS = 1
@@ -234,6 +234,13 @@
     coef_all = coefficients(own_waves, pole_pos * local_k, local_k, local_k * pole_count)
     coef_all = jnp.concatenate([coriolis_step * coef_all[:2], coef_all[2:]], axis=0)
     poles = jnp.take(pole_table, pole_index, axis=1)
+    send_left, send_right = lax.optimization_barrier(
+        (legendre[..., local_k - HALO :].astype(jnp.float32), legendre[..., :HALO].astype(jnp.float32))
+    )
+    edge_left = lax.ppermute(send_left, "pole", rightward)
+    edge_right = lax.ppermute(send_right, "pole", leftward)
+    edges = jnp.concatenate([edge_right, edge_left], axis=3)
+    edges = edges.reshape(slots, 2, half_count, lat_rows, 2 * HALO)
     onehot = (wave_table[:, None] == jnp.arange(waves, dtype=jnp.int32)[None, :]).astype(jnp.float32)
     onehot = onehot.reshape(wave_count, GROUPS, group, waves)
     leg_blocks = legendre.reshape(slots, 2, half_count, lat_rows, local_k)
@@ -252,8 +259,13 @@
         leg = leg_blocks[g * group : (g + 1) * group]
         products = jnp.einsum("mpwlk,pwmcl->cpmk", leg, both, preferred_element_type=jnp.float32)
         spectra = products[:comps] + products[comps:]
-        left_halo = lax.ppermute(spectra[..., local_k - HALO :], "pole", rightward)
-        right_halo = lax.ppermute(spectra[..., :HALO], "pole", leftward)
+        halo_products = jnp.einsum(
+            "mpwlk,pwmcl->cpmk", edges[g * group : (g + 1) * group], both.astype(jnp.float32),
+            precision=lax.Precision.HIGHEST, preferred_element_type=jnp.float32,
+        )
+        halos = halo_products[:comps] + halo_products[comps:]
+        right_halo = halos[..., :HALO]
+        left_halo = halos[..., HALO:]
         gap = jnp.zeros(spectra.shape[:3] + (RING - local_k - 2 * HALO,), jnp.float32)
         wide = jnp.concatenate([spectra, right_halo, gap, left_halo], axis=3)
         coef = coef_all[:, :, g * group : (g + 1) * group]

time: 65.8 us -> 128 us (1.95)
  the two profiles are of different devices: /device:TPU:6 before, /device:TPU:64 now
where the time goes in v6:
time: 128 us; the launch traced here: 127 us
  local copies, waits for them, and re-layouts  50.3 us (39%)
  waiting for transfers between devices  31.8 us (25%)
  starting transfers between devices  13.9 us (11%)
  Pallas kernels  12.6 us (10%)
  matrix products  11.8 us (9%)
  other arithmetic  6.03 us (5%)
    ppermute x1, waiting for transfers between devices, shards(): edge_left = lax.ppermute(send_left, 'pole', rightward)  31.8 us
    unnamed x17, local copies, waits for them, and re-layouts  22.6 us
    slice x1, local copies, waits for them, and re-layouts, shards(): legendre[..., :HALO].astype(jnp.float32)  19.3 us
    pallas_call x1, Pallas kernels, solve_poles(): pl.pallas_call(pole_kernel, out_shape=jax.ShapeDtypeStruct((6, parities,...  12.6 us
    dot_general x1, matrix products, shards(): jnp.einsum('mpwlk,pwmcl->cpmk', leg, both, preferred_element_type=jnp.flo...  7.31 us
    ppermute x1, starting transfers between devices, shards(): edge_right = lax.ppermute(send_right, 'pole', leftward)  5.74 us
    all_to_all x1, starting transfers between devices, shards(): lax.all_to_all(columns, 'wave', split_axis=0, concat_axis=0, tiled=True)  5.69 us
    dot_general x1, matrix products, shards(): jnp.einsum('mpwlk,pwmcl->cpmk', edges[g * group:(g + 1) * group], both.as...  2.69 us
  transfers between devices with their start and end apart: 3, of which 1 were waited for; matrix products, arithmetic and copies ran while one was open for 8% of the time, Pallas kernels for 0%

profile of v6, /device:TPU:64, one launch (start us, length us, event | category | flops | bytes accessed | tf_op | source)
XLA Modules:
  0.0 126.8 jit_solution(12712942882321440445)
XLA Ops:
  0.0 19.3 %fusion.33 = (bf16[16,2,1536,4]{3,2,1,0:T(8,128)(2,1)}, bf16[16,2,1536,4]{3,2,1,0:T(8,128)(2,1)}) fusion(bf16[16,2,1536,128]{3,2,1,0:T(8,128)(2,1)} %param.6), kind=kLoop, calls=%fused_computation.67 | loop fusion | bytes 1572864 | tf_op jit(solution)/shard_map/slice | solution.py:238
  19.3 10.5 %copy.39 = bf16[16,2,1536,4]{2,0,3,1:T(8,128)(2,1)S(1)} copy(bf16[16,2,1536,4]{3,2,1,0:T(8,128)(2,1)} %get-tuple-element.12) | data formatting | bytes 786432
  29.9 10.5 %copy.40 = bf16[16,2,1536,4]{2,0,3,1:T(8,128)(2,1)S(1)} copy(bf16[16,2,1536,4]{3,2,1,0:T(8,128)(2,1)} %get-tuple-element.11) | data formatting | bytes 786432
  40.5 2.5 %collective-permute-start.1 = (f32[16,2,1536,4]{2,0,3,1:T(8,128)S(1)}, f32[16,2,1536,4]{2,0,3,1:T(8,128)}, u32[]{:S(2)}, u32[]{:S(2)}) collective-permute-start(f32[16,2,1536,4]{2,0,3,1:T(8,128)S(1)} %convert_element_type.37), channel_id=1, source_target_pairs={{0,1},{1,2},{2,3},{3,4},{4,5},{5,6},{6,7},{8,9},{9,10},{10,11},{11... | collective-permute-start | bytes 2359304 | tf_op jit(solution)/shard_map/ppermute | solution.py:240
  43.0 5.7 %collective-permute-start = (f32[16,2,1536,4]{2,0,3,1:T(8,128)S(1)}, f32[16,2,1536,4]{2,0,3,1:T(8,128)}, u32[]{:S(2)}, u32[]{:S(2)}) collective-permute-start(f32[16,2,1536,4]{2,0,3,1:T(8,128)S(1)} %convert_element_type.38), channel_id=1, source_target_pairs={{1,0},{2,1},{3,2},{4,3},{5,4},{6,5},{7,6},{9,8},{10,9},{11,10},{12... | collective-permute-start | bytes 2359304 | tf_op jit(solution)/shard_map/ppermute | solution.py:241
  48.8 1.8 %fusion.10 = f32[256,1152]{1,0:T(8,128)} fusion(f32[256,1152]{0,1:T(8,128)S(1)} %bitcast.23, s32[256]{0:T(256)S(1)} %copy-done.4), kind=kOutput, calls=%fused_computation.16 | convolution fusion | flops 906035200 | bytes 2360320
  50.6 5.7 %all-to-all-start = ((f32[16,16,1152]{2,1,0:T(8,128)}), f32[16,16,1152]{2,1,0:T(8,128)}, u32[]{:S(2)}, u32[]{:S(2)}) async-start(f32[16,16,1152]{2,1,0:T(8,128)} %bitcast.12), calls=%async_computation | async-start | bytes 2359296 | tf_op jit(solution)/shard_map/all_to_all | solution.py:252
  56.9 0.6 gather_fusion
  57.5 0.7 pad_maximum_fusion.10.coef_ref
  58.2 0.6 select_bitcast_fusion.poles_ref
  58.9 31.8 %collective-permute-done.1 = f32[16,2,1536,4]{2,0,3,1:T(8,128)} collective-permute-done((f32[16,2,1536,4]{2,0,3,1:T(8,128)S(1)}, f32[16,2,1536,4]{2,0,3,1:T(8,128)}, u32[]{:S(2)}, u32[]{:S(2)}) %collective-permute-start.1) | collective-permute-done | bytes 786464 | tf_op jit(solution)/shard_map/ppermute | solution.py:240
  90.7 1.6 %copy.33 = f32[16,2,1536,4]{2,3,1,0:T(4,128)S(1)} copy(f32[16,2,1536,4]{2,0,3,1:T(8,128)} %collective-permute-done.1) | data formatting | bytes 1572864 | tf_op jit(solution)/shard_map/ppermute | solution.py:240
  92.4 1.6 %copy.32 = f32[16,2,1536,4]{2,3,1,0:T(4,128)S(1)} copy(f32[16,2,1536,4]{2,0,3,1:T(8,128)} %collective-permute-done) | data formatting | bytes 1572864 | tf_op jit(solution)/shard_map/ppermute | solution.py:241
  94.4 2.0 %reshape.242 = f32[16,2,8,192,8]{3,2,4,1,0:T(8,128)} reshape(f32[16,2,1536,8]{2,3,1,0:T(8,128)S(1)} %pad_maximum_fusion.2) | data formatting | bytes 3145728 | tf_op jit(solution)/shard_map/reshape | solution.py:243
  96.3 2.1 %slice_add_fusion = (f32[8,16,1152]{2,1,0:T(8,128)}, f32[8,16,1152]{2,1,0:T(8,128)S(1)}) fusion(f32[16,16,1152]{2,1,0:T(8,128)} %all-to-all-done), kind=kLoop, calls=%fused_computation.13 | loop fusion | flops 294912 | bytes 2359296 | tf_op jit(solution)/shard_map/add | solution.py:256
  98.5 0.4 sub.27
  98.9 1.5 %add.196 = f32[1,8,16,6,192]{4,3,2,1,0:T(8,128)S(1)} reshape(f32[8,16,1152]{2,1,0:T(8,128)} %get-tuple-element.13) | data formatting | bytes 1179648 | tf_op jit(solution)/shard_map/add | solution.py:256
  100.7 0.5 subtract_convert_fusion
  101.2 0.5 copy-done.1
  101.7 1.0 copy-done.3
  102.7 2.7 %fusion.7 = f32[2,16,12,8]{2,3,1,0:T(8,128)S(1)} fusion(f32[16,2,8,192,8]{3,2,4,1,0:T(8,128)S(1)} %copy-done.2, bf16[2,8,16,6,192]{4,3,1,2,0:T(8,128)(2,1)S(1)} %subtract_convert_fusion, bf16[2,8,16,6,192]{4,3,1,2,0:T(8,128)(2,1)S(1)} %copy.52), kind=kOutput, calls=%fused_computation.11 | convolution fusion | flops 58982400 | bytes 2764800 | tf_op jit(solution)/shard_map/mpwlk,pwmcl->cpmk/dot_general | solution.py:262
  105.8 7.3 %fusion.4 = f32[2,16,12,128]{3,2,1,0:T(8,128)S(1)} fusion(bf16[16,2,8,192,128]{4,3,2,1,0:T(8,128)(2,1)} %bitcast.24, bf16[2,8,16,6,192]{4,3,1,2,0:T(8,128)(2,1)} %copy-done.3, bf16[2,8,16,6,192]{4,3,1,2,0:T(8,128)(2,1)} %copy-done.1), kind=kOutput, calls=%fused_computation.10 | convolution fusion | flops 153354240 | bytes 13959168 | tf_op jit(solution)/shard_map/mpwlk,pwmcl->cpmk/dot_general | solution.py:260
  113.4 0.8 pad_maximum_fusion.9.spec_ref
  114.2 12.6 %shard_map.55 = f32[6,2,16,128]{3,2,1,0:T(8,128)} custom-call(f32[4,32]{1,0:T(4,128)} %select_bitcast_fusion.poles_ref, f32[8,2,16,256]{3,2,1,0:T(8,128)} %pad_maximum_fusion.9.spec_ref, f32[4,2,16,256]{3,2,1,0:T(8,128)} %pad_maximum_fusion.10.coef_ref), custom_call_target="tpu_custom_call" | custom-call | tf_op jit(solution)/shard_map/pallas_call | solution.py:140
  (41 shorter events, 2.1 us)
Async XLA Ops:
  0.0 48.7 %copy-start = (f32[6,256,192]{1,2,0:T(8,128)S(1)}, f32[6,256,192]{1,2,0:T(8,128)}, u32[]{:S(2)}) copy-start(f32[6,256,192]{1,2,0:T(8,128)} %param.5) | copy-start | bytes 3538948
  29.9 18.9 %copy-start.4 = (s32[256]{0:T(256)S(1)}, s32[256]{0:T(256)}, u32[]{:S(2)}) copy-start(s32[256]{0:T(256)} %param.7) | copy-start | bytes 3076
  40.5 50.3 %collective-permute-start.1 = (f32[16,2,1536,4]{2,0,3,1:T(8,128)S(1)}, f32[16,2,1536,4]{2,0,3,1:T(8,128)}, u32[]{:S(2)}, u32[]{:S(2)}) collective-permute-start(f32[16,2,1536,4]{2,0,3,1:T(8,128)S(1)} %convert_element_type.37), channel_id=1, source_target_pairs={{0,1},{1,2},{2,3},{3,4},{4,5},{5,6},{6,7},{8,9},{9,10},{10,11},{11... | collective-permute-start | bytes 2359304 | tf_op jit(solution)/shard_map/ppermute | solution.py:240
  43.0 49.4 %collective-permute-start = (f32[16,2,1536,4]{2,0,3,1:T(8,128)S(1)}, f32[16,2,1536,4]{2,0,3,1:T(8,128)}, u32[]{:S(2)}, u32[]{:S(2)}) collective-permute-start(f32[16,2,1536,4]{2,0,3,1:T(8,128)S(1)} %convert_element_type.38), channel_id=1, source_target_pairs={{1,0},{2,1},{3,2},{4,3},{5,4},{6,5},{7,6},{9,8},{10,9},{11,10},{12... | collective-permute-start | bytes 2359304 | tf_op jit(solution)/shard_map/ppermute | solution.py:241
  48.7 7.6 %copy-start.6 = (s32[32]{0:T(128)S(1)}, s32[32]{0:T(128)}, u32[]{:S(2)}) copy-start(s32[32]{0:T(128)} %param.9) | copy-start | bytes 388
  48.7 8.0 %copy-start.5 = (f32[4,64]{1,0:T(4,128)S(1)}, f32[4,64]{1,0:T(4,128)}, u32[]{:S(2)}) copy-start(f32[4,64]{1,0:T(4,128)} %param.8) | copy-start | bytes 3076
  50.6 45.7 %all-to-all-start = ((f32[16,16,1152]{2,1,0:T(8,128)}), f32[16,16,1152]{2,1,0:T(8,128)}, u32[]{:S(2)}, u32[]{:S(2)}) async-start(f32[16,16,1152]{2,1,0:T(8,128)} %bitcast.12), calls=%async_computation | async-start | bytes 2359296 | tf_op jit(solution)/shard_map/all_to_all | solution.py:252
  100.7 1.0 copy-start.1
  100.7 2.0 %copy-start.2 = (f32[16,2,8,192,8]{3,2,4,1,0:T(8,128)S(1)}, f32[16,2,8,192,8]{3,2,4,1,0:T(8,128)}, u32[]{:S(2)}) copy-start(f32[16,2,8,192,8]{3,2,4,1,0:T(8,128)} %reshape.242) | copy-start | bytes 4718596
  101.7 1.0 copy-start.3

commit v7 on v6

--- a/solution.py
+++ b/solution.py
@@ -234,13 +234,12 @@
     coef_all = coefficients(own_waves, pole_pos * local_k, local_k, local_k * pole_count)
     coef_all = jnp.concatenate([coriolis_step * coef_all[:2], coef_all[2:]], axis=0)
     poles = jnp.take(pole_table, pole_index, axis=1)
-    send_left, send_right = lax.optimization_barrier(
-        (legendre[..., local_k - HALO :].astype(jnp.float32), legendre[..., :HALO].astype(jnp.float32))
-    )
+    send_left = jnp.swapaxes(legendre[..., local_k - HALO :], 2, 3).astype(jnp.float32)
+    send_right = jnp.swapaxes(legendre[..., :HALO], 2, 3).astype(jnp.float32)
     edge_left = lax.ppermute(send_left, "pole", rightward)
     edge_right = lax.ppermute(send_right, "pole", leftward)
-    edges = jnp.concatenate([edge_right, edge_left], axis=3)
-    edges = edges.reshape(slots, 2, half_count, lat_rows, 2 * HALO)
+    edges = jnp.concatenate([edge_right, edge_left], axis=2)
+    edges = edges.reshape(slots, 2, 2 * HALO, half_count, lat_rows)
     onehot = (wave_table[:, None] == jnp.arange(waves, dtype=jnp.int32)[None, :]).astype(jnp.float32)
     onehot = onehot.reshape(wave_count, GROUPS, group, waves)
     leg_blocks = legendre.reshape(slots, 2, half_count, lat_rows, local_k)
@@ -260,8 +259,11 @@
         products = jnp.einsum("mpwlk,pwmcl->cpmk", leg, both, preferred_element_type=jnp.float32)
         spectra = products[:comps] + products[comps:]
         halo_products = jnp.einsum(
-            "mpwlk,pwmcl->cpmk", edges[g * group : (g + 1) * group], both.astype(jnp.float32),
-            precision=lax.Precision.HIGHEST, preferred_element_type=jnp.float32,
+            "mpkwl,pwmcl->cpmk",
+            edges[g * group : (g + 1) * group],
+            both.astype(jnp.float32),
+            precision=lax.Precision.HIGHEST,
+            preferred_element_type=jnp.float32,
         )
         halos = halo_products[:comps] + halo_products[comps:]
         right_halo = halos[..., :HALO]

time: 128 us -> 116 us (0.906)
  the two profiles are of different devices: /device:TPU:64 before, /device:TPU:6 now
where the time goes in v7:
time: 116 us; the launch traced here: 115 us
  local copies, waits for them, and re-layouts  49.1 us (42%)
  waiting for transfers between devices  20.2 us (17%)
  starting transfers between devices  14.2 us (12%)
  Pallas kernels  12.6 us (11%)
  matrix products  11.8 us (10%)
  other arithmetic  6.94 us (6%)
    unnamed x17, local copies, waits for them, and re-layouts  22.6 us
    ppermute x1, waiting for transfers between devices, shards(): edge_right = lax.ppermute(send_right, 'pole', leftward)  20.2 us
    slice x1, local copies, waits for them, and re-layouts, shards(): send_right = jnp.swapaxes(legendre[..., :HALO], 2, 3).astype(jnp.float32)  19.3 us
    pallas_call x1, Pallas kernels, solve_poles(): pl.pallas_call(pole_kernel, out_shape=jax.ShapeDtypeStruct((6, parities,...  12.6 us
    dot_general x1, matrix products, shards(): jnp.einsum('mpwlk,pwmcl->cpmk', leg, both, preferred_element_type=jnp.flo...  7.31 us
    all_to_all x1, starting transfers between devices, shards(): lax.all_to_all(columns, 'wave', split_axis=0, concat_axis=0, tiled=True)  5.99 us
    ppermute x1, starting transfers between devices, shards(): edge_left = lax.ppermute(send_left, 'pole', rightward)  5.78 us
    dot_general x1, matrix products, shards(): jnp.einsum('mpkwl,pwmcl->cpmk', edges[g * group:(g + 1) * group], both.as...  2.69 us
  transfers between devices with their start and end apart: 3, of which 1 were waited for; matrix products, arithmetic and copies ran while one was open for 18% of the time, Pallas kernels for 0%

profile of v7, /device:TPU:6, one launch (start us, length us, event | category | flops | bytes accessed | tf_op | source)
XLA Modules:
  0.0 115.2 jit_solution(6147775499444777258)
XLA Ops:
  0.0 19.3 %fusion.33 = (bf16[16,2,1536,4]{3,2,1,0:T(8,128)(2,1)}, bf16[16,2,1536,4]{3,2,1,0:T(8,128)(2,1)}) fusion(bf16[16,2,1536,128]{3,2,1,0:T(8,128)(2,1)} %param.6), kind=kLoop, calls=%fused_computation.69 | loop fusion | bytes 1572864 | tf_op jit(solution)/shard_map/slice | solution.py:238
  19.3 10.5 %copy.40 = bf16[16,2,1536,4]{2,0,3,1:T(8,128)(2,1)S(1)} copy(bf16[16,2,1536,4]{3,2,1,0:T(8,128)(2,1)} %get-tuple-element.8) | data formatting | bytes 786432
  29.9 5.8 %collective-permute-start.1 = (f32[16,2,4,1536]{3,0,2,1:T(8,128)S(1)}, f32[16,2,4,1536]{3,0,2,1:T(8,128)S(1)}, u32[]{:S(2)}, u32[]{:S(2)}) collective-permute-start(f32[16,2,4,1536]{3,0,2,1:T(8,128)S(1)} %convert_bitcast_fusion), channel_id=1, source_target_pairs={{0,1},{1,2},{2,3},{3,4},{4,5},{5,6},{6,7},{8,9},{9,10},{10,11},{11... | collective-permute-start | bytes 2359304 | tf_op jit(solution)/shard_map/ppermute | solution.py:239
  35.7 10.5 %copy.39 = bf16[16,2,1536,4]{2,0,3,1:T(8,128)(2,1)S(1)} copy(bf16[16,2,1536,4]{3,2,1,0:T(8,128)(2,1)} %get-tuple-element.7) | data formatting | bytes 786432
  46.2 1.0 convert_bitcast_fusion.1
  47.2 2.5 %collective-permute-start = (f32[16,2,4,1536]{3,0,2,1:T(8,128)}, f32[16,2,4,1536]{3,0,2,1:T(8,128)}, u32[]{:S(2)}, u32[]{:S(2)}) collective-permute-start(f32[16,2,4,1536]{3,0,2,1:T(8,128)} %convert_bitcast_fusion.1), channel_id=1, source_target_pairs={{1,0},{2,1},{3,2},{4,3},{5,4},{6,5},{7,6},{9,8},{10,9},{11,10},{12... | collective-permute-start | bytes 2359304 | tf_op jit(solution)/shard_map/ppermute | solution.py:240
  49.7 1.8 %fusion.10 = f32[256,1152]{1,0:T(8,128)} fusion(f32[256,1152]{0,1:T(8,128)S(1)} %bitcast.25, s32[256]{0:T(256)S(1)} %copy-done.4), kind=kOutput, calls=%fused_computation.18 | convolution fusion | flops 906035200 | bytes 2360320
  51.5 6.0 %all-to-all-start = ((f32[16,16,1152]{2,1,0:T(8,128)}), f32[16,16,1152]{2,1,0:T(8,128)}, u32[]{:S(2)}, u32[]{:S(2)}) async-start(f32[16,16,1152]{2,1,0:T(8,128)} %bitcast.14), calls=%async_computation | async-start | bytes 2359296 | tf_op jit(solution)/shard_map/all_to_all | solution.py:251
  58.1 0.6 gather_fusion
  58.7 0.7 pad_maximum_fusion.10.coef_ref
  59.4 0.6 select_bitcast_fusion.poles_ref
  60.1 0.5 copy.33
  60.6 20.2 %collective-permute-done = f32[16,2,4,1536]{3,0,2,1:T(8,128)} collective-permute-done((f32[16,2,4,1536]{3,0,2,1:T(8,128)}, f32[16,2,4,1536]{3,0,2,1:T(8,128)}, u32[]{:S(2)}, u32[]{:S(2)}) %collective-permute-start) | collective-permute-done | bytes 786464 | tf_op jit(solution)/shard_map/ppermute | solution.py:240
  80.8 1.6 %copy.32 = f32[16,2,4,1536]{3,2,1,0:T(4,128)S(1)} copy(f32[16,2,4,1536]{3,0,2,1:T(8,128)} %collective-permute-done) | data formatting | bytes 1572864 | tf_op jit(solution)/shard_map/ppermute | solution.py:240
  82.8 2.0 %reshape.242 = f32[16,2,8,8,192]{4,3,2,1,0:T(8,128)} reshape(f32[16,2,8,1536]{3,2,1,0:T(8,128)S(1)} %pad_maximum_fusion.2) | data formatting | bytes 3145728 | tf_op jit(solution)/shard_map/reshape | solution.py:242
  84.8 2.1 %slice_add_fusion = (f32[8,16,1152]{2,1,0:T(8,128)}, f32[8,16,1152]{2,1,0:T(8,128)S(1)}) fusion(f32[16,16,1152]{2,1,0:T(8,128)} %all-to-all-done), kind=kLoop, calls=%fused_computation.15 | loop fusion | flops 294912 | bytes 2359296 | tf_op jit(solution)/shard_map/add | solution.py:255
  87.3 1.5 %add.196 = f32[1,8,16,6,192]{4,3,2,1,0:T(8,128)S(1)} reshape(f32[8,16,1152]{2,1,0:T(8,128)} %get-tuple-element.9) | data formatting | bytes 1179648 | tf_op jit(solution)/shard_map/add | solution.py:255
  89.2 0.5 subtract_convert_fusion
  89.7 0.5 copy-done.1
  90.2 1.0 copy-done.3
  91.1 2.7 %fusion.7 = f32[2,16,12,8]{2,3,1,0:T(8,128)S(1)} fusion(f32[16,2,8,8,192]{4,3,2,1,0:T(8,128)S(1)} %copy-done.2, bf16[2,8,16,6,192]{4,3,1,2,0:T(8,128)(2,1)S(1)} %subtract_convert_fusion, bf16[2,8,16,6,192]{4,3,1,2,0:T(8,128)(2,1)S(1)} %copy.52), kind=kOutput, calls=%fused_computation.11 | convolution fusion | flops 58982400 | bytes 2764800 | tf_op jit(solution)/shard_map/mpkwl,pwmcl->cpmk/dot_general | solution.py:261
  94.3 7.3 %fusion.4 = f32[2,16,12,128]{3,2,1,0:T(8,128)S(1)} fusion(bf16[16,2,8,192,128]{4,3,2,1,0:T(8,128)(2,1)} %bitcast.26, bf16[2,8,16,6,192]{4,3,1,2,0:T(8,128)(2,1)} %copy-done.3, bf16[2,8,16,6,192]{4,3,1,2,0:T(8,128)(2,1)} %copy-done.1), kind=kOutput, calls=%fused_computation.10 | convolution fusion | flops 153354240 | bytes 13959168 | tf_op jit(solution)/shard_map/mpwlk,pwmcl->cpmk/dot_general | solution.py:259
  101.8 0.8 pad_maximum_fusion.9.spec_ref
  102.6 12.6 %shard_map.55 = f32[6,2,16,128]{3,2,1,0:T(8,128)} custom-call(f32[4,32]{1,0:T(4,128)} %select_bitcast_fusion.poles_ref, f32[8,2,16,256]{3,2,1,0:T(8,128)} %pad_maximum_fusion.9.spec_ref, f32[4,2,16,256]{3,2,1,0:T(8,128)} %pad_maximum_fusion.10.coef_ref), custom_call_target="tpu_custom_call" | custom-call | tf_op jit(solution)/shard_map/pallas_call | solution.py:140
  (41 shorter events, 2.5 us)
Async XLA Ops:
  0.0 49.6 %copy-start = (f32[6,256,192]{1,2,0:T(8,128)S(1)}, f32[6,256,192]{1,2,0:T(8,128)}, u32[]{:S(2)}) copy-start(f32[6,256,192]{1,2,0:T(8,128)} %param.5) | copy-start | bytes 3538948
  29.9 30.2 %collective-permute-start.1 = (f32[16,2,4,1536]{3,0,2,1:T(8,128)S(1)}, f32[16,2,4,1536]{3,0,2,1:T(8,128)S(1)}, u32[]{:S(2)}, u32[]{:S(2)}) collective-permute-start(f32[16,2,4,1536]{3,0,2,1:T(8,128)S(1)} %convert_bitcast_fusion), channel_id=1, source_target_pairs={{0,1},{1,2},{2,3},{3,4},{4,5},{5,6},{6,7},{8,9},{9,10},{10,11},{11... | collective-permute-start | bytes 2359304 | tf_op jit(solution)/shard_map/ppermute | solution.py:239
  35.6 14.0 %copy-start.4 = (s32[256]{0:T(256)S(1)}, s32[256]{0:T(256)}, u32[]{:S(2)}) copy-start(s32[256]{0:T(256)} %param.7) | copy-start | bytes 3076
  47.2 33.7 %collective-permute-start = (f32[16,2,4,1536]{3,0,2,1:T(8,128)}, f32[16,2,4,1536]{3,0,2,1:T(8,128)}, u32[]{:S(2)}, u32[]{:S(2)}) collective-permute-start(f32[16,2,4,1536]{3,0,2,1:T(8,128)} %convert_bitcast_fusion.1), channel_id=1, source_target_pairs={{1,0},{2,1},{3,2},{4,3},{5,4},{6,5},{7,6},{9,8},{10,9},{11,10},{12... | collective-permute-start | bytes 2359304 | tf_op jit(solution)/shard_map/ppermute | solution.py:240
  49.6 7.9 %copy-start.6 = (s32[32]{0:T(128)S(1)}, s32[32]{0:T(128)}, u32[]{:S(2)}) copy-start(s32[32]{0:T(128)} %param.9) | copy-start | bytes 388
  49.6 8.3 %copy-start.5 = (f32[4,64]{1,0:T(4,128)S(1)}, f32[4,64]{1,0:T(4,128)}, u32[]{:S(2)}) copy-start(f32[4,64]{1,0:T(4,128)} %param.8) | copy-start | bytes 3076
  51.5 33.3 %all-to-all-start = ((f32[16,16,1152]{2,1,0:T(8,128)}), f32[16,16,1152]{2,1,0:T(8,128)}, u32[]{:S(2)}, u32[]{:S(2)}) async-start(f32[16,16,1152]{2,1,0:T(8,128)} %bitcast.14), calls=%async_computation | async-start | bytes 2359296 | tf_op jit(solution)/shard_map/all_to_all | solution.py:251
  89.2 1.0 copy-start.1
  89.2 2.0 %copy-start.2 = (f32[16,2,8,8,192]{4,3,2,1,0:T(8,128)S(1)}, f32[16,2,8,8,192]{4,3,2,1,0:T(8,128)}, u32[]{:S(2)}) copy-start(f32[16,2,8,8,192]{4,3,2,1,0:T(8,128)} %reshape.242) | copy-start | bytes 4718596
  90.2 1.0 copy-start.3

commit v8 on v4

--- a/solution.py
+++ b/solution.py
@@ -6,8 +6,9 @@
 from jax.sharding import PartitionSpec as P
 
 SWEEPS = 8
-HALO = 8
-RING = 256
+HALO_K = 4
+HALO = 2 * HALO_K
+RING = 384
 CHUNK = 8
 GROUPS = 1
 INTERLEAVE = 4
@@ -28,11 +29,10 @@
     lane = jnp.arange(RING, dtype=jnp.int32)
     index = jnp.where(lane >= RING - HALO, base + lane - RING, base + lane)
     inside = ((lane < width + HALO) | (lane >= RING - HALO)) & (index >= 0) & (index < total)
-    index = jnp.clip(index, 0, total - 1).astype(jnp.float32)
-    parity = jnp.arange(2, dtype=jnp.int32).astype(jnp.float32)
-    order = (2.0 * index[None, :] + parity[:, None])[:, None, :]
-    upper_inside = inside[None, None, :] & (order + 1.0 < 2.0 * total)
-    wave = wavenum[None, :, None]
+    order = jnp.clip(index, 0, total - 1).astype(jnp.float32)[None, :]
+    upper_inside = inside & (index + 1 < total)
+    lower_inside = inside & (index - 1 >= 0)
+    wave = wavenum[:, None]
     degree = wave + order
     product = degree * (degree + 1.0)
     rossby = coriolis_step * wave / jnp.maximum(product, 2.0)
@@ -43,103 +43,89 @@
     e_hi = jnp.sqrt(
         after * (2.0 * wave + after) / jnp.maximum(4.0 * upper_deg * upper_deg - 1.0, 1.0)
     )
-    e_lo = jnp.where(inside[None, None, :], e_lo, 0.0)
-    e_hi = jnp.where(upper_inside, e_hi, 0.0)
+    e_lo = jnp.where(lower_inside[None, :], e_lo, 0.0)
+    e_hi = jnp.where(upper_inside[None, :], e_hi, 0.0)
     return jnp.stack([e_lo, e_hi, rossby, gravity], axis=0)
 
 
 def pole_kernel(poles_ref, spec_ref, coef_ref, out_ref):
     npoles = poles_ref.shape[1]
-    rows = spec_ref.shape[2]
-    lanes = spec_ref.shape[3]
-    width = out_ref.shape[3]
+    rows = spec_ref.shape[1]
+    lanes = spec_ref.shape[2]
+    width = out_ref.shape[2]
     out_ref[...] = jnp.zeros(out_ref.shape, jnp.float32)
 
     def pole_step(step, carry):
-        lanes_work = []
+        work = []
         for u in range(INTERLEAVE):
             q = step * INTERLEAVE + u
             scal = [poles_ref[i, q] for i in range(4)]
             for r0 in range(0, rows, CHUNK):
-                lanes_work.append((scal, pl.ds(r0, CHUNK)))
-
-        def ld(ref, i, p, sl):
-            return ref[i, p, sl, :]
+                work.append((scal, pl.ds(r0, CHUNK)))
+
+        def ld(ref, i, sl):
+            return ref[i, sl, :]
 
         def near(x, sl):
-            n0 = ld(coef_ref, 0, 0, sl) * pltpu.roll(x[1], 1, 1) + ld(coef_ref, 1, 0, sl) * x[1]
-            n1 = ld(coef_ref, 0, 1, sl) * x[0] + ld(coef_ref, 1, 1, sl) * pltpu.roll(
-                x[0], lanes - 1, 1
+            return ld(coef_ref, 0, sl) * pltpu.roll(x, 1, 1) + ld(coef_ref, 1, sl) * pltpu.roll(
+                x, lanes - 1, 1
             )
-            return (n0, n1)
 
         prep = []
-        for (a_re, a_im, _, _), sl in lanes_work:
-            inv, dinv, lift, base = [], [], [], []
-            for p in range(2):
-                grav = ld(coef_ref, 3, p, sl)
-                b_im = a_im + ld(coef_ref, 2, p, sl)
-                b_rec = 1.0 / (a_re * a_re + b_im * b_im)
-                inv.append((a_re * b_rec, -b_im * b_rec))
-                det_re = a_re * a_re - b_im * a_im + grav * grav
-                det_im = a_re * a_im + b_im * a_re
-                det_rec = 1.0 / (det_re * det_re + det_im * det_im)
-                dv = (det_re * det_rec, -det_im * det_rec)
-                dinv.append(dv)
-                lift.append(cmul(a_re, a_im, dv[0], dv[1]))
-                base.append(cmul(ld(spec_ref, 6, p, sl), ld(spec_ref, 7, p, sl), dv[0], dv[1]))
+        for (a_re, a_im, _, _), sl in work:
+            grav = ld(coef_ref, 3, sl)
+            b_im = a_im + ld(coef_ref, 2, sl)
+            b_rec = 1.0 / (a_re * a_re + b_im * b_im)
+            inv = (a_re * b_rec, -b_im * b_rec)
+            det_re = a_re * a_re - b_im * a_im + grav * grav
+            det_im = a_re * a_im + b_im * a_re
+            det_rec = 1.0 / (det_re * det_re + det_im * det_im)
+            dinv = (det_re * det_rec, -det_im * det_rec)
+            lift = cmul(a_re, a_im, dinv[0], dinv[1])
+            base = cmul(ld(spec_ref, 6, sl), ld(spec_ref, 7, sl), dinv[0], dinv[1])
             prep.append((inv, dinv, lift, base))
-        state = [None] * len(lanes_work)
+        state = [None] * len(work)
         for sweep in range(SWEEPS):
-            for n, ((a_re, a_im, _, _), sl) in enumerate(lanes_work):
+            for n, ((a_re, a_im, _, _), sl) in enumerate(work):
                 inv, dinv, lift, base = prep[n]
-                if sweep > 0:
+                if sweep == 0:
+                    rzr, rzi = ld(spec_ref, 0, sl), ld(spec_ref, 1, sl)
+                    rdr, rdi = ld(spec_ref, 2, sl), ld(spec_ref, 3, sl)
+                else:
                     zr, zi, dr, di, _, _ = state[n]
-                    nzr, nzi, ndr, ndi = near(zr, sl), near(zi, sl), near(dr, sl), near(di, sl)
-                zr, zi, dr, di, hr, hi = [], [], [], [], [], []
-                for p in range(2):
-                    if sweep == 0:
-                        rzr, rzi = ld(spec_ref, 0, p, sl), ld(spec_ref, 1, p, sl)
-                        rdr, rdi = ld(spec_ref, 2, p, sl), ld(spec_ref, 3, p, sl)
-                    else:
-                        rzr = ld(spec_ref, 0, p, sl) - ndr[p]
-                        rzi = ld(spec_ref, 1, p, sl) - ndi[p]
-                        rdr = ld(spec_ref, 2, p, sl) + nzr[p]
-                        rdi = ld(spec_ref, 3, p, sl) + nzi[p]
-                    z_re, z_im = cmul(rzr, rzi, inv[p][0], inv[p][1])
-                    zr.append(z_re)
-                    zi.append(z_im)
-                    d_re, d_im = cmul(lift[p][0], lift[p][1], rdr, rdi)
-                    dr.append(d_re + base[p][0])
-                    di.append(d_im + base[p][1])
-                    if sweep == SWEEPS - 1:
-                        grav = ld(coef_ref, 3, p, sl)
-                        b_im = a_im + ld(coef_ref, 2, p, sl)
-                        h0r = ld(spec_ref, 4, p, sl)
-                        h0i = ld(spec_ref, 5, p, sl)
-                        nh_re = a_re * h0r - b_im * h0i - grav * rdr
-                        nh_im = a_re * h0i + b_im * h0r - grav * rdi
-                        h_re, h_im = cmul(nh_re, nh_im, dinv[p][0], dinv[p][1])
-                        hr.append(h_re)
-                        hi.append(h_im)
+                    rzr = ld(spec_ref, 0, sl) - near(dr, sl)
+                    rzi = ld(spec_ref, 1, sl) - near(di, sl)
+                    rdr = ld(spec_ref, 2, sl) + near(zr, sl)
+                    rdi = ld(spec_ref, 3, sl) + near(zi, sl)
+                zr, zi = cmul(rzr, rzi, inv[0], inv[1])
+                d_re, d_im = cmul(lift[0], lift[1], rdr, rdi)
+                dr, di = d_re + base[0], d_im + base[1]
+                hr = hi = None
+                if sweep == SWEEPS - 1:
+                    grav = ld(coef_ref, 3, sl)
+                    b_im = a_im + ld(coef_ref, 2, sl)
+                    h0r = ld(spec_ref, 4, sl)
+                    h0i = ld(spec_ref, 5, sl)
+                    nh_re = a_re * h0r - b_im * h0i - grav * rdr
+                    nh_im = a_re * h0i + b_im * h0r - grav * rdi
+                    hr, hi = cmul(nh_re, nh_im, dinv[0], dinv[1])
                 state[n] = (zr, zi, dr, di, hr, hi)
-        for n, ((_, _, w_re, w_im), sl) in enumerate(lanes_work):
+        for n, ((_, _, w_re, w_im), sl) in enumerate(work):
             zr, zi, dr, di, hr, hi = state[n]
             for field, (f_re, f_im) in enumerate(((zr, zi), (dr, di), (hr, hi))):
-                for p in range(2):
-                    o_re, o_im = cmul(w_re, w_im, f_re[p], f_im[p])
-                    out_ref[2 * field, p, sl, :] += o_re[:, :width]
-                    out_ref[2 * field + 1, p, sl, :] += o_im[:, :width]
+                o_re, o_im = cmul(w_re, w_im, f_re, f_im)
+                out_ref[2 * field, sl, :] += o_re[:, :width]
+                out_ref[2 * field + 1, sl, :] += o_im[:, :width]
         return carry
 
     lax.fori_loop(0, npoles // INTERLEAVE, pole_step, 0)
 
 
 def solve_poles(poles, wide, coef, width):
-    _, parities, rows, _ = wide.shape
+    _, rows, _ = wide.shape
     return pl.pallas_call(
         pole_kernel,
-        out_shape=jax.ShapeDtypeStruct((6, parities, rows, width), jnp.float32),
+        out_shape=jax.ShapeDtypeStruct((6, rows, width), jnp.float32),
         in_specs=[
             pl.BlockSpec(memory_space=pltpu.SMEM),
             pl.BlockSpec(memory_space=pltpu.VMEM),
@@ -231,7 +217,7 @@
     own_waves = lax.dynamic_slice_in_dim(wave_table, lax.axis_index("wave") * slots, slots).astype(
         jnp.float32
     )
-    coef_all = coefficients(own_waves, pole_pos * local_k, local_k, local_k * pole_count)
+    coef_all = coefficients(own_waves, pole_pos * 2 * local_k, 2 * local_k, 2 * local_k * pole_count)
     coef_all = jnp.concatenate([coriolis_step * coef_all[:2], coef_all[2:]], axis=0)
     poles = jnp.take(pole_table, pole_index, axis=1)
     onehot = (wave_table[:, None] == jnp.arange(waves, dtype=jnp.int32)[None, :]).astype(jnp.float32)
@@ -252,13 +238,20 @@
         leg = leg_blocks[g * group : (g + 1) * group]
         products = jnp.einsum("mpwlk,pwmcl->cpmk", leg, both, preferred_element_type=jnp.float32)
         spectra = products[:comps] + products[comps:]
-        left_halo = lax.ppermute(spectra[..., local_k - HALO :], "pole", rightward)
-        right_halo = lax.ppermute(spectra[..., :HALO], "pole", leftward)
-        gap = jnp.zeros(spectra.shape[:3] + (RING - local_k - 2 * HALO,), jnp.float32)
-        wide = jnp.concatenate([spectra, right_halo, gap, left_halo], axis=3)
-        coef = coef_all[:, :, g * group : (g + 1) * group]
+        left_halo = lax.ppermute(spectra[..., local_k - HALO_K :], "pole", rightward)
+        right_halo = lax.ppermute(spectra[..., :HALO_K], "pole", leftward)
+
+        def interleave(x):
+            return jnp.moveaxis(x, 1, -1).reshape(x.shape[0], x.shape[2], -1)
+
+        gap = jnp.zeros((comps, group, RING - 2 * local_k - 2 * HALO), jnp.float32)
+        wide = jnp.concatenate(
+            [interleave(spectra), interleave(right_halo), gap, interleave(left_halo)], axis=2
+        )
+        coef = coef_all[:, g * group : (g + 1) * group]
         wide = jnp.concatenate([wide, coef[3][None] * wide[4:6]], axis=0)
-        outs.append(solve_poles(poles, wide, coef, local_k))
+        flat = solve_poles(poles, wide, coef, 2 * local_k)
+        outs.append(jnp.moveaxis(flat.reshape(comps, group, local_k, 2), 3, 1))
     return jnp.concatenate(outs, axis=2)
 
 

time: 65.8 us -> 69.7 us (1.059)
  local copies, waits for them, and re-layouts: 4.18 us -> 7.29 us
  Pallas kernels: 12.6 us -> 13.9 us
    transpose x0 -> x4, local copies, waits for them, and re-layouts: none -> 1.64 us  [the longest x1 0.98 us: shards(): outs.append(jnp.moveaxis(flat.reshape(comps, group, local_k, 2), 3, 1))]
    pallas_call x1, Pallas kernels: 12.6 us -> 13.9 us  [solve_poles(): pl.pallas_call(pole_kernel, out_shape=jax.ShapeDtypeStruct((6, rows, widt...]
    pallas_call x0 -> x1, local copies, waits for them, and re-layouts: none -> 1.15 us  [solve_poles(): pl.pallas_call(pole_kernel, out_shape=jax.ShapeDtypeStruct((6, rows, widt...]
  transfers between devices with their start and end apart: 3 -> 3, of which waited for: 2 -> 3; matrix products, arithmetic and copies ran while one was open for 4% -> 5% of each run, Pallas kernels for 0% -> 0%
where the time goes in v8:
time: 69.7 us; the launch traced here: 69.4 us
  waiting for transfers between devices  22 us (32%)
  Pallas kernels  13.9 us (20%)
  starting transfers between devices  13.6 us (20%)
  matrix products  8.31 us (12%)
  local copies, waits for them, and re-layouts  7.29 us (10%)
  other arithmetic  4.09 us (6%)
    all_to_all x1, waiting for transfers between devices, shards(): lax.all_to_all(columns, 'wave', split_axis=0, concat_axis=0, tiled=True)  15.5 us
    pallas_call x1, Pallas kernels, solve_poles(): pl.pallas_call(pole_kernel, out_shape=jax.ShapeDtypeStruct((6, rows, widt...  13.9 us
    ppermute x1, waiting for transfers between devices, shards(): left_halo = lax.ppermute(spectra[..., local_k - HALO_K:], 'pole', rightward)  6.36 us
    all_to_all x1, starting transfers between devices, shards(): lax.all_to_all(columns, 'wave', split_axis=0, concat_axis=0, tiled=True)  5.93 us
    ppermute x1, starting transfers between devices, shards(): right_halo = lax.ppermute(spectra[..., :HALO_K], 'pole', leftward)  5.76 us
    dot_general x1, matrix products, shards(): jnp.einsum('mpwlk,pwmcl->cpmk', leg, both, preferred_element_type=jnp.flo...  5.71 us
    unnamed x1, matrix products  2.59 us
    ppermute x1, starting transfers between devices, shards(): left_halo = lax.ppermute(spectra[..., local_k - HALO_K:], 'pole', rightward)  1.92 us
  transfers between devices with their start and end apart: 3, of which 3 were waited for; matrix products, arithmetic and copies ran while one was open for 5% of the time, Pallas kernels for 0%

profile of v8, /device:TPU:6, one launch (start us, length us, event | category | flops | bytes accessed | tf_op | source)
XLA Modules:
  0.0 69.4 jit_solution(14615641091940875892)
XLA Ops:
  0.0 1.3 %copy-done = f32[6,256,192]{1,2,0:T(8,128)S(1)} copy-done((f32[6,256,192]{1,2,0:T(8,128)S(1)}, f32[6,256,192]{1,2,0:T(8,128)}, u32[]{:S(2)}) %copy-start) | copy-done | bytes 1179672
  1.3 2.6 %fusion.10 = f32[256,1152]{1,0:T(8,128)} fusion(f32[256,1152]{0,1:T(8,128)S(1)} %bitcast.24, s32[256]{0:T(256)} %param.7), kind=kOutput, calls=%fused_computation.13 | convolution fusion | flops 906035200 | bytes 2360320
  3.9 5.9 %all-to-all-start = ((f32[16,16,1152]{2,1,0:T(8,128)}), f32[16,16,1152]{2,1,0:T(8,128)S(1)}, u32[]{:S(2)}, u32[]{:S(2)}) async-start(f32[16,16,1152]{2,1,0:T(8,128)} %bitcast.19), calls=%async_computation | async-start | bytes 2359296 | tf_op jit(solution)/shard_map/all_to_all | solution.py:231
  10.1 0.6 gather_fusion
  10.9 0.6 pad_maximum_fusion.2.coef_ref
  11.5 0.6 select_bitcast_fusion.poles_ref
  12.2 15.5 %all-to-all-done = f32[16,16,1152]{2,1,0:T(8,128)S(1)} async-done(((f32[16,16,1152]{2,1,0:T(8,128)}), f32[16,16,1152]{2,1,0:T(8,128)S(1)}, u32[]{:S(2)}, u32[]{:S(2)}) %all-to-all-start) | async-done | bytes 1179680 | tf_op jit(solution)/shard_map/all_to_all | solution.py:231
  27.7 0.9 %slice_add_fusion = (f32[8,16,1152]{2,1,0:T(8,128)S(1)}, f32[8,16,1152]{2,1,0:T(8,128)}) fusion(f32[16,16,1152]{2,1,0:T(8,128)S(1)} %all-to-all-done), kind=kLoop, calls=%fused_computation.11 | loop fusion | flops 294912 | bytes 2359296 | tf_op jit(solution)/shard_map/add | solution.py:235
  28.6 0.4 add.195
  29.0 1.5 %sub.30 = f32[1,8,16,6,192]{4,3,2,1,0:T(8,128)S(1)} reshape(f32[8,16,1152]{2,1,0:T(8,128)} %get-tuple-element.8) | data formatting | bytes 1179648 | tf_op jit(solution)/shard_map/sub | solution.py:235
  30.5 0.3 pad_maximum_fusion
  30.9 0.5 subtract_convert_fusion
  31.4 5.7 %fusion.5 = f32[12,2,16,128]{3,0,2,1:T(8,128)S(1)} fusion(bf16[16,2,8,192,128]{4,3,2,1,0:T(8,128)(2,1)} %bitcast.31, bf16[2,8,16,6,192]{4,3,1,2,0:T(8,128)(2,1)S(1)} %subtract_convert_fusion, bf16[2,8,16,6,192]{4,3,1,2,0:T(8,128)(2,1)S(1)} %copy.37), kind=kOutput, calls=%fused_computation.9 | convolution fusion | flops 153354240 | bytes 13959168 | tf_op jit(solution)/shard_map/mpwlk,pwmcl->cpmk/dot_general | solution.py:239
  37.2 5.8 %collective-permute-start = (f32[6,2,16,4]{3,0,2,1:T(8,128)S(1)}, f32[6,2,16,4]{3,0,2,1:T(8,128)S(1)}, u32[]{:S(2)}, u32[]{:S(2)}) collective-permute-start(f32[6,2,16,4]{3,0,2,1:T(8,128)S(1)} %get-tuple-element.9), channel_id=1, source_target_pairs={{1,0},{2,1},{3,2},{4,3},{5,4},{6,5},{7,6},{9,8},{10,9},{11,10},{12... | collective-permute-start | bytes 9224 | tf_op jit(solution)/shard_map/ppermute | solution.py:242
  43.0 1.9 %collective-permute-start.1 = (f32[6,2,16,4]{3,0,2,1:T(8,128)S(1)}, f32[6,2,16,4]{3,0,2,1:T(8,128)S(1)}, u32[]{:S(2)}, u32[]{:S(2)}) collective-permute-start(f32[6,2,16,4]{3,0,2,1:T(8,128)S(1)} %get-tuple-element.10), channel_id=1, source_target_pairs={{0,1},{1,2},{2,3},{3,4},{4,5},{5,6},{6,7},{8,9},{9,10},{10,11},{11... | collective-permute-start | bytes 9224 | tf_op jit(solution)/shard_map/ppermute | solution.py:241
  44.9 0.4 copy.21
  45.3 0.2 copy.24
  45.6 0.2 copy.22
  45.9 6.4 %collective-permute-done.1 = f32[6,2,16,4]{3,0,2,1:T(8,128)S(1)} collective-permute-done((f32[6,2,16,4]{3,0,2,1:T(8,128)S(1)}, f32[6,2,16,4]{3,0,2,1:T(8,128)S(1)}, u32[]{:S(2)}, u32[]{:S(2)}) %collective-permute-start.1) | collective-permute-done | bytes 3104 | tf_op jit(solution)/shard_map/ppermute | solution.py:241
  52.2 0.2 copy.23
  52.6 0.8 %pad_maximum_fusion.1.spec_ref = f32[8,16,384]{2,1,0:T(8,128)} fusion(f32[2,16,384]{2,1,0:T(8,128)S(1)} %fusion.12, f32[6,16,8]{2,1,0:T(8,128)S(1)} %copy.26, f32[6,16,112]{2,1,0:T(8,128)S(1)} %broadcast_in_dim.42, f32[6,16,8]{2,1,0:T(8,128)S(1)} %copy.25, f32[6,16,256]{2,1,0:T(8,128)S(1)} %copy.24), kind=kLoop, calls=%fused_computation.14 | loop fusion | flops 196608 | bytes 393216 | tf_op jit(solution)/shard_map/concatenate | solution.py:252
  53.3 13.9 %shard_map.55 = f32[6,16,256]{2,1,0:T(8,128)} custom-call(f32[4,32]{1,0:T(4,128)} %select_bitcast_fusion.poles_ref, f32[8,16,384]{2,1,0:T(8,128)} %pad_maximum_fusion.1.spec_ref, f32[4,16,384]{2,1,0:T(8,128)} %pad_maximum_fusion.2.coef_ref), custom_call_target="tpu_custom_call" | custom-call | tf_op jit(solution)/shard_map/pallas_call | solution.py:126
  67.2 1.2 %copy.27 = f32[6,16,256]{1,2,0:T(8,128)S(1)} copy(f32[6,16,256]{2,1,0:T(8,128)} %shard_map.55) | data formatting | bytes 196608 | tf_op jit(solution)/shard_map/pallas_call | solution.py:126
  68.4 1.0 %copy.28 = f32[6,2,16,128]{3,2,1,0:T(8,128)} copy(f32[6,2,16,128]{2,1,3,0:T(2,128)S(1)} %bitcast.26) | data formatting | bytes 196608 | tf_op jit(solution)/shard_map/transpose | solution.py:254
  (29 shorter events, 1.1 us)
Async XLA Ops:
  0.0 1.3 %copy-start = (f32[6,256,192]{1,2,0:T(8,128)S(1)}, f32[6,256,192]{1,2,0:T(8,128)}, u32[]{:S(2)}) copy-start(f32[6,256,192]{1,2,0:T(8,128)} %param.5) | copy-start | bytes 3538948
  1.3 8.6 %copy-start.1 = (s32[256]{0:T(256)S(1)}, s32[256]{0:T(256)}, u32[]{:S(2)}) copy-start(s32[256]{0:T(256)} %param.7) | copy-start | bytes 3076
  1.3 8.7 %copy-start.2 = (f32[4,64]{1,0:T(4,128)S(1)}, f32[4,64]{1,0:T(4,128)}, u32[]{:S(2)}) copy-start(f32[4,64]{1,0:T(4,128)} %param.8) | copy-start | bytes 3076
  1.3 8.8 %copy-start.3 = (s32[32]{0:T(128)S(1)}, s32[32]{0:T(128)}, u32[]{:S(2)}) copy-start(s32[32]{0:T(128)} %param.9) | copy-start | bytes 388
  3.9 23.8 %all-to-all-start = ((f32[16,16,1152]{2,1,0:T(8,128)}), f32[16,16,1152]{2,1,0:T(8,128)S(1)}, u32[]{:S(2)}, u32[]{:S(2)}) async-start(f32[16,16,1152]{2,1,0:T(8,128)} %bitcast.19), calls=%async_computation | async-start | bytes 2359296 | tf_op jit(solution)/shard_map/all_to_all | solution.py:231
  37.2 8.4 %collective-permute-start = (f32[6,2,16,4]{3,0,2,1:T(8,128)S(1)}, f32[6,2,16,4]{3,0,2,1:T(8,128)S(1)}, u32[]{:S(2)}, u32[]{:S(2)}) collective-permute-start(f32[6,2,16,4]{3,0,2,1:T(8,128)S(1)} %get-tuple-element.9), channel_id=1, source_target_pairs={{1,0},{2,1},{3,2},{4,3},{5,4},{6,5},{7,6},{9,8},{10,9},{11,10},{12... | collective-permute-start | bytes 9224 | tf_op jit(solution)/shard_map/ppermute | solution.py:242
  43.0 9.3 %collective-permute-start.1 = (f32[6,2,16,4]{3,0,2,1:T(8,128)S(1)}, f32[6,2,16,4]{3,0,2,1:T(8,128)S(1)}, u32[]{:S(2)}, u32[]{:S(2)}) collective-permute-start(f32[6,2,16,4]{3,0,2,1:T(8,128)S(1)} %get-tuple-element.10), channel_id=1, source_target_pairs={{0,1},{1,2},{2,3},{3,4},{4,5},{5,6},{6,7},{8,9},{9,10},{10,11},{11... | collective-permute-start | bytes 9224 | tf_op jit(solution)/shard_map/ppermute | solution.py:241

commit v9 on v4

--- a/solution.py
+++ b/solution.py
@@ -250,8 +250,8 @@
         high, low = split_high(parts)
         both = jnp.concatenate([high, low], axis=3)
         leg = leg_blocks[g * group : (g + 1) * group]
-        products = jnp.einsum("mpwlk,pwmcl->cpmk", leg, both, preferred_element_type=jnp.float32)
-        spectra = products[:comps] + products[comps:]
+        products = jnp.einsum("mpwlk,pwmcl->mpkc", leg, both, preferred_element_type=jnp.float32)
+        spectra = jnp.transpose(products[..., :comps] + products[..., comps:], (3, 1, 0, 2))
         left_halo = lax.ppermute(spectra[..., local_k - HALO :], "pole", rightward)
         right_halo = lax.ppermute(spectra[..., :HALO], "pole", leftward)
         gap = jnp.zeros(spectra.shape[:3] + (RING - local_k - 2 * HALO,), jnp.float32)

time: 65.8 us -> 66.7 us (1.014)
  matrix products: 8.31 us -> 9.19 us
    dot_general x1, matrix products: 5.71 us -> 6.6 us  [shards(): jnp.einsum('mpwlk,pwmcl->mpkc', leg, both, preferred_element_type=jnp.flo...]
where the time goes in v9:
time: 66.7 us; the launch traced here: 66.3 us
  waiting for transfers between devices  22.3 us (33%)
  starting transfers between devices  13.6 us (20%)
  Pallas kernels  12.6 us (19%)
  matrix products  9.19 us (14%)
  other arithmetic  4.25 us (6%)
  local copies, waits for them, and re-layouts  4.24 us (6%)
    all_to_all x1, waiting for transfers between devices, shards(): lax.all_to_all(columns, 'wave', split_axis=0, concat_axis=0, tiled=True)  16 us
    pallas_call x1, Pallas kernels, solve_poles(): pl.pallas_call(pole_kernel, out_shape=jax.ShapeDtypeStruct((6, parities,...  12.6 us
    dot_general x1, matrix products, shards(): jnp.einsum('mpwlk,pwmcl->mpkc', leg, both, preferred_element_type=jnp.flo...  6.6 us
    ppermute x1, waiting for transfers between devices, shards(): left_halo = lax.ppermute(spectra[..., local_k - HALO:], 'pole', rightward)  6.31 us
    all_to_all x1, starting transfers between devices, shards(): lax.all_to_all(columns, 'wave', split_axis=0, concat_axis=0, tiled=True)  5.93 us
    ppermute x1, starting transfers between devices, shards(): right_halo = lax.ppermute(spectra[..., :HALO], 'pole', leftward)  5.76 us
    unnamed x1, matrix products  2.59 us
    ppermute x1, starting transfers between devices, shards(): left_halo = lax.ppermute(spectra[..., local_k - HALO:], 'pole', rightward)  1.92 us
  transfers between devices with their start and end apart: 3, of which 2 were waited for; matrix products, arithmetic and copies ran while one was open for 4% of the time, Pallas kernels for 0%

profile of v9, /device:TPU:6, one launch (start us, length us, event | category | flops | bytes accessed | tf_op | source)
XLA Modules:
  0.0 66.3 jit_solution(9465431223174886098)
XLA Ops:
  0.0 1.3 %copy-done = f32[6,256,192]{1,2,0:T(8,128)S(1)} copy-done((f32[6,256,192]{1,2,0:T(8,128)S(1)}, f32[6,256,192]{1,2,0:T(8,128)}, u32[]{:S(2)}) %copy-start) | copy-done | bytes 1179672
  1.3 2.6 %fusion.7 = f32[256,1152]{1,0:T(8,128)} fusion(f32[256,1152]{0,1:T(8,128)S(1)} %bitcast.18, s32[256]{0:T(256)} %param.7), kind=kOutput, calls=%fused_computation.13 | convolution fusion | flops 906035200 | bytes 2360320
  3.9 5.9 %all-to-all-start = ((f32[16,16,1152]{2,1,0:T(8,128)}), f32[16,16,1152]{2,1,0:T(8,128)S(1)}, u32[]{:S(2)}, u32[]{:S(2)}) async-start(f32[16,16,1152]{2,1,0:T(8,128)} %bitcast.10), calls=%async_computation | async-start | bytes 2359296 | tf_op jit(solution)/shard_map/all_to_all | solution.py:245
  10.1 0.1 copy.11
  10.2 0.6 gather_fusion
  10.9 0.1 fusion.28
  11.0 0.6 select_bitcast_fusion.poles_ref
  11.7 16.0 %all-to-all-done = f32[16,16,1152]{2,1,0:T(8,128)S(1)} async-done(((f32[16,16,1152]{2,1,0:T(8,128)}), f32[16,16,1152]{2,1,0:T(8,128)S(1)}, u32[]{:S(2)}, u32[]{:S(2)}) %all-to-all-start) | async-done | bytes 1179680 | tf_op jit(solution)/shard_map/all_to_all | solution.py:245
  27.7 0.9 %slice_add_fusion = (f32[8,16,1152]{2,1,0:T(8,128)S(1)}, f32[8,16,1152]{2,1,0:T(8,128)}) fusion(f32[16,16,1152]{2,1,0:T(8,128)S(1)} %all-to-all-done), kind=kLoop, calls=%fused_computation.10 | loop fusion | flops 294912 | bytes 2359296 | tf_op jit(solution)/shard_map/add | solution.py:249
  28.6 0.4 add.193
  29.0 1.5 %sub.27 = f32[1,8,16,6,192]{4,3,2,1,0:T(8,128)S(1)} reshape(f32[8,16,1152]{2,1,0:T(8,128)} %get-tuple-element.8) | data formatting | bytes 1179648 | tf_op jit(solution)/shard_map/sub | solution.py:249
  30.5 0.2 pad_maximum_fusion
  30.7 0.1 copy.22
  30.8 0.4 subtract_convert_fusion
  31.3 6.6 %fusion.4 = f32[16,2,12,128]{3,2,1,0:T(8,128)S(1)} fusion(bf16[16,2,8,192,128]{4,3,2,1,0:T(8,128)(2,1)} %bitcast.19, bf16[2,8,16,6,192]{4,3,1,0,2:T(8,128)(2,1)S(1)} %subtract_convert_fusion, bf16[2,8,16,6,192]{4,3,1,0,2:T(8,128)(2,1)S(1)} %copy.22), kind=kOutput, calls=%fused_computation.8 | convolution fusion | flops 153354240 | bytes 13959168 | tf_op jit(solution)/shard_map/mpwlk,pwmcl->mpkc/dot_general | solution.py:253
  37.9 0.1 copy.23
  38.1 0.1 fusion.30
  38.1 5.8 %collective-permute-start = (f32[6,2,16,8]{3,2,1,0:T(8,128)S(1)}, f32[6,2,16,8]{3,2,1,0:T(8,128)S(1)}, u32[]{:S(2)}, u32[]{:S(2)}) collective-permute-start(f32[6,2,16,8]{3,2,1,0:T(8,128)S(1)} %get-tuple-element.9), channel_id=1, source_target_pairs={{1,0},{2,1},{3,2},{4,3},{5,4},{6,5},{7,6},{9,8},{10,9},{11,10},{12... | collective-permute-start | bytes 18440 | tf_op jit(solution)/shard_map/ppermute | solution.py:256
  43.9 1.9 %collective-permute-start.1 = (f32[6,2,16,8]{3,2,1,0:T(8,128)S(1)}, f32[6,2,16,8]{3,2,1,0:T(8,128)S(1)}, u32[]{:S(2)}, u32[]{:S(2)}) collective-permute-start(f32[6,2,16,8]{3,2,1,0:T(8,128)S(1)} %get-tuple-element.10), channel_id=1, source_target_pairs={{0,1},{1,2},{2,3},{3,4},{4,5},{5,6},{6,7},{8,9},{9,10},{10,11},{11... | collective-permute-start | bytes 18440 | tf_op jit(solution)/shard_map/ppermute | solution.py:255
  45.8 0.7 %pad_maximum_fusion.2.coef_ref = f32[4,2,16,256]{3,2,1,0:T(8,128)} fusion(f32[1,2,16,256]{3,2,1,0:T(8,128)S(1)} %get-tuple-element.13, f32[1,2,16,256]{3,2,1,0:T(8,128)S(1)} %get-tuple-element.14, f32[2,2,16,256]{3,2,1,0:T(8,128)S(1)} %maximum_multiply_fusion), kind=kLoop, calls=%fused_computation.15 | loop fusion | flops 65536 | bytes 262144 | tf_op jit(solution)/shard_map/concatenate | solution.py:235
  46.5 6.3 %collective-permute-done.1 = f32[6,2,16,8]{3,2,1,0:T(8,128)S(1)} collective-permute-done((f32[6,2,16,8]{3,2,1,0:T(8,128)S(1)}, f32[6,2,16,8]{3,2,1,0:T(8,128)S(1)}, u32[]{:S(2)}, u32[]{:S(2)}) %collective-permute-start.1) | collective-permute-done | bytes 6176 | tf_op jit(solution)/shard_map/ppermute | solution.py:255
  52.8 0.1 fusion.10
  52.9 0.8 %pad_maximum_fusion.1.spec_ref = f32[8,2,16,256]{3,2,1,0:T(8,128)} fusion(f32[2,2,16,256]{3,2,1,0:T(8,128)S(1)} %fusion.10, f32[6,2,16,8]{3,2,1,0:T(8,128)S(1)} %collective-permute-done.1, f32[6,2,16,112]{3,2,1,0:T(8,128)S(1)} %broadcast_in_dim.48, f32[6,2,16,8]{3,2,1,0:T(8,128)S(1)} %collective-permute-done, f32[6,2,16,128]{3,2,1,0:T(8,128)S(1)} %fusion.9), kind=kLoop, calls=%fused_computation.11 | loop fusion | flops 262144 | bytes 524288 | tf_op jit(solution)/shard_map/concatenate | solution.py:260
  53.8 12.6 %shard_map.55 = f32[6,2,16,128]{3,2,1,0:T(8,128)} custom-call(f32[4,32]{1,0:T(4,128)} %select_bitcast_fusion.poles_ref, f32[8,2,16,256]{3,2,1,0:T(8,128)} %pad_maximum_fusion.1.spec_ref, f32[4,2,16,256]{3,2,1,0:T(8,128)} %pad_maximum_fusion.2.coef_ref), custom_call_target="tpu_custom_call" | custom-call | tf_op jit(solution)/shard_map/pallas_call | solution.py:140
  (23 shorter events, 0.5 us)
Async XLA Ops:
  0.0 1.3 %copy-start = (f32[6,256,192]{1,2,0:T(8,128)S(1)}, f32[6,256,192]{1,2,0:T(8,128)}, u32[]{:S(2)}) copy-start(f32[6,256,192]{1,2,0:T(8,128)} %param.5) | copy-start | bytes 3538948
  1.3 8.6 %copy-start.1 = (s32[256]{0:T(256)S(1)}, s32[256]{0:T(256)}, u32[]{:S(2)}) copy-start(s32[256]{0:T(256)} %param.7) | copy-start | bytes 3076
  1.3 8.8 %copy-start.2 = (f32[4,64]{1,0:T(4,128)S(1)}, f32[4,64]{1,0:T(4,128)}, u32[]{:S(2)}) copy-start(f32[4,64]{1,0:T(4,128)} %param.8) | copy-start | bytes 3076
  1.3 8.9 %copy-start.3 = (s32[32]{0:T(128)S(1)}, s32[32]{0:T(128)}, u32[]{:S(2)}) copy-start(s32[32]{0:T(128)} %param.9) | copy-start | bytes 388
  3.9 23.8 %all-to-all-start = ((f32[16,16,1152]{2,1,0:T(8,128)}), f32[16,16,1152]{2,1,0:T(8,128)S(1)}, u32[]{:S(2)}, u32[]{:S(2)}) async-start(f32[16,16,1152]{2,1,0:T(8,128)} %bitcast.10), calls=%async_computation | async-start | bytes 2359296 | tf_op jit(solution)/shard_map/all_to_all | solution.py:245
  38.1 8.4 %collective-permute-start = (f32[6,2,16,8]{3,2,1,0:T(8,128)S(1)}, f32[6,2,16,8]{3,2,1,0:T(8,128)S(1)}, u32[]{:S(2)}, u32[]{:S(2)}) collective-permute-start(f32[6,2,16,8]{3,2,1,0:T(8,128)S(1)} %get-tuple-element.9), channel_id=1, source_target_pairs={{1,0},{2,1},{3,2},{4,3},{5,4},{6,5},{7,6},{9,8},{10,9},{11,10},{12... | collective-permute-start | bytes 18440 | tf_op jit(solution)/shard_map/ppermute | solution.py:256
  43.9 8.9 %collective-permute-start.1 = (f32[6,2,16,8]{3,2,1,0:T(8,128)S(1)}, f32[6,2,16,8]{3,2,1,0:T(8,128)S(1)}, u32[]{:S(2)}, u32[]{:S(2)}) collective-permute-start(f32[6,2,16,8]{3,2,1,0:T(8,128)S(1)} %get-tuple-element.10), channel_id=1, source_target_pairs={{0,1},{1,2},{2,3},{3,4},{4,5},{5,6},{6,7},{8,9},{9,10},{10,11},{11... | collective-permute-start | bytes 18440 | tf_op jit(solution)/shard_map/ppermute | solution.py:255

commit v10 on v4

--- a/solution.py
+++ b/solution.py
@@ -240,7 +240,7 @@
     outs = []
     for g in range(GROUPS):
         pick = onehot[:, g].reshape(wave_count * group, waves)
-        columns = jnp.einsum("sm,cml->scl", pick, grid, precision=lax.Precision.HIGHEST)
+        columns = jnp.einsum("sm,cml->scl", pick, grid, precision=lax.Precision.HIGH)
         columns = columns.reshape(wave_count * group, comps * lat_rows)
         regrouped = lax.all_to_all(columns, "wave", split_axis=0, concat_axis=0, tiled=True)
         regrouped = regrouped.reshape(wave_count, group, comps, lat_rows)

time: 65.8 us -> 65.5 us (level)
  no operation moved by 1% of the time
where the time goes in v10:
time: 65.5 us; the launch traced here: 65.2 us
  waiting for transfers between devices  22.3 us (34%)
  starting transfers between devices  13.6 us (21%)
  Pallas kernels  12.6 us (19%)
  matrix products  8.04 us (12%)
  other arithmetic  4.28 us (7%)
  local copies, waits for them, and re-layouts  4.18 us (6%)
    all_to_all x1, waiting for transfers between devices, shards(): lax.all_to_all(columns, 'wave', split_axis=0, concat_axis=0, tiled=True)  16 us
    pallas_call x1, Pallas kernels, solve_poles(): pl.pallas_call(pole_kernel, out_shape=jax.ShapeDtypeStruct((6, parities,...  12.6 us
    ppermute x1, waiting for transfers between devices, shards(): left_halo = lax.ppermute(spectra[..., local_k - HALO:], 'pole', rightward)  6.31 us
    all_to_all x1, starting transfers between devices, shards(): lax.all_to_all(columns, 'wave', split_axis=0, concat_axis=0, tiled=True)  5.93 us
    ppermute x1, starting transfers between devices, shards(): right_halo = lax.ppermute(spectra[..., :HALO], 'pole', leftward)  5.76 us
    dot_general x1, matrix products, shards(): jnp.einsum('mpwlk,pwmcl->cpmk', leg, both, preferred_element_type=jnp.flo...  5.71 us
    unnamed x1, matrix products  2.33 us
    ppermute x1, starting transfers between devices, shards(): left_halo = lax.ppermute(spectra[..., local_k - HALO:], 'pole', rightward)  1.92 us
  transfers between devices with their start and end apart: 3, of which 2 were waited for; matrix products, arithmetic and copies ran while one was open for 4% of the time, Pallas kernels for 0%

profile of v10, /device:TPU:6, one launch (start us, length us, event | category | flops | bytes accessed | tf_op | source)
XLA Modules:
  0.0 65.2 jit_solution(5341577929186247497)
XLA Ops:
  0.0 1.3 %copy-done = f32[6,256,192]{1,2,0:T(8,128)S(1)} copy-done((f32[6,256,192]{1,2,0:T(8,128)S(1)}, f32[6,256,192]{1,2,0:T(8,128)}, u32[]{:S(2)}) %copy-start) | copy-done | bytes 1179672
  1.3 2.3 %fusion.10 = f32[256,1152]{1,0:T(8,128)} fusion(f32[256,1152]{0,1:T(8,128)S(1)} %bitcast.15, s32[256]{0:T(256)} %param.7), kind=kOutput, calls=%fused_computation.14 | convolution fusion | flops 453050368 | bytes 2360320
  3.6 5.9 %all-to-all-start = ((f32[16,16,1152]{2,1,0:T(8,128)}), f32[16,16,1152]{2,1,0:T(8,128)S(1)}, u32[]{:S(2)}, u32[]{:S(2)}) async-start(f32[16,16,1152]{2,1,0:T(8,128)} %bitcast.9), calls=%async_computation | async-start | bytes 2359296 | tf_op jit(solution)/shard_map/all_to_all | solution.py:245
  9.8 0.1 copy.12
  10.0 0.6 gather_fusion
  10.6 0.1 fusion.30
  10.8 0.6 select_bitcast_fusion.poles_ref
  11.4 0.1 fusion.20
  11.5 16.0 %all-to-all-done = f32[16,16,1152]{2,1,0:T(8,128)S(1)} async-done(((f32[16,16,1152]{2,1,0:T(8,128)}), f32[16,16,1152]{2,1,0:T(8,128)S(1)}, u32[]{:S(2)}, u32[]{:S(2)}) %all-to-all-start) | async-done | bytes 1179680 | tf_op jit(solution)/shard_map/all_to_all | solution.py:245
  27.4 0.9 %slice_add_fusion = (f32[8,16,1152]{2,1,0:T(8,128)S(1)}, f32[8,16,1152]{2,1,0:T(8,128)}) fusion(f32[16,16,1152]{2,1,0:T(8,128)S(1)} %all-to-all-done), kind=kLoop, calls=%fused_computation.11 | loop fusion | flops 294912 | bytes 2359296 | tf_op jit(solution)/shard_map/add | solution.py:249
  28.3 0.4 add.193
  28.7 1.5 %sub.27 = f32[1,8,16,6,192]{4,3,2,1,0:T(8,128)S(1)} reshape(f32[8,16,1152]{2,1,0:T(8,128)} %get-tuple-element.8) | data formatting | bytes 1179648 | tf_op jit(solution)/shard_map/sub | solution.py:249
  30.2 0.3 pad_maximum_fusion
  30.5 0.1 copy.28
  30.6 0.4 subtract_convert_fusion
  31.1 5.7 %fusion.5 = f32[2,16,12,128]{3,2,1,0:T(8,128)S(1)} fusion(bf16[16,2,8,192,128]{4,3,2,1,0:T(8,128)(2,1)} %bitcast.17, bf16[2,8,16,6,192]{4,3,1,2,0:T(8,128)(2,1)S(1)} %subtract_convert_fusion, bf16[2,8,16,6,192]{4,3,1,2,0:T(8,128)(2,1)S(1)} %copy.28), kind=kOutput, calls=%fused_computation.9 | convolution fusion | flops 153354240 | bytes 13959168 | tf_op jit(solution)/shard_map/mpwlk,pwmcl->cpmk/dot_general | solution.py:253
  36.9 0.1 fusion.32
  37.0 5.8 %collective-permute-start = (f32[6,2,16,8]{3,2,1,0:T(8,128)S(1)}, f32[6,2,16,8]{3,2,1,0:T(8,128)S(1)}, u32[]{:S(2)}, u32[]{:S(2)}) collective-permute-start(f32[6,2,16,8]{3,2,1,0:T(8,128)S(1)} %get-tuple-element.9), channel_id=1, source_target_pairs={{1,0},{2,1},{3,2},{4,3},{5,4},{6,5},{7,6},{9,8},{10,9},{11,10},{12... | collective-permute-start | bytes 18440 | tf_op jit(solution)/shard_map/ppermute | solution.py:256
  42.7 1.9 %collective-permute-start.1 = (f32[6,2,16,8]{3,2,1,0:T(8,128)S(1)}, f32[6,2,16,8]{3,2,1,0:T(8,128)S(1)}, u32[]{:S(2)}, u32[]{:S(2)}) collective-permute-start(f32[6,2,16,8]{3,2,1,0:T(8,128)S(1)} %get-tuple-element.10), channel_id=1, source_target_pairs={{0,1},{1,2},{2,3},{3,4},{4,5},{5,6},{6,7},{8,9},{9,10},{10,11},{11... | collective-permute-start | bytes 18440 | tf_op jit(solution)/shard_map/ppermute | solution.py:255
  44.7 0.7 %pad_maximum_fusion.2.coef_ref = f32[4,2,16,256]{3,2,1,0:T(8,128)} fusion(f32[1,2,16,256]{3,2,1,0:T(8,128)S(1)} %get-tuple-element.13, f32[1,2,16,256]{3,2,1,0:T(8,128)S(1)} %get-tuple-element.14, f32[2,2,16,256]{3,2,1,0:T(8,128)S(1)} %maximum_multiply_fusion), kind=kLoop, calls=%fused_computation.16 | loop fusion | flops 65536 | bytes 262144 | tf_op jit(solution)/shard_map/concatenate | solution.py:235
  45.3 6.3 %collective-permute-done.1 = f32[6,2,16,8]{3,2,1,0:T(8,128)S(1)} collective-permute-done((f32[6,2,16,8]{3,2,1,0:T(8,128)S(1)}, f32[6,2,16,8]{3,2,1,0:T(8,128)S(1)}, u32[]{:S(2)}, u32[]{:S(2)}) %collective-permute-start.1) | collective-permute-done | bytes 6176 | tf_op jit(solution)/shard_map/ppermute | solution.py:255
  51.7 0.1 fusion.12
  51.8 0.8 %pad_maximum_fusion.1.spec_ref = f32[8,2,16,256]{3,2,1,0:T(8,128)} fusion(f32[2,2,16,256]{3,2,1,0:T(8,128)S(1)} %fusion.12, f32[6,2,16,8]{3,2,1,0:T(8,128)S(1)} %collective-permute-done.1, f32[6,2,16,112]{3,2,1,0:T(8,128)S(1)} %broadcast_in_dim.48, f32[6,2,16,8]{3,2,1,0:T(8,128)S(1)} %collective-permute-done, f32[6,2,16,128]{3,2,1,0:T(8,128)S(1)} %slice_add_fusion.1), kind=kLoop, calls=%fused_computation.12 | loop fusion | flops 262144 | bytes 524288 | tf_op jit(solution)/shard_map/concatenate | solution.py:260
  52.6 12.6 %shard_map.55 = f32[6,2,16,128]{3,2,1,0:T(8,128)} custom-call(f32[4,32]{1,0:T(4,128)} %select_bitcast_fusion.poles_ref, f32[8,2,16,256]{3,2,1,0:T(8,128)} %pad_maximum_fusion.1.spec_ref, f32[4,2,16,256]{3,2,1,0:T(8,128)} %pad_maximum_fusion.2.coef_ref), custom_call_target="tpu_custom_call" | custom-call | tf_op jit(solution)/shard_map/pallas_call | solution.py:140
  (23 shorter events, 0.5 us)
Async XLA Ops:
  0.0 1.3 %copy-start = (f32[6,256,192]{1,2,0:T(8,128)S(1)}, f32[6,256,192]{1,2,0:T(8,128)}, u32[]{:S(2)}) copy-start(f32[6,256,192]{1,2,0:T(8,128)} %param.5) | copy-start | bytes 3538948
  1.3 8.3 %copy-start.1 = (s32[256]{0:T(256)S(1)}, s32[256]{0:T(256)}, u32[]{:S(2)}) copy-start(s32[256]{0:T(256)} %param.7) | copy-start | bytes 3076
  1.3 8.6 %copy-start.2 = (f32[4,64]{1,0:T(4,128)S(1)}, f32[4,64]{1,0:T(4,128)}, u32[]{:S(2)}) copy-start(f32[4,64]{1,0:T(4,128)} %param.8) | copy-start | bytes 3076
  1.3 8.7 %copy-start.3 = (s32[32]{0:T(128)S(1)}, s32[32]{0:T(128)}, u32[]{:S(2)}) copy-start(s32[32]{0:T(128)} %param.9) | copy-start | bytes 388
  3.6 23.8 %all-to-all-start = ((f32[16,16,1152]{2,1,0:T(8,128)}), f32[16,16,1152]{2,1,0:T(8,128)S(1)}, u32[]{:S(2)}, u32[]{:S(2)}) async-start(f32[16,16,1152]{2,1,0:T(8,128)} %bitcast.9), calls=%async_computation | async-start | bytes 2359296 | tf_op jit(solution)/shard_map/all_to_all | solution.py:245
  37.0 8.4 %collective-permute-start = (f32[6,2,16,8]{3,2,1,0:T(8,128)S(1)}, f32[6,2,16,8]{3,2,1,0:T(8,128)S(1)}, u32[]{:S(2)}, u32[]{:S(2)}) collective-permute-start(f32[6,2,16,8]{3,2,1,0:T(8,128)S(1)} %get-tuple-element.9), channel_id=1, source_target_pairs={{1,0},{2,1},{3,2},{4,3},{5,4},{6,5},{7,6},{9,8},{10,9},{11,10},{12... | collective-permute-start | bytes 18440 | tf_op jit(solution)/shard_map/ppermute | solution.py:256
  42.7 8.9 %collective-permute-start.1 = (f32[6,2,16,8]{3,2,1,0:T(8,128)S(1)}, f32[6,2,16,8]{3,2,1,0:T(8,128)S(1)}, u32[]{:S(2)}, u32[]{:S(2)}) collective-permute-start(f32[6,2,16,8]{3,2,1,0:T(8,128)S(1)} %get-tuple-element.10), channel_id=1, source_target_pairs={{0,1},{1,2},{2,3},{3,4},{4,5},{5,6},{6,7},{8,9},{9,10},{10,11},{11... | collective-permute-start | bytes 18440 | tf_op jit(solution)/shard_map/ppermute | solution.py:255

commit v11 on v4

--- a/solution.py
+++ b/solution.py
@@ -6,7 +6,7 @@
 from jax.sharding import PartitionSpec as P
 
 SWEEPS = 8
-HALO = 8
+HALO = 4
 RING = 256
 CHUNK = 8
 GROUPS = 1
@@ -226,8 +226,8 @@
     group = slots // GROUPS
     pole_count = lax.axis_size("pole")
     pole_pos = lax.axis_index("pole")
-    rightward = [(i, i + 1) for i in range(pole_count - 1)]
-    leftward = [(i + 1, i) for i in range(pole_count - 1)]
+    rightward = [(i, (i + 1) % pole_count) for i in range(pole_count)]
+    leftward = [((i + 1) % pole_count, i) for i in range(pole_count)]
     own_waves = lax.dynamic_slice_in_dim(wave_table, lax.axis_index("wave") * slots, slots).astype(
         jnp.float32
     )
@@ -254,6 +254,8 @@
         spectra = products[:comps] + products[comps:]
         left_halo = lax.ppermute(spectra[..., local_k - HALO :], "pole", rightward)
         right_halo = lax.ppermute(spectra[..., :HALO], "pole", leftward)
+        left_halo = jnp.where(pole_pos > 0, left_halo, 0.0)
+        right_halo = jnp.where(pole_pos < pole_count - 1, right_halo, 0.0)
         gap = jnp.zeros(spectra.shape[:3] + (RING - local_k - 2 * HALO,), jnp.float32)
         wide = jnp.concatenate([spectra, right_halo, gap, left_halo], axis=3)
         coef = coef_all[:, :, g * group : (g + 1) * group]

time: 65.8 us -> 61.7 us (0.938)
  starting transfers between devices: 13.6 us -> 10.4 us
  waiting for transfers between devices: 22.3 us -> 21.2 us
    ppermute x1, starting transfers between devices: 5.76 us -> 0.85 us  [shards(): right_halo = lax.ppermute(spectra[..., :HALO], 'pole', leftward)]
    ppermute x1, waiting for transfers between devices: 6.31 us -> 1.92 us  [shards(): left_halo = lax.ppermute(spectra[..., local_k - HALO:], 'pole', rightward)]
    ppermute x1, waiting for transfers between devices: 0.01 us -> 3.34 us  [shards(): right_halo = lax.ppermute(spectra[..., :HALO], 'pole', leftward)]
    ppermute x1, starting transfers between devices: 1.92 us -> 3.65 us  [shards(): left_halo = lax.ppermute(spectra[..., local_k - HALO:], 'pole', rightward)]
  transfers between devices with their start and end apart: 3 -> 3, of which waited for: 2 -> 3; matrix products, arithmetic and copies ran while one was open for 4% -> 4% of each run, Pallas kernels for 0% -> 0%
where the time goes in v11:
time: 61.7 us; the launch traced here: 61.2 us
  waiting for transfers between devices  21.2 us (34%)
  Pallas kernels  12.6 us (20%)
  starting transfers between devices  10.4 us (17%)
  matrix products  8.31 us (13%)
  other arithmetic  4.3 us (7%)
  local copies, waits for them, and re-layouts  4.18 us (7%)
    all_to_all x1, waiting for transfers between devices, shards(): lax.all_to_all(columns, 'wave', split_axis=0, concat_axis=0, tiled=True)  16 us
    pallas_call x1, Pallas kernels, solve_poles(): pl.pallas_call(pole_kernel, out_shape=jax.ShapeDtypeStruct((6, parities,...  12.6 us
    all_to_all x1, starting transfers between devices, shards(): lax.all_to_all(columns, 'wave', split_axis=0, concat_axis=0, tiled=True)  5.93 us
    dot_general x1, matrix products, shards(): jnp.einsum('mpwlk,pwmcl->cpmk', leg, both, preferred_element_type=jnp.flo...  5.71 us
    ppermute x1, starting transfers between devices, shards(): left_halo = lax.ppermute(spectra[..., local_k - HALO:], 'pole', rightward)  3.65 us
    ppermute x1, waiting for transfers between devices, shards(): right_halo = lax.ppermute(spectra[..., :HALO], 'pole', leftward)  3.34 us
    unnamed x1, matrix products  2.59 us
    ppermute x1, waiting for transfers between devices, shards(): left_halo = lax.ppermute(spectra[..., local_k - HALO:], 'pole', rightward)  1.92 us
  transfers between devices with their start and end apart: 3, of which 3 were waited for; matrix products, arithmetic and copies ran while one was open for 4% of the time, Pallas kernels for 0%

profile of v11, /device:TPU:6, one launch (start us, length us, event | category | flops | bytes accessed | tf_op | source)
XLA Modules:
  0.0 61.2 jit_solution(6643460116960440171)
XLA Ops:
  0.0 1.3 %copy-done = f32[6,256,192]{1,2,0:T(8,128)S(1)} copy-done((f32[6,256,192]{1,2,0:T(8,128)S(1)}, f32[6,256,192]{1,2,0:T(8,128)}, u32[]{:S(2)}) %copy-start) | copy-done | bytes 1179672
  1.3 2.6 %fusion.10 = f32[256,1152]{1,0:T(8,128)} fusion(f32[256,1152]{0,1:T(8,128)S(1)} %bitcast.15, s32[256]{0:T(256)} %param.7), kind=kOutput, calls=%fused_computation.14 | convolution fusion | flops 906035200 | bytes 2360320
  3.9 5.9 %all-to-all-start = ((f32[16,16,1152]{2,1,0:T(8,128)}), f32[16,16,1152]{2,1,0:T(8,128)S(1)}, u32[]{:S(2)}, u32[]{:S(2)}) async-start(f32[16,16,1152]{2,1,0:T(8,128)} %bitcast.9), calls=%async_computation | async-start | bytes 2359296 | tf_op jit(solution)/shard_map/all_to_all | solution.py:245
  10.1 0.1 copy.12
  10.2 0.6 gather_fusion
  10.9 0.1 fusion.30
  11.0 0.6 select_bitcast_fusion.poles_ref
  11.7 16.0 %all-to-all-done = f32[16,16,1152]{2,1,0:T(8,128)S(1)} async-done(((f32[16,16,1152]{2,1,0:T(8,128)}), f32[16,16,1152]{2,1,0:T(8,128)S(1)}, u32[]{:S(2)}, u32[]{:S(2)}) %all-to-all-start) | async-done | bytes 1179680 | tf_op jit(solution)/shard_map/all_to_all | solution.py:245
  27.7 0.9 %slice_add_fusion = (f32[8,16,1152]{2,1,0:T(8,128)S(1)}, f32[8,16,1152]{2,1,0:T(8,128)}) fusion(f32[16,16,1152]{2,1,0:T(8,128)S(1)} %all-to-all-done), kind=kLoop, calls=%fused_computation.11 | loop fusion | flops 294912 | bytes 2359296 | tf_op jit(solution)/shard_map/add | solution.py:249
  28.6 0.4 add.193
  29.0 1.5 %sub.27 = f32[1,8,16,6,192]{4,3,2,1,0:T(8,128)S(1)} reshape(f32[8,16,1152]{2,1,0:T(8,128)} %get-tuple-element.8) | data formatting | bytes 1179648 | tf_op jit(solution)/shard_map/sub | solution.py:249
  30.5 0.3 pad_maximum_fusion
  30.7 0.1 copy.28
  30.9 0.4 subtract_convert_fusion
  31.3 5.7 %fusion.5 = f32[2,16,12,128]{3,2,1,0:T(8,128)S(1)} fusion(bf16[16,2,8,192,128]{4,3,2,1,0:T(8,128)(2,1)} %bitcast.17, bf16[2,8,16,6,192]{4,3,1,2,0:T(8,128)(2,1)S(1)} %subtract_convert_fusion, bf16[2,8,16,6,192]{4,3,1,2,0:T(8,128)(2,1)S(1)} %copy.28), kind=kOutput, calls=%fused_computation.9 | convolution fusion | flops 153354240 | bytes 13959168 | tf_op jit(solution)/shard_map/mpwlk,pwmcl->cpmk/dot_general | solution.py:253
  37.1 0.1 fusion.32
  37.2 3.7 %collective-permute-start.1 = (f32[6,2,16,4]{3,2,1,0:T(8,128)S(1)}, f32[6,2,16,4]{3,2,1,0:T(8,128)S(1)}, u32[]{:S(2)}, u32[]{:S(2)}) collective-permute-start(f32[6,2,16,4]{3,2,1,0:T(8,128)S(1)} %get-tuple-element.10), channel_id=1, source_target_pairs={{0,1},{1,2},{2,3},{3,4},{4,5},{5,6},{6,7},{7,0},{8,9},{9,10},{10,1... | collective-permute-start | bytes 9224 | tf_op jit(solution)/shard_map/ppermute | solution.py:255
  40.9 0.7 %pad_maximum_fusion.2.coef_ref = f32[4,2,16,256]{3,2,1,0:T(8,128)} fusion(f32[1,2,16,256]{3,2,1,0:T(8,128)S(1)} %get-tuple-element.13, f32[1,2,16,256]{3,2,1,0:T(8,128)S(1)} %get-tuple-element.14, f32[2,2,16,256]{3,2,1,0:T(8,128)S(1)} %maximum_multiply_fusion), kind=kLoop, calls=%fused_computation.16 | loop fusion | flops 65536 | bytes 262144 | tf_op jit(solution)/shard_map/concatenate | solution.py:235
  41.6 0.8 %collective-permute-start = (f32[6,2,16,4]{3,2,1,0:T(8,128)S(1)}, f32[6,2,16,4]{3,2,1,0:T(8,128)S(1)}, u32[]{:S(2)}, u32[]{:S(2)}) collective-permute-start(f32[6,2,16,4]{3,2,1,0:T(8,128)S(1)} %get-tuple-element.9), channel_id=1, source_target_pairs={{1,0},{2,1},{3,2},{4,3},{5,4},{6,5},{7,6},{0,7},{9,8},{10,9},{11,1... | collective-permute-start | bytes 9224 | tf_op jit(solution)/shard_map/ppermute | solution.py:256
  42.4 1.9 %collective-permute-done.1 = f32[6,2,16,4]{3,2,1,0:T(8,128)S(1)} collective-permute-done((f32[6,2,16,4]{3,2,1,0:T(8,128)S(1)}, f32[6,2,16,4]{3,2,1,0:T(8,128)S(1)}, u32[]{:S(2)}, u32[]{:S(2)}) %collective-permute-start.1) | collective-permute-done | bytes 3104 | tf_op jit(solution)/shard_map/ppermute | solution.py:255
  44.3 3.3 %collective-permute-done = f32[6,2,16,4]{3,2,1,0:T(8,128)S(1)} collective-permute-done((f32[6,2,16,4]{3,2,1,0:T(8,128)S(1)}, f32[6,2,16,4]{3,2,1,0:T(8,128)S(1)}, u32[]{:S(2)}, u32[]{:S(2)}) %collective-permute-start) | collective-permute-done | bytes 3104 | tf_op jit(solution)/shard_map/ppermute | solution.py:256
  47.7 0.1 fusion.12
  47.8 0.8 %pad_maximum_fusion.1.spec_ref = f32[8,2,16,256]{3,2,1,0:T(8,128)} fusion(f32[2,2,16,256]{3,2,1,0:T(8,128)S(1)} %fusion.12, f32[6,2,16,4]{3,2,1,0:T(8,128)S(1)} %broadcast_select_fusion, f32[6,2,16,120]{3,2,1,0:T(8,128)S(1)} %broadcast_in_dim.54, f32[6,2,16,4]{3,2,1,0:T(8,128)S(1)} %broadcast_select_fusion.1, f32[6,2,16,128]{3,2,1,0:T(8,128)S(1)} %slice_add_fusion.1), kind=kLoop, calls=%fused_computation.12 | loop fusion | flops 262144 | bytes 524288 | tf_op jit(solution)/shard_map/concatenate | solution.py:262
  48.6 12.6 %shard_map.55 = f32[6,2,16,128]{3,2,1,0:T(8,128)} custom-call(f32[4,32]{1,0:T(4,128)} %select_bitcast_fusion.poles_ref, f32[8,2,16,256]{3,2,1,0:T(8,128)} %pad_maximum_fusion.1.spec_ref, f32[4,2,16,256]{3,2,1,0:T(8,128)} %pad_maximum_fusion.2.coef_ref), custom_call_target="tpu_custom_call" | custom-call | tf_op jit(solution)/shard_map/pallas_call | solution.py:140
  (25 shorter events, 0.6 us)
Async XLA Ops:
  0.0 1.3 %copy-start = (f32[6,256,192]{1,2,0:T(8,128)S(1)}, f32[6,256,192]{1,2,0:T(8,128)}, u32[]{:S(2)}) copy-start(f32[6,256,192]{1,2,0:T(8,128)} %param.5) | copy-start | bytes 3538948
  1.3 8.6 %copy-start.1 = (s32[256]{0:T(256)S(1)}, s32[256]{0:T(256)}, u32[]{:S(2)}) copy-start(s32[256]{0:T(256)} %param.7) | copy-start | bytes 3076
  1.3 8.8 %copy-start.2 = (f32[4,64]{1,0:T(4,128)S(1)}, f32[4,64]{1,0:T(4,128)}, u32[]{:S(2)}) copy-start(f32[4,64]{1,0:T(4,128)} %param.8) | copy-start | bytes 3076
  1.3 8.9 %copy-start.3 = (s32[32]{0:T(128)S(1)}, s32[32]{0:T(128)}, u32[]{:S(2)}) copy-start(s32[32]{0:T(128)} %param.9) | copy-start | bytes 388
  3.9 23.8 %all-to-all-start = ((f32[16,16,1152]{2,1,0:T(8,128)}), f32[16,16,1152]{2,1,0:T(8,128)S(1)}, u32[]{:S(2)}, u32[]{:S(2)}) async-start(f32[16,16,1152]{2,1,0:T(8,128)} %bitcast.9), calls=%async_computation | async-start | bytes 2359296 | tf_op jit(solution)/shard_map/all_to_all | solution.py:245
  37.2 7.1 %collective-permute-start.1 = (f32[6,2,16,4]{3,2,1,0:T(8,128)S(1)}, f32[6,2,16,4]{3,2,1,0:T(8,128)S(1)}, u32[]{:S(2)}, u32[]{:S(2)}) collective-permute-start(f32[6,2,16,4]{3,2,1,0:T(8,128)S(1)} %get-tuple-element.10), channel_id=1, source_target_pairs={{0,1},{1,2},{2,3},{3,4},{4,5},{5,6},{6,7},{7,0},{8,9},{9,10},{10,1... | collective-permute-start | bytes 9224 | tf_op jit(solution)/shard_map/ppermute | solution.py:255
  41.6 6.1 %collective-permute-start = (f32[6,2,16,4]{3,2,1,0:T(8,128)S(1)}, f32[6,2,16,4]{3,2,1,0:T(8,128)S(1)}, u32[]{:S(2)}, u32[]{:S(2)}) collective-permute-start(f32[6,2,16,4]{3,2,1,0:T(8,128)S(1)} %get-tuple-element.9), channel_id=1, source_target_pairs={{1,0},{2,1},{3,2},{4,3},{5,4},{6,5},{7,6},{0,7},{9,8},{10,9},{11,1... | collective-permute-start | bytes 9224 | tf_op jit(solution)/shard_map/ppermute | solution.py:256

commit v12 on v11

--- a/solution.py
+++ b/solution.py
@@ -243,12 +243,13 @@
         columns = jnp.einsum("sm,cml->scl", pick, grid, precision=lax.Precision.HIGHEST)
         columns = columns.reshape(wave_count * group, comps * lat_rows)
         regrouped = lax.all_to_all(columns, "wave", split_axis=0, concat_axis=0, tiled=True)
-        regrouped = regrouped.reshape(wave_count, group, comps, lat_rows)
+        regrouped = regrouped.reshape(wave_count, group, comps * lat_rows)
         north = regrouped[:half_count]
         south = regrouped[half_count:]
         parts = jnp.stack([north + south, north - south], axis=0)
         high, low = split_high(parts)
         both = jnp.concatenate([high, low], axis=3)
+        both = both.reshape(2, half_count, group, 2 * comps, lat_rows)
         leg = leg_blocks[g * group : (g + 1) * group]
         products = jnp.einsum("mpwlk,pwmcl->cpmk", leg, both, preferred_element_type=jnp.float32)
         spectra = products[:comps] + products[comps:]

time: 61.7 us -> 62.9 us (1.019)
  matrix products: 8.31 us -> 9.59 us
  other arithmetic: 4.3 us -> 3.1 us
  local copies, waits for them, and re-layouts: 4.18 us -> 5.2 us
    reshape x0 -> x1, local copies, waits for them, and re-layouts: none -> 3.01 us  [shards(): both = both.reshape(2, half_count, group, 2 * comps, lat_rows)]
    sub x1 -> x0, local copies, waits for them, and re-layouts: 1.46 us -> none  [shards(): parts = jnp.stack([north + south, north - south], axis=0)]
    dot_general x1, matrix products: 5.71 us -> 7.07 us  [shards(): jnp.einsum('mpwlk,pwmcl->cpmk', leg, both, preferred_element_type=jnp.flo...]
    add x1, other arithmetic: 0.9 us -> 0.08 us  [shards(): parts = jnp.stack([north + south, north - south], axis=0)]
where the time goes in v12:
time: 62.9 us; the launch traced here: 62.4 us
  waiting for transfers between devices  21.2 us (34%)
  Pallas kernels  12.6 us (20%)
  starting transfers between devices  10.6 us (17%)
  matrix products  9.59 us (15%)
  local copies, waits for them, and re-layouts  5.2 us (8%)
  other arithmetic  3.1 us (5%)
    all_to_all x1, waiting for transfers between devices, shards(): lax.all_to_all(columns, 'wave', split_axis=0, concat_axis=0, tiled=True)  16 us
    pallas_call x1, Pallas kernels, solve_poles(): pl.pallas_call(pole_kernel, out_shape=jax.ShapeDtypeStruct((6, parities,...  12.6 us
    dot_general x1, matrix products, shards(): jnp.einsum('mpwlk,pwmcl->cpmk', leg, both, preferred_element_type=jnp.flo...  7.07 us
    all_to_all x1, starting transfers between devices, shards(): lax.all_to_all(columns, 'wave', split_axis=0, concat_axis=0, tiled=True)  6.06 us
    ppermute x1, starting transfers between devices, shards(): left_halo = lax.ppermute(spectra[..., local_k - HALO:], 'pole', rightward)  3.65 us
    ppermute x1, waiting for transfers between devices, shards(): right_halo = lax.ppermute(spectra[..., :HALO], 'pole', leftward)  3.34 us
    reshape x1, local copies, waits for them, and re-layouts, shards(): both = both.reshape(2, half_count, group, 2 * comps, lat_rows)  3.01 us
    unnamed x1, matrix products  2.53 us
  transfers between devices with their start and end apart: 3, of which 3 were waited for; matrix products, arithmetic and copies ran while one was open for 4% of the time, Pallas kernels for 0%

profile of v12, /device:TPU:6, one launch (start us, length us, event | category | flops | bytes accessed | tf_op | source)
XLA Modules:
  0.0 62.4 jit_solution(8399852607748175259)
XLA Ops:
  0.0 1.3 %copy-done = f32[6,256,192]{1,2,0:T(8,128)S(1)} copy-done((f32[6,256,192]{1,2,0:T(8,128)S(1)}, f32[6,256,192]{1,2,0:T(8,128)}, u32[]{:S(2)}) %copy-start) | copy-done | bytes 1179672
  1.3 2.5 %fusion.9 = f32[256,1152]{1,0:T(8,128)} fusion(f32[256,1152]{0,1:T(8,128)S(1)} %bitcast.21, s32[256]{0:T(256)} %param.7), kind=kOutput, calls=%fused_computation.13 | convolution fusion | flops 906035200 | bytes 2360320
  3.8 6.1 %all-to-all-start = ((f32[16,16,1152]{2,1,0:T(8,128)}), f32[16,16,1152]{2,1,0:T(8,128)S(1)}, u32[]{:S(2)}, u32[]{:S(2)}) async-start(f32[16,16,1152]{2,1,0:T(8,128)} %bitcast.11), calls=%async_computation | async-start | bytes 2359296 | tf_op jit(solution)/shard_map/all_to_all | solution.py:245
  9.9 0.1 broadcast_multiply_fusion.1
  10.2 0.1 copy.11
  10.3 0.6 gather_fusion
  11.0 0.1 fusion.29
  11.1 0.6 select_bitcast_fusion.poles_ref
  11.7 0.1 fusion.19
  11.8 16.0 %all-to-all-done = f32[16,16,1152]{2,1,0:T(8,128)S(1)} async-done(((f32[16,16,1152]{2,1,0:T(8,128)}), f32[16,16,1152]{2,1,0:T(8,128)S(1)}, u32[]{:S(2)}, u32[]{:S(2)}) %all-to-all-start) | async-done | bytes 1179680 | tf_op jit(solution)/shard_map/all_to_all | solution.py:245
  27.8 0.1 fusion.8
  27.9 0.1 subtract_convert_fusion
  28.1 0.1 pad_maximum_fusion.1
  28.2 3.0 %reshape.211 = bf16[2,8,16,12,192]{4,3,2,1,0:T(8,128)(2,1)} reshape(bf16[2,8,16,2304]{3,2,1,0:T(8,128)(2,1)S(1)} %pad_maximum_fusion.1) | data formatting | bytes 2359296 | tf_op jit(solution)/shard_map/reshape | solution.py:252
  31.2 7.1 %fusion.3 = f32[2,16,12,128]{3,2,1,0:T(8,128)S(1)} fusion(bf16[16,2,8,192,128]{4,3,2,1,0:T(8,128)(2,1)} %bitcast.23, bf16[2,8,16,12,192]{4,3,2,1,0:T(8,128)(2,1)} %reshape.211), kind=kOutput, calls=%fused_computation.7 | convolution fusion | flops 150994944 | bytes 13959168 | tf_op jit(solution)/shard_map/mpwlk,pwmcl->cpmk/dot_general | solution.py:254
  38.4 0.1 fusion.30
  38.4 3.6 %collective-permute-start.1 = (f32[6,2,16,4]{3,2,1,0:T(8,128)S(1)}, f32[6,2,16,4]{3,2,1,0:T(8,128)S(1)}, u32[]{:S(2)}, u32[]{:S(2)}) collective-permute-start(f32[6,2,16,4]{3,2,1,0:T(8,128)S(1)} %get-tuple-element.10), channel_id=1, source_target_pairs={{0,1},{1,2},{2,3},{3,4},{4,5},{5,6},{6,7},{7,0},{8,9},{9,10},{10,1... | collective-permute-start | bytes 9224 | tf_op jit(solution)/shard_map/ppermute | solution.py:256
  42.1 0.7 %pad_maximum_fusion.3.coef_ref = f32[4,2,16,256]{3,2,1,0:T(8,128)} fusion(f32[1,2,16,256]{3,2,1,0:T(8,128)S(1)} %get-tuple-element.13, f32[1,2,16,256]{3,2,1,0:T(8,128)S(1)} %get-tuple-element.14, f32[2,2,16,256]{3,2,1,0:T(8,128)S(1)} %maximum_multiply_fusion), kind=kLoop, calls=%fused_computation.15 | loop fusion | flops 65536 | bytes 262144 | tf_op jit(solution)/shard_map/concatenate | solution.py:235
  42.8 0.9 %collective-permute-start = (f32[6,2,16,4]{3,2,1,0:T(8,128)S(1)}, f32[6,2,16,4]{3,2,1,0:T(8,128)S(1)}, u32[]{:S(2)}, u32[]{:S(2)}) collective-permute-start(f32[6,2,16,4]{3,2,1,0:T(8,128)S(1)} %get-tuple-element.9), channel_id=1, source_target_pairs={{1,0},{2,1},{3,2},{4,3},{5,4},{6,5},{7,6},{0,7},{9,8},{10,9},{11,1... | collective-permute-start | bytes 9224 | tf_op jit(solution)/shard_map/ppermute | solution.py:257
  43.6 1.9 %collective-permute-done.1 = f32[6,2,16,4]{3,2,1,0:T(8,128)S(1)} collective-permute-done((f32[6,2,16,4]{3,2,1,0:T(8,128)S(1)}, f32[6,2,16,4]{3,2,1,0:T(8,128)S(1)}, u32[]{:S(2)}, u32[]{:S(2)}) %collective-permute-start.1) | collective-permute-done | bytes 3104 | tf_op jit(solution)/shard_map/ppermute | solution.py:256
  45.5 3.3 %collective-permute-done = f32[6,2,16,4]{3,2,1,0:T(8,128)S(1)} collective-permute-done((f32[6,2,16,4]{3,2,1,0:T(8,128)S(1)}, f32[6,2,16,4]{3,2,1,0:T(8,128)S(1)}, u32[]{:S(2)}, u32[]{:S(2)}) %collective-permute-start) | collective-permute-done | bytes 3104 | tf_op jit(solution)/shard_map/ppermute | solution.py:257
  48.9 0.1 fusion.11
  49.0 0.8 %pad_maximum_fusion.2.spec_ref = f32[8,2,16,256]{3,2,1,0:T(8,128)} fusion(f32[2,2,16,256]{3,2,1,0:T(8,128)S(1)} %fusion.11, f32[6,2,16,4]{3,2,1,0:T(8,128)S(1)} %broadcast_select_fusion, f32[6,2,16,120]{3,2,1,0:T(8,128)S(1)} %broadcast_in_dim.54, f32[6,2,16,4]{3,2,1,0:T(8,128)S(1)} %broadcast_select_fusion.1, f32[6,2,16,128]{3,2,1,0:T(8,128)S(1)} %slice_add_fusion), kind=kLoop, calls=%fused_computation.11 | loop fusion | flops 262144 | bytes 524288 | tf_op jit(solution)/shard_map/concatenate | solution.py:263
  49.8 12.6 %shard_map.55 = f32[6,2,16,128]{3,2,1,0:T(8,128)} custom-call(f32[4,32]{1,0:T(4,128)} %select_bitcast_fusion.poles_ref, f32[8,2,16,256]{3,2,1,0:T(8,128)} %pad_maximum_fusion.2.spec_ref, f32[4,2,16,256]{3,2,1,0:T(8,128)} %pad_maximum_fusion.3.coef_ref), custom_call_target="tpu_custom_call" | custom-call | tf_op jit(solution)/shard_map/pallas_call | solution.py:140
  (24 shorter events, 0.5 us)
Async XLA Ops:
  0.0 1.3 %copy-start = (f32[6,256,192]{1,2,0:T(8,128)S(1)}, f32[6,256,192]{1,2,0:T(8,128)}, u32[]{:S(2)}) copy-start(f32[6,256,192]{1,2,0:T(8,128)} %param.5) | copy-start | bytes 3538948
  3.8 6.1 %copy-start.1 = (s32[256]{0:T(256)S(1)}, s32[256]{0:T(256)}, u32[]{:S(2)}) copy-start(s32[256]{0:T(256)} %param.7) | copy-start | bytes 3076
  3.8 6.4 %copy-start.2 = (f32[4,64]{1,0:T(4,128)S(1)}, f32[4,64]{1,0:T(4,128)}, u32[]{:S(2)}) copy-start(f32[4,64]{1,0:T(4,128)} %param.8) | copy-start | bytes 3076
  3.8 6.5 %copy-start.3 = (s32[32]{0:T(128)S(1)}, s32[32]{0:T(128)}, u32[]{:S(2)}) copy-start(s32[32]{0:T(128)} %param.9) | copy-start | bytes 388
  3.8 24.0 %all-to-all-start = ((f32[16,16,1152]{2,1,0:T(8,128)}), f32[16,16,1152]{2,1,0:T(8,128)S(1)}, u32[]{:S(2)}, u32[]{:S(2)}) async-start(f32[16,16,1152]{2,1,0:T(8,128)} %bitcast.11), calls=%async_computation | async-start | bytes 2359296 | tf_op jit(solution)/shard_map/all_to_all | solution.py:245
  38.4 7.1 %collective-permute-start.1 = (f32[6,2,16,4]{3,2,1,0:T(8,128)S(1)}, f32[6,2,16,4]{3,2,1,0:T(8,128)S(1)}, u32[]{:S(2)}, u32[]{:S(2)}) collective-permute-start(f32[6,2,16,4]{3,2,1,0:T(8,128)S(1)} %get-tuple-element.10), channel_id=1, source_target_pairs={{0,1},{1,2},{2,3},{3,4},{4,5},{5,6},{6,7},{7,0},{8,9},{9,10},{10,1... | collective-permute-start | bytes 9224 | tf_op jit(solution)/shard_map/ppermute | solution.py:256
  42.8 6.1 %collective-permute-start = (f32[6,2,16,4]{3,2,1,0:T(8,128)S(1)}, f32[6,2,16,4]{3,2,1,0:T(8,128)S(1)}, u32[]{:S(2)}, u32[]{:S(2)}) collective-permute-start(f32[6,2,16,4]{3,2,1,0:T(8,128)S(1)} %get-tuple-element.9), channel_id=1, source_target_pairs={{1,0},{2,1},{3,2},{4,3},{5,4},{6,5},{7,6},{0,7},{9,8},{10,9},{11,1... | collective-permute-start | bytes 9224 | tf_op jit(solution)/shard_map/ppermute | solution.py:257

commit v13 on v11

--- a/solution.py
+++ b/solution.py
@@ -48,11 +48,19 @@
     return jnp.stack([e_lo, e_hi, rossby, gravity], axis=0)
 
 
-def pole_kernel(poles_ref, spec_ref, coef_ref, out_ref):
+def pole_kernel(poles_ref, own_ref, right_ref, left_ref, coef_ref, out_ref, spec_ref):
     npoles = poles_ref.shape[1]
     rows = spec_ref.shape[2]
     lanes = spec_ref.shape[3]
     width = out_ref.shape[3]
+    halo = right_ref.shape[3]
+    comps = own_ref.shape[0]
+    spec_ref[...] = jnp.zeros(spec_ref.shape, jnp.float32)
+    spec_ref[:comps, :, :, :width] = own_ref[...]
+    spec_ref[:comps, :, :, width : width + halo] = right_ref[...]
+    spec_ref[:comps, :, :, lanes - halo :] = left_ref[...]
+    for c in range(2):
+        spec_ref[comps + c] = coef_ref[3] * spec_ref[comps - 2 + c]
     out_ref[...] = jnp.zeros(out_ref.shape, jnp.float32)
 
     def pole_step(step, carry):
@@ -135,18 +143,17 @@
     lax.fori_loop(0, npoles // INTERLEAVE, pole_step, 0)
 
 
-def solve_poles(poles, wide, coef, width):
-    _, parities, rows, _ = wide.shape
+def solve_poles(poles, own, right, left, coef):
+    comps, parities, rows, width = own.shape
+    lanes = coef.shape[3]
     return pl.pallas_call(
         pole_kernel,
-        out_shape=jax.ShapeDtypeStruct((6, parities, rows, width), jnp.float32),
-        in_specs=[
-            pl.BlockSpec(memory_space=pltpu.SMEM),
-            pl.BlockSpec(memory_space=pltpu.VMEM),
-            pl.BlockSpec(memory_space=pltpu.VMEM),
-        ],
+        out_shape=jax.ShapeDtypeStruct((comps, parities, rows, width), jnp.float32),
+        in_specs=[pl.BlockSpec(memory_space=pltpu.SMEM)]
+        + [pl.BlockSpec(memory_space=pltpu.VMEM)] * 4,
         out_specs=pl.BlockSpec(memory_space=pltpu.VMEM),
-    )(poles, wide, coef)
+        scratch_shapes=[pltpu.VMEM((comps + 2, parities, rows, lanes), jnp.float32)],
+    )(poles, own, right, left, coef)
 
 
 def cmul(are, aim, bre, bim):
@@ -256,11 +263,8 @@
         right_halo = lax.ppermute(spectra[..., :HALO], "pole", leftward)
         left_halo = jnp.where(pole_pos > 0, left_halo, 0.0)
         right_halo = jnp.where(pole_pos < pole_count - 1, right_halo, 0.0)
-        gap = jnp.zeros(spectra.shape[:3] + (RING - local_k - 2 * HALO,), jnp.float32)
-        wide = jnp.concatenate([spectra, right_halo, gap, left_halo], axis=3)
         coef = coef_all[:, :, g * group : (g + 1) * group]
-        wide = jnp.concatenate([wide, coef[3][None] * wide[4:6]], axis=0)
-        outs.append(solve_poles(poles, wide, coef, local_k))
+        outs.append(solve_poles(poles, spectra, right_halo, left_halo, coef))
     return jnp.concatenate(outs, axis=2)
 
 

time: 61.7 us -> 65.7 us (1.065)
  the two profiles are of different devices: /device:TPU:6 before, /device:TPU:0 now
where the time goes in v13:
time: 65.7 us; the launch traced here: 65.4 us
  waiting for transfers between devices  23.6 us (36%)
  Pallas kernels  12.7 us (19%)
  starting transfers between devices  11.9 us (18%)
  matrix products  8.31 us (13%)
  other arithmetic  4.56 us (7%)
  local copies, waits for them, and re-layouts  4.18 us (6%)
    all_to_all x1, waiting for transfers between devices, shards(): lax.all_to_all(columns, 'wave', split_axis=0, concat_axis=0, tiled=True)  16 us
    pallas_call x1, Pallas kernels, solve_poles(): pl.pallas_call(pole_kernel, out_shape=jax.ShapeDtypeStruct((comps, pariti...  12.7 us
    ppermute x1, waiting for transfers between devices, shards(): left_halo = lax.ppermute(spectra[..., local_k - HALO:], 'pole', rightward)  6.04 us
    all_to_all x1, starting transfers between devices, shards(): lax.all_to_all(columns, 'wave', split_axis=0, concat_axis=0, tiled=True)  6.01 us
    ppermute x1, starting transfers between devices, shards(): right_halo = lax.ppermute(spectra[..., :HALO], 'pole', leftward)  5.85 us
    dot_general x1, matrix products, shards(): jnp.einsum('mpwlk,pwmcl->cpmk', leg, both, preferred_element_type=jnp.flo...  5.71 us
    unnamed x1, matrix products  2.59 us
    ppermute x1, waiting for transfers between devices, shards(): right_halo = lax.ppermute(spectra[..., :HALO], 'pole', leftward)  1.55 us
  transfers between devices with their start and end apart: 3, of which 3 were waited for; matrix products, arithmetic and copies ran while one was open for 5% of the time, Pallas kernels for 0%

profile of v13, /device:TPU:0, one launch (start us, length us, event | category | flops | bytes accessed | tf_op | source)
XLA Modules:
  0.0 65.4 jit_solution(5915259073727337897)
XLA Ops:
  0.0 1.3 %copy-done = f32[6,256,192]{1,2,0:T(8,128)S(1)} copy-done((f32[6,256,192]{1,2,0:T(8,128)S(1)}, f32[6,256,192]{1,2,0:T(8,128)}, u32[]{:S(2)}) %copy-start) | copy-done | bytes 1179672
  1.3 2.6 %fusion.10 = f32[256,1152]{1,0:T(8,128)} fusion(f32[256,1152]{0,1:T(8,128)S(1)} %bitcast.15, s32[256]{0:T(256)} %param.7), kind=kOutput, calls=%fused_computation.13 | convolution fusion | flops 906035200 | bytes 2360320
  3.9 6.0 %all-to-all-start = ((f32[16,16,1152]{2,1,0:T(8,128)}), f32[16,16,1152]{2,1,0:T(8,128)S(1)}, u32[]{:S(2)}, u32[]{:S(2)}) async-start(f32[16,16,1152]{2,1,0:T(8,128)} %bitcast.9), calls=%async_computation | async-start | bytes 2359296 | tf_op jit(solution)/shard_map/all_to_all | solution.py:252
  10.0 0.1 copy.12
  10.1 0.1 broadcast_multiply_fusion.1
  10.2 0.6 gather_fusion
  11.0 0.1 fusion.27
  11.1 0.6 select_bitcast_fusion.poles_ref
  11.7 16.0 %all-to-all-done = f32[16,16,1152]{2,1,0:T(8,128)S(1)} async-done(((f32[16,16,1152]{2,1,0:T(8,128)}), f32[16,16,1152]{2,1,0:T(8,128)S(1)}, u32[]{:S(2)}, u32[]{:S(2)}) %all-to-all-start) | async-done | bytes 1179680 | tf_op jit(solution)/shard_map/all_to_all | solution.py:252
  27.8 0.9 %slice_add_fusion = (f32[8,16,1152]{2,1,0:T(8,128)}, f32[8,16,1152]{2,1,0:T(8,128)S(1)}) fusion(f32[16,16,1152]{2,1,0:T(8,128)S(1)} %all-to-all-done), kind=kLoop, calls=%fused_computation.11 | loop fusion | flops 294912 | bytes 2359296 | tf_op jit(solution)/shard_map/add | solution.py:256
  28.7 0.4 sub.27
  29.1 1.5 %add.185 = f32[1,8,16,6,192]{4,3,2,1,0:T(8,128)S(1)} reshape(f32[8,16,1152]{2,1,0:T(8,128)} %get-tuple-element.7) | data formatting | bytes 1179648 | tf_op jit(solution)/shard_map/add | solution.py:256
  30.5 0.3 pad_maximum_fusion
  30.8 0.1 copy.28
  31.0 0.4 subtract_convert_fusion
  31.4 5.7 %fusion.5 = f32[2,16,12,128]{3,2,1,0:T(8,128)S(1)} fusion(bf16[16,2,8,192,128]{4,3,2,1,0:T(8,128)(2,1)} %bitcast.17, bf16[2,8,16,6,192]{4,3,1,2,0:T(8,128)(2,1)S(1)} %subtract_convert_fusion, bf16[2,8,16,6,192]{4,3,1,2,0:T(8,128)(2,1)S(1)} %copy.28), kind=kOutput, calls=%fused_computation.9 | convolution fusion | flops 153354240 | bytes 13959168 | tf_op jit(solution)/shard_map/mpwlk,pwmcl->cpmk/dot_general | solution.py:260
  37.2 0.1 fusion.29
  37.3 5.8 %collective-permute-start = (f32[6,2,16,4]{3,2,1,0:T(8,128)S(1)}, f32[6,2,16,4]{3,2,1,0:T(8,128)S(1)}, u32[]{:S(2)}, u32[]{:S(2)}) collective-permute-start(f32[6,2,16,4]{3,2,1,0:T(8,128)S(1)} %get-tuple-element.10), channel_id=1, source_target_pairs={{1,0},{2,1},{3,2},{4,3},{5,4},{6,5},{7,6},{0,7},{9,8},{10,9},{11,1... | collective-permute-start | bytes 9224 | tf_op jit(solution)/shard_map/ppermute | solution.py:263
  43.2 0.7 %pad_maximum_fusion.1.coef_ref = f32[4,2,16,256]{3,2,1,0:T(8,128)} fusion(f32[1,2,16,256]{3,2,1,0:T(8,128)S(1)} %get-tuple-element.13, f32[1,2,16,256]{3,2,1,0:T(8,128)S(1)} %get-tuple-element.14, f32[2,2,16,256]{3,2,1,0:T(8,128)S(1)} %maximum_multiply_fusion), kind=kLoop, calls=%fused_computation.15 | loop fusion | flops 65536 | bytes 262144 | tf_op jit(solution)/shard_map/concatenate | solution.py:242
  43.8 1.6 %collective-permute-done = f32[6,2,16,4]{3,2,1,0:T(8,128)S(1)} collective-permute-done((f32[6,2,16,4]{3,2,1,0:T(8,128)S(1)}, f32[6,2,16,4]{3,2,1,0:T(8,128)S(1)}, u32[]{:S(2)}, u32[]{:S(2)}) %collective-permute-start) | collective-permute-done | bytes 3104 | tf_op jit(solution)/shard_map/ppermute | solution.py:263
  45.4 0.6 broadcast_select_fusion.1.right_ref
  46.0 6.0 %collective-permute-done.1 = f32[6,2,16,4]{3,2,1,0:T(8,128)S(1)} collective-permute-done((f32[6,2,16,4]{3,2,1,0:T(8,128)S(1)}, f32[6,2,16,4]{3,2,1,0:T(8,128)S(1)}, u32[]{:S(2)}, u32[]{:S(2)}) %collective-permute-start.1) | collective-permute-done | bytes 3104 | tf_op jit(solution)/shard_map/ppermute | solution.py:262
  52.1 0.6 broadcast_select_fusion.left_ref
  52.7 12.7 %shard_map.55 = f32[6,2,16,128]{3,2,1,0:T(8,128)} custom-call(f32[4,32]{1,0:T(4,128)} %select_bitcast_fusion.poles_ref, f32[6,2,16,128]{3,2,1,0:T(8,128)} %copy-done.1, f32[6,2,16,4]{3,2,1,0:T(8,128)} %broadcast_select_fusion.1.right_ref, f32[6,2,16,4]{3,2,1,0:T(8,128)} %broadcast_select_fusion.left_ref, f32[4,2,16,256]{3,2,1,0:T(8,128)} %pad_maximum_fusion.1.coef_ref), custom_call_target="tpu_custom_call" | custom-call | tf_op jit(solution)/shard_map/pallas_call | solution.py:149
  (23 shorter events, 0.4 us)
Async XLA Ops:
  0.0 1.3 %copy-start = (f32[6,256,192]{1,2,0:T(8,128)S(1)}, f32[6,256,192]{1,2,0:T(8,128)}, u32[]{:S(2)}) copy-start(f32[6,256,192]{1,2,0:T(8,128)} %param.5) | copy-start | bytes 3538948
  1.3 8.7 %copy-start.3 = (f32[4,64]{1,0:T(4,128)S(1)}, f32[4,64]{1,0:T(4,128)}, u32[]{:S(2)}) copy-start(f32[4,64]{1,0:T(4,128)} %param.8) | copy-start | bytes 3076
  1.3 8.8 %copy-start.4 = (s32[32]{0:T(128)S(1)}, s32[32]{0:T(128)}, u32[]{:S(2)}) copy-start(s32[32]{0:T(128)} %param.9) | copy-start | bytes 388
  1.3 8.8 %copy-start.2 = (s32[256]{0:T(256)S(1)}, s32[256]{0:T(256)}, u32[]{:S(2)}) copy-start(s32[256]{0:T(256)} %param.7) | copy-start | bytes 3076
  3.9 23.9 %all-to-all-start = ((f32[16,16,1152]{2,1,0:T(8,128)}), f32[16,16,1152]{2,1,0:T(8,128)S(1)}, u32[]{:S(2)}, u32[]{:S(2)}) async-start(f32[16,16,1152]{2,1,0:T(8,128)} %bitcast.9), calls=%async_computation | async-start | bytes 2359296 | tf_op jit(solution)/shard_map/all_to_all | solution.py:252
  37.2 15.5 %copy-start.1 = (f32[6,2,16,128]{3,2,1,0:T(8,128)}, f32[6,2,16,128]{3,2,1,0:T(8,128)S(1)}, u32[]{:S(2)}) copy-start(f32[6,2,16,128]{3,2,1,0:T(8,128)S(1)} %slice_add_fusion.1.own_ref) | copy-start | bytes 294916
  37.3 8.1 %collective-permute-start = (f32[6,2,16,4]{3,2,1,0:T(8,128)S(1)}, f32[6,2,16,4]{3,2,1,0:T(8,128)S(1)}, u32[]{:S(2)}, u32[]{:S(2)}) collective-permute-start(f32[6,2,16,4]{3,2,1,0:T(8,128)S(1)} %get-tuple-element.10), channel_id=1, source_target_pairs={{1,0},{2,1},{3,2},{4,3},{5,4},{6,5},{7,6},{0,7},{9,8},{10,9},{11,1... | collective-permute-start | bytes 9224 | tf_op jit(solution)/shard_map/ppermute | solution.py:263
  43.8 8.2 %collective-permute-start.1 = (f32[6,2,16,4]{3,2,1,0:T(8,128)S(1)}, f32[6,2,16,4]{3,2,1,0:T(8,128)S(1)}, u32[]{:S(2)}, u32[]{:S(2)}) collective-permute-start(f32[6,2,16,4]{3,2,1,0:T(8,128)S(1)} %get-tuple-element.9), channel_id=1, source_target_pairs={{0,1},{1,2},{2,3},{3,4},{4,5},{5,6},{6,7},{7,0},{8,9},{9,10},{10,1... | collective-permute-start | bytes 9224 | tf_op jit(solution)/shard_map/ppermute | solution.py:262

commit v14 on v11

--- a/solution.py
+++ b/solution.py
@@ -48,10 +48,11 @@
     return jnp.stack([e_lo, e_hi, rossby, gravity], axis=0)
 
 
-def pole_kernel(poles_ref, spec_ref, coef_ref, out_ref):
+def pole_kernel(poles_ref, own_ref, edge_ref, coef_ref, out_ref):
     npoles = poles_ref.shape[1]
-    rows = spec_ref.shape[2]
-    lanes = spec_ref.shape[3]
+    rows = own_ref.shape[2]
+    lanes = coef_ref.shape[3]
+    spec_ref = (own_ref, edge_ref)
     width = out_ref.shape[3]
     out_ref[...] = jnp.zeros(out_ref.shape, jnp.float32)
 
@@ -64,6 +65,8 @@
                 lanes_work.append((scal, pl.ds(r0, CHUNK)))
 
         def ld(ref, i, p, sl):
+            if isinstance(ref, tuple):
+                return jnp.concatenate([part[i, p, sl, :] for part in ref], axis=-1)
             return ref[i, p, sl, :]
 
         def near(x, sl):
@@ -135,18 +138,15 @@
     lax.fori_loop(0, npoles // INTERLEAVE, pole_step, 0)
 
 
-def solve_poles(poles, wide, coef, width):
-    _, parities, rows, _ = wide.shape
+def solve_poles(poles, own, edge, coef, width):
+    _, parities, rows, _ = own.shape
     return pl.pallas_call(
         pole_kernel,
         out_shape=jax.ShapeDtypeStruct((6, parities, rows, width), jnp.float32),
-        in_specs=[
-            pl.BlockSpec(memory_space=pltpu.SMEM),
-            pl.BlockSpec(memory_space=pltpu.VMEM),
-            pl.BlockSpec(memory_space=pltpu.VMEM),
-        ],
+        in_specs=[pl.BlockSpec(memory_space=pltpu.SMEM)]
+        + [pl.BlockSpec(memory_space=pltpu.VMEM)] * 3,
         out_specs=pl.BlockSpec(memory_space=pltpu.VMEM),
-    )(poles, wide, coef)
+    )(poles, own, edge, coef)
 
 
 def cmul(are, aim, bre, bim):
@@ -256,11 +256,12 @@
         right_halo = lax.ppermute(spectra[..., :HALO], "pole", leftward)
         left_halo = jnp.where(pole_pos > 0, left_halo, 0.0)
         right_halo = jnp.where(pole_pos < pole_count - 1, right_halo, 0.0)
+        coef = coef_all[:, :, g * group : (g + 1) * group]
+        own = jnp.concatenate([spectra, coef[3][None, ..., :local_k] * spectra[4:6]], axis=0)
         gap = jnp.zeros(spectra.shape[:3] + (RING - local_k - 2 * HALO,), jnp.float32)
-        wide = jnp.concatenate([spectra, right_halo, gap, left_halo], axis=3)
-        coef = coef_all[:, :, g * group : (g + 1) * group]
-        wide = jnp.concatenate([wide, coef[3][None] * wide[4:6]], axis=0)
-        outs.append(solve_poles(poles, wide, coef, local_k))
+        edge = jnp.concatenate([right_halo, gap, left_halo], axis=3)
+        edge = jnp.concatenate([edge, coef[3][None, ..., local_k:] * edge[4:6]], axis=0)
+        outs.append(solve_poles(poles, own, edge, coef, local_k))
     return jnp.concatenate(outs, axis=2)
 
 

time: 61.7 us -> 62.4 us (1.011)
  the two profiles are of different devices: /device:TPU:6 before, /device:TPU:1 now
where the time goes in v14:
time: 62.4 us; the launch traced here: 62.1 us
  waiting for transfers between devices  19 us (30%)
  starting transfers between devices  13 us (21%)
  Pallas kernels  12.6 us (20%)
  matrix products  8.3 us (13%)
  other arithmetic  4.88 us (8%)
  local copies, waits for them, and re-layouts  4.19 us (7%)
    all_to_all x1, waiting for transfers between devices, shards(): lax.all_to_all(columns, 'wave', split_axis=0, concat_axis=0, tiled=True)  14.5 us
    pallas_call x1, Pallas kernels, solve_poles(): pl.pallas_call(pole_kernel, out_shape=jax.ShapeDtypeStruct((6, parities,...  12.6 us
    all_to_all x1, starting transfers between devices, shards(): lax.all_to_all(columns, 'wave', split_axis=0, concat_axis=0, tiled=True)  7.34 us
    dot_general x1, matrix products, shards(): jnp.einsum('mpwlk,pwmcl->cpmk', leg, both, preferred_element_type=jnp.flo...  5.71 us
    ppermute x1, starting transfers between devices, shards(): left_halo = lax.ppermute(spectra[..., local_k - HALO:], 'pole', rightward)  3.37 us
    ppermute x1, waiting for transfers between devices, shards(): right_halo = lax.ppermute(spectra[..., :HALO], 'pole', leftward)  3.13 us
    unnamed x1, matrix products  2.59 us
    ppermute x1, starting transfers between devices, shards(): right_halo = lax.ppermute(spectra[..., :HALO], 'pole', leftward)  2.28 us
  transfers between devices with their start and end apart: 3, of which 3 were waited for; matrix products, arithmetic and copies ran while one was open for 5% of the time, Pallas kernels for 0%

profile of v14, /device:TPU:1, one launch (start us, length us, event | category | flops | bytes accessed | tf_op | source)
XLA Modules:
  0.0 62.1 jit_solution(26771703667623075)
XLA Ops:
  0.0 1.3 %copy-done = f32[6,256,192]{1,2,0:T(8,128)S(1)} copy-done((f32[6,256,192]{1,2,0:T(8,128)S(1)}, f32[6,256,192]{1,2,0:T(8,128)}, u32[]{:S(2)}) %copy-start) | copy-done | bytes 1179672
  1.3 2.6 %fusion.10 = f32[256,1152]{1,0:T(8,128)} fusion(f32[256,1152]{0,1:T(8,128)S(1)} %bitcast.15, s32[256]{0:T(256)} %param.7), kind=kOutput, calls=%fused_computation.13 | convolution fusion | flops 906035200 | bytes 2360320
  3.9 7.3 %all-to-all-start = ((f32[16,16,1152]{2,1,0:T(8,128)}), f32[16,16,1152]{2,1,0:T(8,128)S(1)}, u32[]{:S(2)}, u32[]{:S(2)}) async-start(f32[16,16,1152]{2,1,0:T(8,128)} %bitcast.9), calls=%async_computation | async-start | bytes 2359296 | tf_op jit(solution)/shard_map/all_to_all | solution.py:245
  11.5 0.1 copy.12
  11.6 0.6 gather_fusion
  12.3 0.1 fusion.29
  12.4 0.7 %pad_maximum_fusion.3.coef_ref = f32[4,2,16,256]{3,2,1,0:T(8,128)} fusion(f32[1,2,16,256]{3,2,1,0:T(8,128)S(1)} %get-tuple-element.15, f32[1,2,16,256]{3,2,1,0:T(8,128)S(1)} %get-tuple-element.16, f32[2,2,16,256]{3,2,1,0:T(8,128)S(1)} %maximum_multiply_fusion), kind=kLoop, calls=%fused_computation.17 | loop fusion | flops 65536 | bytes 262144 | tf_op jit(solution)/shard_map/concatenate | solution.py:235
  13.1 0.6 select_bitcast_fusion.poles_ref
  13.8 14.5 %all-to-all-done = f32[16,16,1152]{2,1,0:T(8,128)S(1)} async-done(((f32[16,16,1152]{2,1,0:T(8,128)}), f32[16,16,1152]{2,1,0:T(8,128)S(1)}, u32[]{:S(2)}, u32[]{:S(2)}) %all-to-all-start) | async-done | bytes 1179680 | tf_op jit(solution)/shard_map/all_to_all | solution.py:245
  28.3 0.9 %slice_add_fusion = (f32[8,16,1152]{2,1,0:T(8,128)S(1)}, f32[8,16,1152]{2,1,0:T(8,128)}) fusion(f32[16,16,1152]{2,1,0:T(8,128)S(1)} %all-to-all-done), kind=kLoop, calls=%fused_computation.11 | loop fusion | flops 294912 | bytes 2359296 | tf_op jit(solution)/shard_map/add | solution.py:249
  29.2 0.4 add.193
  29.6 1.5 %sub.27 = f32[1,8,16,6,192]{4,3,2,1,0:T(8,128)S(1)} reshape(f32[8,16,1152]{2,1,0:T(8,128)} %get-tuple-element.8) | data formatting | bytes 1179648 | tf_op jit(solution)/shard_map/sub | solution.py:249
  31.1 0.3 pad_maximum_fusion
  31.4 0.1 copy.28
  31.5 0.4 subtract_convert_fusion
  31.9 5.7 %fusion.5 = f32[2,16,12,128]{3,2,1,0:T(8,128)S(1)} fusion(bf16[16,2,8,192,128]{4,3,2,1,0:T(8,128)(2,1)} %bitcast.17, bf16[2,8,16,6,192]{4,3,1,2,0:T(8,128)(2,1)S(1)} %subtract_convert_fusion, bf16[2,8,16,6,192]{4,3,1,2,0:T(8,128)(2,1)S(1)} %copy.28), kind=kOutput, calls=%fused_computation.9 | convolution fusion | flops 153354240 | bytes 13959168 | tf_op jit(solution)/shard_map/mpwlk,pwmcl->cpmk/dot_general | solution.py:253
  37.8 0.1 fusion.32
  37.9 3.4 %collective-permute-start.1 = (f32[6,2,16,4]{3,2,1,0:T(8,128)S(1)}, f32[6,2,16,4]{3,2,1,0:T(8,128)S(1)}, u32[]{:S(2)}, u32[]{:S(2)}) collective-permute-start(f32[6,2,16,4]{3,2,1,0:T(8,128)S(1)} %get-tuple-element.10), channel_id=1, source_target_pairs={{0,1},{1,2},{2,3},{3,4},{4,5},{5,6},{6,7},{7,0},{8,9},{9,10},{10,1... | collective-permute-start | bytes 9224 | tf_op jit(solution)/shard_map/ppermute | solution.py:255
  41.2 2.3 %collective-permute-start = (f32[6,2,16,4]{3,2,1,0:T(8,128)S(1)}, f32[6,2,16,4]{3,2,1,0:T(8,128)S(1)}, u32[]{:S(2)}, u32[]{:S(2)}) collective-permute-start(f32[6,2,16,4]{3,2,1,0:T(8,128)S(1)} %get-tuple-element.9), channel_id=1, source_target_pairs={{1,0},{2,1},{3,2},{4,3},{5,4},{6,5},{7,6},{0,7},{9,8},{10,9},{11,1... | collective-permute-start | bytes 9224 | tf_op jit(solution)/shard_map/ppermute | solution.py:256
  43.5 0.7 %pad_maximum_fusion.1.own_ref = f32[8,2,16,128]{3,2,1,0:T(8,128)} fusion(f32[2,2,16,128]{3,2,1,0:T(8,128)S(1)} %slice_multiply_fusion, f32[6,2,16,128]{3,2,1,0:T(8,128)S(1)} %slice_add_fusion.1), kind=kLoop, calls=%fused_computation.15 | loop fusion | flops 32768 | bytes 262144 | tf_op jit(solution)/shard_map/concatenate | solution.py:260
  44.2 1.3 %collective-permute-done.1 = f32[6,2,16,4]{3,2,1,0:T(8,128)S(1)} collective-permute-done((f32[6,2,16,4]{3,2,1,0:T(8,128)S(1)}, f32[6,2,16,4]{3,2,1,0:T(8,128)S(1)}, u32[]{:S(2)}, u32[]{:S(2)}) %collective-permute-start.1) | collective-permute-done | bytes 3104 | tf_op jit(solution)/shard_map/ppermute | solution.py:255
  45.5 3.1 %collective-permute-done = f32[6,2,16,4]{3,2,1,0:T(8,128)S(1)} collective-permute-done((f32[6,2,16,4]{3,2,1,0:T(8,128)S(1)}, f32[6,2,16,4]{3,2,1,0:T(8,128)S(1)}, u32[]{:S(2)}, u32[]{:S(2)}) %collective-permute-start) | collective-permute-done | bytes 3104 | tf_op jit(solution)/shard_map/ppermute | solution.py:256
  48.7 0.8 %pad_maximum_fusion.2.edge_ref = f32[8,2,16,128]{3,2,1,0:T(8,128)} fusion(f32[2,2,16,128]{3,2,1,0:T(8,128)S(1)} %fusion.30, f32[6,2,16,4]{3,2,1,0:T(8,128)S(1)} %broadcast_select_fusion, f32[6,2,16,120]{3,2,1,0:T(8,128)S(1)} %broadcast_in_dim.56, f32[6,2,16,4]{3,2,1,0:T(8,128)S(1)} %broadcast_select_fusion.1), kind=kLoop, calls=%fused_computation.16 | loop fusion | flops 98304 | bytes 262144 | tf_op jit(solution)/shard_map/concatenate | solution.py:263
  49.5 12.6 %shard_map.55 = f32[6,2,16,128]{3,2,1,0:T(8,128)} custom-call(f32[4,32]{1,0:T(4,128)} %select_bitcast_fusion.poles_ref, f32[8,2,16,128]{3,2,1,0:T(8,128)} %pad_maximum_fusion.1.own_ref, f32[8,2,16,128]{3,2,1,0:T(8,128)} %pad_maximum_fusion.2.edge_ref, f32[4,2,16,256]{3,2,1,0:T(8,128)} %pad_maximum_fusion.3.coef_ref), custom_call_target="tpu_custom_call" | custom-call | tf_op jit(solution)/shard_map/pallas_call | solution.py:143
  (28 shorter events, 0.7 us)
Async XLA Ops:
  0.0 1.3 %copy-start = (f32[6,256,192]{1,2,0:T(8,128)S(1)}, f32[6,256,192]{1,2,0:T(8,128)}, u32[]{:S(2)}) copy-start(f32[6,256,192]{1,2,0:T(8,128)} %param.5) | copy-start | bytes 3538948
  1.3 10.0 %copy-start.1 = (s32[256]{0:T(256)S(1)}, s32[256]{0:T(256)}, u32[]{:S(2)}) copy-start(s32[256]{0:T(256)} %param.7) | copy-start | bytes 3076
  1.3 10.2 %copy-start.2 = (f32[4,64]{1,0:T(4,128)S(1)}, f32[4,64]{1,0:T(4,128)}, u32[]{:S(2)}) copy-start(f32[4,64]{1,0:T(4,128)} %param.8) | copy-start | bytes 3076
  1.3 10.3 %copy-start.3 = (s32[32]{0:T(128)S(1)}, s32[32]{0:T(128)}, u32[]{:S(2)}) copy-start(s32[32]{0:T(128)} %param.9) | copy-start | bytes 388
  3.9 24.4 %all-to-all-start = ((f32[16,16,1152]{2,1,0:T(8,128)}), f32[16,16,1152]{2,1,0:T(8,128)S(1)}, u32[]{:S(2)}, u32[]{:S(2)}) async-start(f32[16,16,1152]{2,1,0:T(8,128)} %bitcast.9), calls=%async_computation | async-start | bytes 2359296 | tf_op jit(solution)/shard_map/all_to_all | solution.py:245
  37.9 7.6 %collective-permute-start.1 = (f32[6,2,16,4]{3,2,1,0:T(8,128)S(1)}, f32[6,2,16,4]{3,2,1,0:T(8,128)S(1)}, u32[]{:S(2)}, u32[]{:S(2)}) collective-permute-start(f32[6,2,16,4]{3,2,1,0:T(8,128)S(1)} %get-tuple-element.10), channel_id=1, source_target_pairs={{0,1},{1,2},{2,3},{3,4},{4,5},{5,6},{6,7},{7,0},{8,9},{9,10},{10,1... | collective-permute-start | bytes 9224 | tf_op jit(solution)/shard_map/ppermute | solution.py:255
  41.2 7.4 %collective-permute-start = (f32[6,2,16,4]{3,2,1,0:T(8,128)S(1)}, f32[6,2,16,4]{3,2,1,0:T(8,128)S(1)}, u32[]{:S(2)}, u32[]{:S(2)}) collective-permute-start(f32[6,2,16,4]{3,2,1,0:T(8,128)S(1)} %get-tuple-element.9), channel_id=1, source_target_pairs={{1,0},{2,1},{3,2},{4,3},{5,4},{6,5},{7,6},{0,7},{9,8},{10,9},{11,1... | collective-permute-start | bytes 9224 | tf_op jit(solution)/shard_map/ppermute | solution.py:256

commit v15 on v11

--- a/solution.py
+++ b/solution.py
@@ -240,7 +240,7 @@
     outs = []
     for g in range(GROUPS):
         pick = onehot[:, g].reshape(wave_count * group, waves)
-        columns = jnp.einsum("sm,cml->scl", pick, grid, precision=lax.Precision.HIGHEST)
+        columns = jnp.einsum("sm,cml->scl", pick, grid, precision=lax.Precision.HIGH)
         columns = columns.reshape(wave_count * group, comps * lat_rows)
         regrouped = lax.all_to_all(columns, "wave", split_axis=0, concat_axis=0, tiled=True)
         regrouped = regrouped.reshape(wave_count, group, comps, lat_rows)

time: 61.7 us -> 61.5 us (level)
  no operation moved by 1% of the time
where the time goes in v15:
time: 61.5 us; the launch traced here: 61 us
  waiting for transfers between devices  21.2 us (34%)
  Pallas kernels  12.6 us (20%)
  starting transfers between devices  10.4 us (17%)
  matrix products  8.04 us (13%)
  other arithmetic  4.3 us (7%)
  local copies, waits for them, and re-layouts  4.18 us (7%)
    all_to_all x1, waiting for transfers between devices, shards(): lax.all_to_all(columns, 'wave', split_axis=0, concat_axis=0, tiled=True)  16 us
    pallas_call x1, Pallas kernels, solve_poles(): pl.pallas_call(pole_kernel, out_shape=jax.ShapeDtypeStruct((6, parities,...  12.6 us
    all_to_all x1, starting transfers between devices, shards(): lax.all_to_all(columns, 'wave', split_axis=0, concat_axis=0, tiled=True)  5.93 us
    dot_general x1, matrix products, shards(): jnp.einsum('mpwlk,pwmcl->cpmk', leg, both, preferred_element_type=jnp.flo...  5.71 us
    ppermute x1, starting transfers between devices, shards(): left_halo = lax.ppermute(spectra[..., local_k - HALO:], 'pole', rightward)  3.65 us
    ppermute x1, waiting for transfers between devices, shards(): right_halo = lax.ppermute(spectra[..., :HALO], 'pole', leftward)  3.35 us
    unnamed x1, matrix products  2.33 us
    ppermute x1, waiting for transfers between devices, shards(): left_halo = lax.ppermute(spectra[..., local_k - HALO:], 'pole', rightward)  1.92 us
  transfers between devices with their start and end apart: 3, of which 3 were waited for; matrix products, arithmetic and copies ran while one was open for 4% of the time, Pallas kernels for 0%

profile of v15, /device:TPU:6, one launch (start us, length us, event | category | flops | bytes accessed | tf_op | source)
XLA Modules:
  0.0 61.0 jit_solution(11740818212630300080)
XLA Ops:
  0.0 1.3 %copy-done = f32[6,256,192]{1,2,0:T(8,128)S(1)} copy-done((f32[6,256,192]{1,2,0:T(8,128)S(1)}, f32[6,256,192]{1,2,0:T(8,128)}, u32[]{:S(2)}) %copy-start) | copy-done | bytes 1179672
  1.3 2.3 %fusion.10 = f32[256,1152]{1,0:T(8,128)} fusion(f32[256,1152]{0,1:T(8,128)S(1)} %bitcast.15, s32[256]{0:T(256)} %param.7), kind=kOutput, calls=%fused_computation.14 | convolution fusion | flops 453050368 | bytes 2360320
  3.6 5.9 %all-to-all-start = ((f32[16,16,1152]{2,1,0:T(8,128)}), f32[16,16,1152]{2,1,0:T(8,128)S(1)}, u32[]{:S(2)}, u32[]{:S(2)}) async-start(f32[16,16,1152]{2,1,0:T(8,128)} %bitcast.9), calls=%async_computation | async-start | bytes 2359296 | tf_op jit(solution)/shard_map/all_to_all | solution.py:245
  9.8 0.1 copy.12
  10.0 0.6 gather_fusion
  10.6 0.1 fusion.30
  10.8 0.6 select_bitcast_fusion.poles_ref
  11.5 16.0 %all-to-all-done = f32[16,16,1152]{2,1,0:T(8,128)S(1)} async-done(((f32[16,16,1152]{2,1,0:T(8,128)}), f32[16,16,1152]{2,1,0:T(8,128)S(1)}, u32[]{:S(2)}, u32[]{:S(2)}) %all-to-all-start) | async-done | bytes 1179680 | tf_op jit(solution)/shard_map/all_to_all | solution.py:245
  27.4 0.9 %slice_add_fusion = (f32[8,16,1152]{2,1,0:T(8,128)S(1)}, f32[8,16,1152]{2,1,0:T(8,128)}) fusion(f32[16,16,1152]{2,1,0:T(8,128)S(1)} %all-to-all-done), kind=kLoop, calls=%fused_computation.11 | loop fusion | flops 294912 | bytes 2359296 | tf_op jit(solution)/shard_map/add | solution.py:249
  28.3 0.4 add.193
  28.7 1.5 %sub.27 = f32[1,8,16,6,192]{4,3,2,1,0:T(8,128)S(1)} reshape(f32[8,16,1152]{2,1,0:T(8,128)} %get-tuple-element.8) | data formatting | bytes 1179648 | tf_op jit(solution)/shard_map/sub | solution.py:249
  30.2 0.3 pad_maximum_fusion
  30.5 0.1 copy.28
  30.6 0.4 subtract_convert_fusion
  31.1 5.7 %fusion.5 = f32[2,16,12,128]{3,2,1,0:T(8,128)S(1)} fusion(bf16[16,2,8,192,128]{4,3,2,1,0:T(8,128)(2,1)} %bitcast.17, bf16[2,8,16,6,192]{4,3,1,2,0:T(8,128)(2,1)S(1)} %subtract_convert_fusion, bf16[2,8,16,6,192]{4,3,1,2,0:T(8,128)(2,1)S(1)} %copy.28), kind=kOutput, calls=%fused_computation.9 | convolution fusion | flops 153354240 | bytes 13959168 | tf_op jit(solution)/shard_map/mpwlk,pwmcl->cpmk/dot_general | solution.py:253
  36.9 0.1 fusion.32
  37.0 3.7 %collective-permute-start.1 = (f32[6,2,16,4]{3,2,1,0:T(8,128)S(1)}, f32[6,2,16,4]{3,2,1,0:T(8,128)S(1)}, u32[]{:S(2)}, u32[]{:S(2)}) collective-permute-start(f32[6,2,16,4]{3,2,1,0:T(8,128)S(1)} %get-tuple-element.10), channel_id=1, source_target_pairs={{0,1},{1,2},{2,3},{3,4},{4,5},{5,6},{6,7},{7,0},{8,9},{9,10},{10,1... | collective-permute-start | bytes 9224 | tf_op jit(solution)/shard_map/ppermute | solution.py:255
  40.6 0.7 %pad_maximum_fusion.2.coef_ref = f32[4,2,16,256]{3,2,1,0:T(8,128)} fusion(f32[1,2,16,256]{3,2,1,0:T(8,128)S(1)} %get-tuple-element.13, f32[1,2,16,256]{3,2,1,0:T(8,128)S(1)} %get-tuple-element.14, f32[2,2,16,256]{3,2,1,0:T(8,128)S(1)} %maximum_multiply_fusion), kind=kLoop, calls=%fused_computation.16 | loop fusion | flops 65536 | bytes 262144 | tf_op jit(solution)/shard_map/concatenate | solution.py:235
  41.3 0.8 %collective-permute-start = (f32[6,2,16,4]{3,2,1,0:T(8,128)S(1)}, f32[6,2,16,4]{3,2,1,0:T(8,128)S(1)}, u32[]{:S(2)}, u32[]{:S(2)}) collective-permute-start(f32[6,2,16,4]{3,2,1,0:T(8,128)S(1)} %get-tuple-element.9), channel_id=1, source_target_pairs={{1,0},{2,1},{3,2},{4,3},{5,4},{6,5},{7,6},{0,7},{9,8},{10,9},{11,1... | collective-permute-start | bytes 9224 | tf_op jit(solution)/shard_map/ppermute | solution.py:256
  42.1 1.9 %collective-permute-done.1 = f32[6,2,16,4]{3,2,1,0:T(8,128)S(1)} collective-permute-done((f32[6,2,16,4]{3,2,1,0:T(8,128)S(1)}, f32[6,2,16,4]{3,2,1,0:T(8,128)S(1)}, u32[]{:S(2)}, u32[]{:S(2)}) %collective-permute-start.1) | collective-permute-done | bytes 3104 | tf_op jit(solution)/shard_map/ppermute | solution.py:255
  44.1 3.3 %collective-permute-done = f32[6,2,16,4]{3,2,1,0:T(8,128)S(1)} collective-permute-done((f32[6,2,16,4]{3,2,1,0:T(8,128)S(1)}, f32[6,2,16,4]{3,2,1,0:T(8,128)S(1)}, u32[]{:S(2)}, u32[]{:S(2)}) %collective-permute-start) | collective-permute-done | bytes 3104 | tf_op jit(solution)/shard_map/ppermute | solution.py:256
  47.5 0.1 fusion.12
  47.5 0.8 %pad_maximum_fusion.1.spec_ref = f32[8,2,16,256]{3,2,1,0:T(8,128)} fusion(f32[2,2,16,256]{3,2,1,0:T(8,128)S(1)} %fusion.12, f32[6,2,16,4]{3,2,1,0:T(8,128)S(1)} %broadcast_select_fusion, f32[6,2,16,120]{3,2,1,0:T(8,128)S(1)} %broadcast_in_dim.54, f32[6,2,16,4]{3,2,1,0:T(8,128)S(1)} %broadcast_select_fusion.1, f32[6,2,16,128]{3,2,1,0:T(8,128)S(1)} %slice_add_fusion.1), kind=kLoop, calls=%fused_computation.12 | loop fusion | flops 262144 | bytes 524288 | tf_op jit(solution)/shard_map/concatenate | solution.py:262
  48.4 12.6 %shard_map.55 = f32[6,2,16,128]{3,2,1,0:T(8,128)} custom-call(f32[4,32]{1,0:T(4,128)} %select_bitcast_fusion.poles_ref, f32[8,2,16,256]{3,2,1,0:T(8,128)} %pad_maximum_fusion.1.spec_ref, f32[4,2,16,256]{3,2,1,0:T(8,128)} %pad_maximum_fusion.2.coef_ref), custom_call_target="tpu_custom_call" | custom-call | tf_op jit(solution)/shard_map/pallas_call | solution.py:140
  (25 shorter events, 0.6 us)
Async XLA Ops:
  0.0 1.3 %copy-start = (f32[6,256,192]{1,2,0:T(8,128)S(1)}, f32[6,256,192]{1,2,0:T(8,128)}, u32[]{:S(2)}) copy-start(f32[6,256,192]{1,2,0:T(8,128)} %param.5) | copy-start | bytes 3538948
  1.3 8.3 %copy-start.1 = (s32[256]{0:T(256)S(1)}, s32[256]{0:T(256)}, u32[]{:S(2)}) copy-start(s32[256]{0:T(256)} %param.7) | copy-start | bytes 3076
  1.3 8.6 %copy-start.2 = (f32[4,64]{1,0:T(4,128)S(1)}, f32[4,64]{1,0:T(4,128)}, u32[]{:S(2)}) copy-start(f32[4,64]{1,0:T(4,128)} %param.8) | copy-start | bytes 3076
  1.3 8.7 %copy-start.3 = (s32[32]{0:T(128)S(1)}, s32[32]{0:T(128)}, u32[]{:S(2)}) copy-start(s32[32]{0:T(128)} %param.9) | copy-start | bytes 388
  3.6 23.8 %all-to-all-start = ((f32[16,16,1152]{2,1,0:T(8,128)}), f32[16,16,1152]{2,1,0:T(8,128)S(1)}, u32[]{:S(2)}, u32[]{:S(2)}) async-start(f32[16,16,1152]{2,1,0:T(8,128)} %bitcast.9), calls=%async_computation | async-start | bytes 2359296 | tf_op jit(solution)/shard_map/all_to_all | solution.py:245
  37.0 7.1 %collective-permute-start.1 = (f32[6,2,16,4]{3,2,1,0:T(8,128)S(1)}, f32[6,2,16,4]{3,2,1,0:T(8,128)S(1)}, u32[]{:S(2)}, u32[]{:S(2)}) collective-permute-start(f32[6,2,16,4]{3,2,1,0:T(8,128)S(1)} %get-tuple-element.10), channel_id=1, source_target_pairs={{0,1},{1,2},{2,3},{3,4},{4,5},{5,6},{6,7},{7,0},{8,9},{9,10},{10,1... | collective-permute-start | bytes 9224 | tf_op jit(solution)/shard_map/ppermute | solution.py:255
  41.3 6.1 %collective-permute-start = (f32[6,2,16,4]{3,2,1,0:T(8,128)S(1)}, f32[6,2,16,4]{3,2,1,0:T(8,128)S(1)}, u32[]{:S(2)}, u32[]{:S(2)}) collective-permute-start(f32[6,2,16,4]{3,2,1,0:T(8,128)S(1)} %get-tuple-element.9), channel_id=1, source_target_pairs={{1,0},{2,1},{3,2},{4,3},{5,4},{6,5},{7,6},{0,7},{9,8},{10,9},{11,1... | collective-permute-start | bytes 9224 | tf_op jit(solution)/shard_map/ppermute | solution.py:256

commit v16 on v11

--- a/solution.py
+++ b/solution.py
@@ -252,8 +252,13 @@
         leg = leg_blocks[g * group : (g + 1) * group]
         products = jnp.einsum("mpwlk,pwmcl->cpmk", leg, both, preferred_element_type=jnp.float32)
         spectra = products[:comps] + products[comps:]
-        left_halo = lax.ppermute(spectra[..., local_k - HALO :], "pole", rightward)
-        right_halo = lax.ppermute(spectra[..., :HALO], "pole", leftward)
+        edge_shape = spectra.shape[:3] + (HALO,)
+        left_halo = lax.ppermute(
+            spectra[..., local_k - HALO :].reshape(-1, 128), "pole", rightward
+        ).reshape(edge_shape)
+        right_halo = lax.ppermute(spectra[..., :HALO].reshape(-1, 128), "pole", leftward).reshape(
+            edge_shape
+        )
         left_halo = jnp.where(pole_pos > 0, left_halo, 0.0)
         right_halo = jnp.where(pole_pos < pole_count - 1, right_halo, 0.0)
         gap = jnp.zeros(spectra.shape[:3] + (RING - local_k - 2 * HALO,), jnp.float32)

time: 61.7 us -> 65.3 us (1.058)
  the two profiles are of different devices: /device:TPU:6 before, /device:TPU:0 now
where the time goes in v16:
time: 65.3 us; the launch traced here: 65 us
  waiting for transfers between devices  23.1 us (35%)
  Pallas kernels  12.6 us (19%)
  starting transfers between devices  11.9 us (18%)
  matrix products  8.31 us (13%)
  local copies, waits for them, and re-layouts  4.63 us (7%)
  other arithmetic  4.29 us (7%)
    all_to_all x1, waiting for transfers between devices, shards(): lax.all_to_all(columns, 'wave', split_axis=0, concat_axis=0, tiled=True)  16 us
    pallas_call x1, Pallas kernels, solve_poles(): pl.pallas_call(pole_kernel, out_shape=jax.ShapeDtypeStruct((6, parities,...  12.6 us
    ppermute x1, waiting for transfers between devices, shards(): lax.ppermute(spectra[..., local_k - HALO:].reshape(-1, 128), 'pole', righ...  6.62 us
    all_to_all x1, starting transfers between devices, shards(): lax.all_to_all(columns, 'wave', split_axis=0, concat_axis=0, tiled=True)  6.01 us
    ppermute x1, starting transfers between devices, shards(): lax.ppermute(spectra[..., :HALO].reshape(-1, 128), 'pole', leftward)  5.85 us
    dot_general x1, matrix products, shards(): jnp.einsum('mpwlk,pwmcl->cpmk', leg, both, preferred_element_type=jnp.flo...  5.71 us
    unnamed x1, matrix products  2.59 us
    sub x1, local copies, waits for them, and re-layouts, shards(): parts = jnp.stack([north + south, north - south], axis=0)  1.46 us
  transfers between devices with their start and end apart: 3, of which 3 were waited for; matrix products, arithmetic and copies ran while one was open for 4% of the time, Pallas kernels for 0%

profile of v16, /device:TPU:0, one launch (start us, length us, event | category | flops | bytes accessed | tf_op | source)
XLA Modules:
  0.0 65.0 jit_solution(16945288685802148608)
XLA Ops:
  0.0 1.3 %copy-done = f32[6,256,192]{1,2,0:T(8,128)S(1)} copy-done((f32[6,256,192]{1,2,0:T(8,128)S(1)}, f32[6,256,192]{1,2,0:T(8,128)}, u32[]{:S(2)}) %copy-start) | copy-done | bytes 1179672
  1.3 2.6 %fusion.10 = f32[256,1152]{1,0:T(8,128)} fusion(f32[256,1152]{0,1:T(8,128)S(1)} %bitcast.19, s32[256]{0:T(256)} %param.7), kind=kOutput, calls=%fused_computation.14 | convolution fusion | flops 906035200 | bytes 2360320
  3.9 6.0 %all-to-all-start = ((f32[16,16,1152]{2,1,0:T(8,128)}), f32[16,16,1152]{2,1,0:T(8,128)S(1)}, u32[]{:S(2)}, u32[]{:S(2)}) async-start(f32[16,16,1152]{2,1,0:T(8,128)} %bitcast.9), calls=%async_computation | async-start | bytes 2359296 | tf_op jit(solution)/shard_map/all_to_all | solution.py:245
  10.3 0.6 gather_fusion
  11.0 0.1 fusion.30
  11.1 0.6 select_bitcast_fusion.poles_ref
  11.8 16.0 %all-to-all-done = f32[16,16,1152]{2,1,0:T(8,128)S(1)} async-done(((f32[16,16,1152]{2,1,0:T(8,128)}), f32[16,16,1152]{2,1,0:T(8,128)S(1)}, u32[]{:S(2)}, u32[]{:S(2)}) %all-to-all-start) | async-done | bytes 1179680 | tf_op jit(solution)/shard_map/all_to_all | solution.py:245
  27.8 0.9 %slice_add_fusion = (f32[8,16,1152]{2,1,0:T(8,128)S(1)}, f32[8,16,1152]{2,1,0:T(8,128)}) fusion(f32[16,16,1152]{2,1,0:T(8,128)S(1)} %all-to-all-done), kind=kLoop, calls=%fused_computation.11 | loop fusion | flops 294912 | bytes 2359296 | tf_op jit(solution)/shard_map/add | solution.py:249
  28.7 0.4 add.193
  29.1 1.5 %sub.27 = f32[1,8,16,6,192]{4,3,2,1,0:T(8,128)S(1)} reshape(f32[8,16,1152]{2,1,0:T(8,128)} %get-tuple-element.8) | data formatting | bytes 1179648 | tf_op jit(solution)/shard_map/sub | solution.py:249
  30.5 0.3 pad_maximum_fusion
  30.8 0.1 copy.28
  31.0 0.4 subtract_convert_fusion
  31.4 5.7 %fusion.5 = f32[2,16,12,128]{3,2,1,0:T(8,128)S(1)} fusion(bf16[16,2,8,192,128]{4,3,2,1,0:T(8,128)(2,1)} %bitcast.21, bf16[2,8,16,6,192]{4,3,1,2,0:T(8,128)(2,1)S(1)} %subtract_convert_fusion, bf16[2,8,16,6,192]{4,3,1,2,0:T(8,128)(2,1)S(1)} %copy.28), kind=kOutput, calls=%fused_computation.9 | convolution fusion | flops 153354240 | bytes 13959168 | tf_op jit(solution)/shard_map/mpwlk,pwmcl->cpmk/dot_general | solution.py:253
  37.3 0.1 reshape.253
  37.4 5.8 %collective-permute-start = (f32[6,128]{1,0:T(8,128)S(1)}, f32[6,128]{1,0:T(8,128)S(1)}, u32[]{:S(2)}, u32[]{:S(2)}) collective-permute-start(f32[6,128]{1,0:T(8,128)S(1)} %reshape.253), channel_id=1, source_target_pairs={{1,0},{2,1},{3,2},{4,3},{5,4},{6,5},{7,6},{0,7},{9,8},{10,9},{11,1... | collective-permute-start | bytes 9224 | tf_op jit(solution)/shard_map/ppermute | solution.py:259
  43.3 0.7 %pad_maximum_fusion.2.coef_ref = f32[4,2,16,256]{3,2,1,0:T(8,128)} fusion(f32[1,2,16,256]{3,2,1,0:T(8,128)S(1)} %get-tuple-element.13, f32[1,2,16,256]{3,2,1,0:T(8,128)S(1)} %get-tuple-element.14, f32[2,2,16,256]{3,2,1,0:T(8,128)S(1)} %maximum_multiply_fusion), kind=kLoop, calls=%fused_computation.16 | loop fusion | flops 65536 | bytes 262144 | tf_op jit(solution)/shard_map/concatenate | solution.py:235
  44.0 0.1 reshape.254
  44.1 0.5 collective-permute-done
  44.6 0.1 select_n.68
  44.7 6.6 %collective-permute-done.1 = f32[6,128]{1,0:T(8,128)S(1)} collective-permute-done((f32[6,128]{1,0:T(8,128)S(1)}, f32[6,128]{1,0:T(8,128)S(1)}, u32[]{:S(2)}, u32[]{:S(2)}) %collective-permute-start.1) | collective-permute-done | bytes 3104 | tf_op jit(solution)/shard_map/ppermute | solution.py:256
  51.4 0.1 select_n.71
  51.6 0.8 %pad_maximum_fusion.1.spec_ref = f32[8,2,16,256]{3,2,1,0:T(8,128)} fusion(f32[2,2,16,256]{3,2,1,0:T(8,128)S(1)} %fusion.12, f32[6,2,16,4]{3,2,1,0:T(8,128)S(1)} %select_n.71, f32[6,2,16,120]{3,2,1,0:T(8,128)S(1)} %broadcast_in_dim.54, f32[6,2,16,4]{3,2,1,0:T(8,128)S(1)} %select_n.68, f32[6,2,16,128]{3,2,1,0:T(8,128)S(1)} %slice_add_fusion.1), kind=kLoop, calls=%fused_computation.12 | loop fusion | flops 262144 | bytes 524288 | tf_op jit(solution)/shard_map/concatenate | solution.py:267
  52.4 12.6 %shard_map.55 = f32[6,2,16,128]{3,2,1,0:T(8,128)} custom-call(f32[4,32]{1,0:T(4,128)} %select_bitcast_fusion.poles_ref, f32[8,2,16,256]{3,2,1,0:T(8,128)} %pad_maximum_fusion.1.spec_ref, f32[4,2,16,256]{3,2,1,0:T(8,128)} %pad_maximum_fusion.2.coef_ref), custom_call_target="tpu_custom_call" | custom-call | tf_op jit(solution)/shard_map/pallas_call | solution.py:140
  (29 shorter events, 0.9 us)
Async XLA Ops:
  0.0 1.3 %copy-start = (f32[6,256,192]{1,2,0:T(8,128)S(1)}, f32[6,256,192]{1,2,0:T(8,128)}, u32[]{:S(2)}) copy-start(f32[6,256,192]{1,2,0:T(8,128)} %param.5) | copy-start | bytes 3538948
  1.3 8.7 %copy-start.1 = (s32[256]{0:T(256)S(1)}, s32[256]{0:T(256)}, u32[]{:S(2)}) copy-start(s32[256]{0:T(256)} %param.7) | copy-start | bytes 3076
  1.3 8.9 %copy-start.2 = (f32[4,64]{1,0:T(4,128)S(1)}, f32[4,64]{1,0:T(4,128)}, u32[]{:S(2)}) copy-start(f32[4,64]{1,0:T(4,128)} %param.8) | copy-start | bytes 3076
  1.3 9.0 %copy-start.3 = (s32[32]{0:T(128)S(1)}, s32[32]{0:T(128)}, u32[]{:S(2)}) copy-start(s32[32]{0:T(128)} %param.9) | copy-start | bytes 388
  3.9 23.9 %all-to-all-start = ((f32[16,16,1152]{2,1,0:T(8,128)}), f32[16,16,1152]{2,1,0:T(8,128)S(1)}, u32[]{:S(2)}, u32[]{:S(2)}) async-start(f32[16,16,1152]{2,1,0:T(8,128)} %bitcast.9), calls=%async_computation | async-start | bytes 2359296 | tf_op jit(solution)/shard_map/all_to_all | solution.py:245
  37.4 7.2 %collective-permute-start = (f32[6,128]{1,0:T(8,128)S(1)}, f32[6,128]{1,0:T(8,128)S(1)}, u32[]{:S(2)}, u32[]{:S(2)}) collective-permute-start(f32[6,128]{1,0:T(8,128)S(1)} %reshape.253), channel_id=1, source_target_pairs={{1,0},{2,1},{3,2},{4,3},{5,4},{6,5},{7,6},{0,7},{9,8},{10,9},{11,1... | collective-permute-start | bytes 9224 | tf_op jit(solution)/shard_map/ppermute | solution.py:259
  44.1 7.3 %collective-permute-start.1 = (f32[6,128]{1,0:T(8,128)S(1)}, f32[6,128]{1,0:T(8,128)S(1)}, u32[]{:S(2)}, u32[]{:S(2)}) collective-permute-start(f32[6,128]{1,0:T(8,128)S(1)} %reshape.254), channel_id=1, source_target_pairs={{0,1},{1,2},{2,3},{3,4},{4,5},{5,6},{6,7},{7,0},{8,9},{9,10},{10,1... | collective-permute-start | bytes 9224 | tf_op jit(solution)/shard_map/ppermute | solution.py:256
